TPU v7x, 256 devices: a whole 4x4x8 slice. The times are simulated.
256 devices in a mesh: blk: 32 (over y_hi, z, core), pair: 8 (over y_lo, x).
Axes of the slice: x: 4, y: 4 (y_hi: 2, y_lo: 2; y = y_hi * 2 + y_lo), z: 8, core: 2. Of those that a mesh axis runs over, the one named last changes fastest.
Arguments:
- particles: float32 [262144, 512], P(('blk', 'pair'))
- log_prior: float32 [262144], P(('blk', 'pair'))
- transition: bfloat16 [512, 512], replicated, may hold values from -0.25 to 0.25
- drive_vector: float32 [512], replicated, may hold values from -3 to 3
- current: float32 [4], replicated, may hold values from -4 to 4
- decay_rate: float32 [512], replicated, may hold values from 0.3 to 0.98
- obs_matrix: bfloat16 [512, 128], replicated, may hold values from -0.25 to 0.25
- obs_weight: float32 [128], replicated, may hold values from 0.05 to 0.5
- observed: float32 [4, 128], replicated
- ancestors: int32 [262144], P(('blk', 'pair')), may hold values from 0 to 1023
- cycle_pick: int32 [65536], P(('blk', 'pair')), may hold values from 0 to 1023, as said below
- pair_pick: int32 [8192], P(('blk', 'pair')), may hold values from 0 to 1023, as said below
Outputs:
- migrated: float32 [262144, 512], P(('blk', 'pair'))
- group_logw: float32 [262144], P(('blk', 'pair'))
- mean_state: float32 [512], replicated
Inputs may be any that keep to these rules, and one draw needn't show every extreme that they name: On each device, cycle_pick's 256 entries and pair_pick's 32 entries are distinct local positions, none shared between the two. `pair_pick`: distinct local positions, none in the same device's cycle_pick.
All inputs are finite; a program needn't handle non-finite values.
Results may differ from a plain program's by a relative error of at most 0.013.
Values sent between devices are 32-bit elements; how exact they have to be, the bound alone decides.
No kernel may reach another device: no remote copies, remote signals or barrier semaphores. Data moves between devices by JAX's collectives and lax.ppermute only.
A program may use at most 64 MiB of HBM per device.

v0:
```python
import functools

import jax
import jax.numpy as jnp
from jax import lax
from jax.sharding import Mesh
from jax.sharding import PartitionSpec as P

STEPS = 4
BLK = ("blk_0", "blk_1", "blk_2")
PAIR = ("pair_0", "pair_1")
BLK_PAIR = ("blk_0", "blk_1", "blk_2", "pair_0", "pair_1")


def by_axis(shard, axes):
    return functools.reduce(lax.pmax, axes, shard)


def by_axis_2(shard, axes):
    for axis in axes:
        shard = lax.psum(shard, axis)
    return shard


def shifted(block, axis, distance):
    devices = range(lax.axis_size(axis))
    route = [((i - distance) % len(devices), i) for i in devices]
    return lax.ppermute(block, axis, route)


def per_device(
    particles,
    log_prior,
    transition,
    drive_vector,
    current,
    decay_rate,
    obs_matrix,
    obs_weight,
    observed,
    ancestors,
    cycle_pick,
    pair_pick,
):
    state = particles
    logw = log_prior
    rounded = state.astype(jnp.bfloat16)
    for step_index in range(STEPS):
        drift = (
            jnp.dot(rounded, transition, preferred_element_type=jnp.float32)
            + current[step_index] * drive_vector
        )
        state = decay_rate * state + jnp.tanh(drift)
        rounded = state.astype(jnp.bfloat16)
        predicted = jnp.dot(rounded, obs_matrix, preferred_element_type=jnp.float32)
        misfit = predicted - observed[step_index]
        logw = logw - 0.5 * jnp.sum(obs_weight * misfit * misfit, axis=1)
    groups = lax.axis_size(BLK) * lax.axis_size(PAIR)
    rows_here = state.shape[0]
    resampled = state[ancestors]
    cycle_sent = resampled[cycle_pick]
    pair_sent = resampled[pair_pick]
    peak = by_axis(jnp.max(logw), BLK_PAIR)
    expw = jnp.exp(logw - peak)
    local_sum = jnp.sum(expw)
    weighted = jnp.dot(expw, state, precision=lax.Precision.HIGHEST)
    total, summed = (by_axis_2(local_sum, BLK_PAIR), by_axis_2(weighted, BLK_PAIR))
    mean_state = summed / total
    dev_logw = jnp.log(jnp.maximum(groups * local_sum / total, 0.1))
    weight_cell = jnp.reshape(dev_logw, (1,))
    cycle_in, cycle_w = shifted((cycle_sent, weight_cell), BLK, 1)
    half_pair = lax.axis_size(PAIR) // 2
    pair_in, pair_w = shifted((pair_sent, weight_cell), PAIR, half_pair)
    migrated = resampled.at[cycle_pick].set(cycle_in).at[pair_pick].set(pair_in)
    base_w = jnp.full((rows_here,), dev_logw, jnp.float32)
    group_logw = base_w.at[cycle_pick].set(cycle_w[0]).at[pair_pick].set(pair_w[0])
    return (migrated, group_logw, mean_state)


def solution(mesh):
    torus = Mesh(
        mesh.devices.reshape(2, 8, 2, 2, 4), ("blk_0", "blk_1", "blk_2", "pair_0", "pair_1")
    )
    in_specs = (
        P(BLK_PAIR, None),
        P(BLK_PAIR),
        P(),
        P(),
        P(),
        P(),
        P(),
        P(),
        P(),
        P(BLK_PAIR),
        P(BLK_PAIR),
        P(BLK_PAIR),
    )
    out_specs = (P(BLK_PAIR, None), P(BLK_PAIR), P())
    return jax.shard_map(
        per_device, mesh=torus, in_specs=in_specs, out_specs=out_specs, check_vma=False
    )
```

profile of v0, /device:TPU:2, one launch (start us, length us, event | category | flops | bytes accessed | tf_op | source)
XLA Modules:
  0.0 136.8 jit_solution(18018592090877388813)
XLA Ops:
  0.6 0.0 copy-start
  0.6 1.5 %fusion.21 = (f32[1]{0:T(128)}, f32[1]{0:T(128)}, f32[1]{0:T(128)}, f32[1]{0:T(128)}) fusion(f32[4]{0:T(128)} %param.16), kind=kLoop, calls=%fused_computation.52 | loop fusion | bytes 32 | tf_op jit(solution)/shard_map/slice | solution.py:51
  2.1 0.8 slice_bitcast_fusion.3
  3.0 3.3 %broadcast_multiply_fusion = (f32[512]{0:T(512)S(1)}, f32[512]{0:T(512)S(1)}, f32[512]{0:T(512)S(1)}, f32[512]{0:T(512)S(1)}) fusion(f32[512]{0:T(512)} %param.15, f32[]{:T(128)} %bitcast.3, f32[]{:T(128)} %bitcast.1, f32[]{:T(128)} %bitcast, f32[]{:T(128)} %bitcast.2), kind=kLoop, calls=%fused_computation.42 | loop fusion | flops 2048 | bytes 10256 | tf_op jit(solution)/shard_map/mul | solution.py:51
  6.3 0.0 copy-done
  6.3 0.0 copy-start.7
  6.3 3.0 %tanh_add_fusion.3 = f32[1024,512]{1,0:T(8,128)S(1)} fusion(f32[1024,512]{1,0:T(8,128)} %param.12, bf16[512,512]{1,0:T(8,128)(2,1)S(1)} %copy-done, f32[512]{0:T(512)S(1)} %get-tuple-element.23, f32[512]{0:T(512)} %param.17), kind=kOutput, calls=%fused_computation.10 | convolution fusion | flops 538968064 | bytes 4722688 | tf_op jit(solution)/shard_map/dot_general | solution.py:50
  9.3 0.0 copy-done.7
  9.3 0.0 copy-start.2
  9.3 0.0 copy-start.3
  9.3 0.7 tanh_add_fusion.2
  10.0 0.1 copy-done.2
  10.2 0.0 copy-done.3
  10.2 0.5 fusion.9
  10.7 0.5 fusion.8
  11.2 0.7 tanh_add_fusion.1
  11.9 0.5 fusion.7
  12.4 0.7 tanh_add_fusion
  13.2 0.0 copy-start.4
  13.2 0.0 copy-start.6
  13.2 0.0 copy-start.5
  13.2 0.5 fusion.4
  13.7 0.1 copy-done.4
  13.9 0.6 fusion.20
  14.5 7.0 %pmax.35 = f32[]{:T(128)} all-reduce(f32[]{:T(128)} %get-tuple-element.15), channel_id=1, replica_groups=mesh['blk_0'=2,'blk_1'=8,'blk_2'=2,'pair_0'=2,'pair_1'=4] {'blk_0'}, use_global_device_ids=true, to_apply=%region_7.0 | all-reduce | flops 1 | bytes 8 | tf_op jit(solution)/shard_map/pmax | solution.py:16
  21.5 20.6 %pmax.36 = f32[]{:T(128)} all-reduce(f32[]{:T(128)} %pmax.35), channel_id=1, replica_groups=mesh['blk_0'=2,'blk_1'=8,'blk_2'=2,'pair_0'=2,'pair_1'=4] {'blk_1'}, use_global_device_ids=true, to_apply=%region_8.0 | all-reduce | flops 1 | bytes 8 | tf_op jit(solution)/shard_map/pmax | solution.py:16
  42.1 3.1 %pmax.37 = f32[]{:T(128)} all-reduce(f32[]{:T(128)} %pmax.36), channel_id=1, replica_groups=mesh['blk_0'=2,'blk_1'=8,'blk_2'=2,'pair_0'=2,'pair_1'=4] {'blk_2'}, use_global_device_ids=true, to_apply=%region_9.0 | all-reduce | flops 1 | bytes 8 | tf_op jit(solution)/shard_map/pmax | solution.py:16
  45.2 5.5 %pmax.38 = f32[]{:T(128)} all-reduce(f32[]{:T(128)} %pmax.37), channel_id=1, replica_groups=mesh['blk_0'=2,'blk_1'=8,'blk_2'=2,'pair_0'=2,'pair_1'=4] {'pair_0'}, use_global_device_ids=true, to_apply=%region_10.0 | all-reduce | flops 1 | bytes 8 | tf_op jit(solution)/shard_map/pmax | solution.py:16
  50.8 9.2 %pmax.39 = f32[]{:T(128)} all-reduce(f32[]{:T(128)} %pmax.38), channel_id=1, replica_groups=mesh['blk_0'=2,'blk_1'=8,'blk_2'=2,'pair_0'=2,'pair_1'=4] {'pair_1'}, use_global_device_ids=true, to_apply=%region_11.0 | all-reduce | flops 1 | bytes 8 | tf_op jit(solution)/shard_map/pmax | solution.py:16
  60.0 1.2 fusion.19
  61.2 1.1 fusion.22
  63.0 7.1 %all-reduce.4 = (f32[]{:T(128)}, f32[512]{0:T(512)S(1)}) all-reduce(f32[]{:T(128)} %get-tuple-element.13, f32[512]{0:T(512)S(1)} %bitcast.32), channel_id=1, replica_groups=mesh['blk_0'=2,'blk_1'=8,'blk_2'=2,'pair_0'=2,'pair_1'=4] {'blk_0'}, use_global_device_ids=true, to_apply=%region_13.0 | all-reduce | flops 513 | bytes 4104 | tf_op jit(solution)/shard_map/psum | solution.py:21
  70.1 14.8 %all-reduce = (f32[]{:T(128)}, f32[512]{0:T(512)S(1)}) all-reduce(f32[]{:T(128)} %get-tuple-element.11, f32[512]{0:T(512)S(1)} %get-tuple-element.12), channel_id=1, replica_groups=mesh['blk_0'=2,'blk_1'=8,'blk_2'=2,'pair_0'=2,'pair_1'=4] {'blk_1'}, use_global_device_ids=true, to_apply=%region_14.0 | all-reduce | flops 513 | bytes 4104 | tf_op jit(solution)/shard_map/psum | solution.py:21
  84.8 3.1 %all-reduce.3 = (f32[]{:T(128)}, f32[512]{0:T(512)S(1)}) all-reduce(f32[]{:T(128)} %get-tuple-element.3, f32[512]{0:T(512)S(1)} %get-tuple-element.4), channel_id=1, replica_groups=mesh['blk_0'=2,'blk_1'=8,'blk_2'=2,'pair_0'=2,'pair_1'=4] {'blk_2'}, use_global_device_ids=true, to_apply=%region_15.0 | all-reduce | flops 513 | bytes 4104 | tf_op jit(solution)/shard_map/psum | solution.py:21
  87.9 5.5 %all-reduce.2 = (f32[]{:T(128)}, f32[512]{0:T(512)S(1)}) all-reduce(f32[]{:T(128)} %get-tuple-element.9, f32[512]{0:T(512)S(1)} %get-tuple-element.10), channel_id=1, replica_groups=mesh['blk_0'=2,'blk_1'=8,'blk_2'=2,'pair_0'=2,'pair_1'=4] {'pair_0'}, use_global_device_ids=true, to_apply=%region_16.0 | all-reduce | flops 513 | bytes 4104 | tf_op jit(solution)/shard_map/psum | solution.py:21
  93.4 10.7 %all-reduce.1 = (f32[]{:T(128)}, f32[512]{0:T(512)S(1)}) all-reduce(f32[]{:T(128)} %get-tuple-element.7, f32[512]{0:T(512)S(1)} %get-tuple-element.8), channel_id=1, replica_groups=mesh['blk_0'=2,'blk_1'=8,'blk_2'=2,'pair_0'=2,'pair_1'=4] {'pair_1'}, use_global_device_ids=true, to_apply=%region_17.0 | all-reduce | flops 513 | bytes 4104 | tf_op jit(solution)/shard_map/psum | solution.py:21
  104.9 3.0 %collective-permute-start.3 = (f32[1]{0:T(128)}, f32[1]{0:T(128)}, u32[]{:S(2)}, u32[]{:S(2)}) collective-permute-start(f32[1]{0:T(128)} %bitcast.8), channel_id=1, source_target_pairs={{4,0},{5,1},{6,2},{7,3},{0,4},{1,5},{2,6},{3,7},{12,8},{13,9},{14,... | collective-permute-start | bytes 20 | tf_op jit(solution)/shard_map/ppermute | solution.py:28
  107.9 1.0 collective-permute-start.2
  108.9 0.0 copy-done.6
  108.9 0.0 copy-done.5
  108.9 4.9 %gather_fusion = f32[1024,512]{1,0:T(8,128)} fusion(f32[1024,512]{1,0:T(8,128)S(1)} %tanh_add_fusion, s32[1024]{0:T(1024)S(1)} %fusion.16), kind=kCustom, calls=%fused_computation | custom fusion | bytes 4198400 | tf_op jit(solution)/shard_map/gather | solution.py:60
  113.8 0.0 copy-start.8
  113.8 2.8 %gather_fusion.1 = f32[256,512]{1,0:T(8,128)S(1)} fusion(f32[1024,512]{1,0:T(8,128)} %gather_fusion, s32[1024]{0:T(1024)S(1)} %pad_clamp_fusion.1), kind=kCustom, calls=%fused_computation.1 | custom fusion | bytes 1049600 | tf_op jit(solution)/shard_map/gather | solution.py:61
  116.6 2.0 %collective-permute-start = (f32[256,512]{1,0:T(8,128)S(1)}, f32[256,512]{1,0:T(8,128)S(1)}, u32[]{:S(2)}, u32[]{:S(2)}) collective-permute-start(f32[256,512]{1,0:T(8,128)S(1)} %gather_fusion.1), channel_id=1, source_target_pairs={{248,0},{0,8},{8,16},{16,24},{24,32},{32,40},{40,48},{48,56},{56,6... | collective-permute-start | bytes 1572872 | tf_op jit(solution)/shard_map/ppermute | solution.py:28
  118.6 0.0 copy-done.8
  118.6 2.2 %gather_fusion.2 = f32[32,512]{1,0:T(8,128)S(1)} fusion(f32[1024,512]{1,0:T(8,128)} %gather_fusion, s32[1024]{0:T(1024)S(1)} %pad_clamp_fusion), kind=kCustom, calls=%fused_computation.2 | custom fusion | bytes 131200 | tf_op jit(solution)/shard_map/gather | solution.py:62
  120.8 0.5 collective-permute-start.1
  121.3 1.2 broadcast_divide_fusion
  122.5 0.0 collective-permute-done.2
  122.5 0.6 broadcast.26
  123.2 1.4 %scatter_custom_fusion.2 = f32[1024]{0:T(1024)S(1)} fusion(s32[256]{0:T(256)S(1)} %compare_select_fusion.1, f32[256]{0:T(256)S(1)} %broadcast.26, f32[]{:T(128)} %log.3), kind=kCustom, calls=%fused_computation.39 | custom fusion | bytes 4100 | tf_op jit(solution)/shard_map/scatter | solution.py:76
  124.6 0.0 collective-permute-done.3
  124.6 0.6 broadcast.27
  125.2 0.7 scatter_fusion.2
  125.9 0.0 copy-start.1
  125.9 3.1 %collective-permute-done = f32[256,512]{1,0:T(8,128)S(1)} collective-permute-done((f32[256,512]{1,0:T(8,128)S(1)}, f32[256,512]{1,0:T(8,128)S(1)}, u32[]{:S(2)}, u32[]{:S(2)}) %collective-permute-start) | collective-permute-done | bytes 524320 | tf_op jit(solution)/shard_map/ppermute | solution.py:28
  129.0 4.3 %scatter_fusion = f32[1024,512]{1,0:T(8,128)} fusion(f32[1024,512]{1,0:T(8,128)} %gather_fusion, s32[256]{0:T(256)S(1)} %compare_select_fusion.1, f32[256,512]{1,0:T(8,128)S(1)} %collective-permute-done), kind=kCustom, calls=%fused_computation.3 | custom fusion | bytes 1573888 | tf_op jit(solution)/shard_map/scatter | solution.py:74
  133.3 0.0 copy-done.1
  133.3 0.0 collective-permute-done.1
  133.3 3.6 %scatter_fusion.1 = f32[1024,512]{1,0:T(8,128)} fusion(f32[1024,512]{1,0:T(8,128)} %scatter_fusion, s32[32]{0:T(128)S(1)} %compare_select_fusion.2, f32[32,512]{1,0:T(8,128)S(1)} %collective-permute-done.1), kind=kCustom, calls=%fused_computation.4 | custom fusion | bytes 196736 | tf_op jit(solution)/shard_map/scatter | solution.py:74
  (5 shorter events, 0.0 us)
Async XLA Ops:
  0.6 5.6 %copy-start = (bf16[512,512]{1,0:T(8,128)(2,1)S(1)}, bf16[512,512]{1,0:T(8,128)(2,1)}, u32[]{:S(2)}) copy-start(bf16[512,512]{1,0:T(8,128)(2,1)} %param.14) | copy-start | bytes 1572868
  6.3 3.0 %copy-start.7 = (f32[512]{0:T(512)S(1)}, f32[512]{0:T(512)}, u32[]{:S(2)}) copy-start(f32[512]{0:T(512)} %param.17) | copy-start | bytes 6148
  9.3 0.9 copy-start.2
  9.3 0.9 copy-start.3
  13.2 0.7 copy-start.4
  13.2 95.7 %copy-start.6 = (s32[256]{0:T(256)S(1)}, s32[256]{0:T(256)}, u32[]{:S(2)}) copy-start(s32[256]{0:T(256)} %param.22) | copy-start | bytes 3076
  13.2 95.7 %copy-start.5 = (s32[1024]{0:T(1024)S(1)}, s32[1024]{0:T(1024)}, u32[]{:S(2)}) copy-start(s32[1024]{0:T(1024)} %param.21) | copy-start | bytes 12292
  104.9 19.7 %collective-permute-start.3 = (f32[1]{0:T(128)}, f32[1]{0:T(128)}, u32[]{:S(2)}, u32[]{:S(2)}) collective-permute-start(f32[1]{0:T(128)} %bitcast.8), channel_id=1, source_target_pairs={{4,0},{5,1},{6,2},{7,3},{0,4},{1,5},{2,6},{3,7},{12,8},{13,9},{14,... | collective-permute-start | bytes 20 | tf_op jit(solution)/shard_map/ppermute | solution.py:28
  107.9 14.6 %collective-permute-start.2 = (f32[1]{0:T(128)}, f32[1]{0:T(128)}, u32[]{:S(2)}, u32[]{:S(2)}) collective-permute-start(f32[1]{0:T(128)} %bitcast.8), channel_id=1, source_target_pairs={{248,0},{0,8},{8,16},{16,24},{24,32},{32,40},{40,48},{48,56},{56,6... | collective-permute-start | bytes 20 | tf_op jit(solution)/shard_map/ppermute | solution.py:28
  113.8 4.8 %copy-start.8 = (s32[32]{0:T(128)S(1)}, s32[32]{0:T(128)}, u32[]{:S(2)}) copy-start(s32[32]{0:T(128)} %param.23) | copy-start | bytes 388
  116.6 12.4 %collective-permute-start = (f32[256,512]{1,0:T(8,128)S(1)}, f32[256,512]{1,0:T(8,128)S(1)}, u32[]{:S(2)}, u32[]{:S(2)}) collective-permute-start(f32[256,512]{1,0:T(8,128)S(1)} %gather_fusion.1), channel_id=1, source_target_pairs={{248,0},{0,8},{8,16},{16,24},{24,32},{32,40},{40,48},{48,56},{56,6... | collective-permute-start | bytes 1572872 | tf_op jit(solution)/shard_map/ppermute | solution.py:28
  120.8 12.5 %collective-permute-start.1 = (f32[32,512]{1,0:T(8,128)S(1)}, f32[32,512]{1,0:T(8,128)S(1)}, u32[]{:S(2)}, u32[]{:S(2)}) collective-permute-start(f32[32,512]{1,0:T(8,128)S(1)} %gather_fusion.2), channel_id=1, source_target_pairs={{4,0},{5,1},{6,2},{7,3},{0,4},{1,5},{2,6},{3,7},{12,8},{13,9},{14,... | collective-permute-start | bytes 196616 | tf_op jit(solution)/shard_map/ppermute | solution.py:28
  125.9 7.4 %copy-start.1 = (f32[1024]{0:T(1024)}, f32[1024]{0:T(1024)S(1)}, u32[]{:S(2)}) copy-start(f32[1024]{0:T(1024)S(1)} %scatter_fusion.2) | copy-start | bytes 12292
where the time goes:
time: 137 us
  blocking collectives  86.7 us (63%)
  local copies, waits for them, and re-layouts  23.7 us (17%)
  matrix products  8.26 us (6%)
  other arithmetic  6.42 us (5%)
  starting transfers between devices  6.42 us (5%)
  waiting for transfers between devices  3.1 us (2%)
  between operations  2.23 us (2%)
    pmax x5, blocking collectives, by_axis(): return functools.reduce(lax.pmax, axes, shard)  45.5 us
    psum x5, blocking collectives, by_axis_2(): shard = lax.psum(shard, axis)  41.2 us
    scatter x2, local copies, waits for them, and re-layouts, per_device(): migrated = resampled.at[cycle_pick].set(cycle_in).at[pair_pick].set(pair_in)  7.84 us
    ppermute x4, starting transfers between devices, shifted(): return lax.ppermute(block, axis, route)  6.42 us
    dot_general x4, matrix products, per_device(): jnp.dot(rounded, transition, preferred_element_type=jnp.float32)  5.19 us
    gather x1, local copies, waits for them, and re-layouts, per_device(): resampled = state[ancestors]  4.87 us
    mul x1, other arithmetic, per_device(): current[step_index] * drive_vector  3.31 us
    ppermute x4, waiting for transfers between devices, shifted(): return lax.ppermute(block, axis, route)  3.1 us
  transfers between devices with their start and end apart: 4, of which 1 were waited for; matrix products, arithmetic and copies ran while one was open for 14% of the time, Pallas kernels for 0%

commit v1 on v0

--- a/solution.py
+++ b/solution.py
@@ -10,16 +10,6 @@
 BLK = ("blk_0", "blk_1", "blk_2")
 PAIR = ("pair_0", "pair_1")
 BLK_PAIR = ("blk_0", "blk_1", "blk_2", "pair_0", "pair_1")
-
-
-def by_axis(shard, axes):
-    return functools.reduce(lax.pmax, axes, shard)
-
-
-def by_axis_2(shard, axes):
-    for axis in axes:
-        shard = lax.psum(shard, axis)
-    return shard
 
 
 def shifted(block, axis, distance):
@@ -55,25 +45,47 @@
         predicted = jnp.dot(rounded, obs_matrix, preferred_element_type=jnp.float32)
         misfit = predicted - observed[step_index]
         logw = logw - 0.5 * jnp.sum(obs_weight * misfit * misfit, axis=1)
-    groups = lax.axis_size(BLK) * lax.axis_size(PAIR)
+    n_blk = lax.axis_size(BLK)
+    n_pair = lax.axis_size(PAIR)
+    groups = n_blk * n_pair
     rows_here = state.shape[0]
-    resampled = state[ancestors]
-    cycle_sent = resampled[cycle_pick]
-    pair_sent = resampled[pair_pick]
-    peak = by_axis(jnp.max(logw), BLK_PAIR)
+    n_cycle = cycle_pick.shape[0]
+    n_pairs = pair_pick.shape[0]
+
+    cycle_in = shifted(state[ancestors[cycle_pick]], BLK, 1)
+    pair_in = shifted(state[ancestors[pair_pick]], PAIR, n_pair // 2)
+
+    peak = lax.pmax(jnp.max(logw), BLK_PAIR)
     expw = jnp.exp(logw - peak)
     local_sum = jnp.sum(expw)
     weighted = jnp.dot(expw, state, precision=lax.Precision.HIGHEST)
-    total, summed = (by_axis_2(local_sum, BLK_PAIR), by_axis_2(weighted, BLK_PAIR))
-    mean_state = summed / total
-    dev_logw = jnp.log(jnp.maximum(groups * local_sum / total, 0.1))
-    weight_cell = jnp.reshape(dev_logw, (1,))
-    cycle_in, cycle_w = shifted((cycle_sent, weight_cell), BLK, 1)
-    half_pair = lax.axis_size(PAIR) // 2
-    pair_in, pair_w = shifted((pair_sent, weight_cell), PAIR, half_pair)
-    migrated = resampled.at[cycle_pick].set(cycle_in).at[pair_pick].set(pair_in)
-    base_w = jnp.full((rows_here,), dev_logw, jnp.float32)
-    group_logw = base_w.at[cycle_pick].set(cycle_w[0]).at[pair_pick].set(pair_w[0])
+    me = lax.axis_index(BLK_PAIR)
+    slots = jnp.zeros((groups,), jnp.float32).at[me].set(local_sum)
+    summed = lax.psum(jnp.concatenate([slots, weighted]), BLK_PAIR)
+    sums = summed[:groups]
+    total = jnp.sum(sums)
+    mean_state = summed[groups:] / total
+    all_logw = jnp.log(jnp.maximum(groups * sums / total, 0.1))
+
+    b = lax.axis_index(BLK)
+    p = lax.axis_index(PAIR)
+    own_w = all_logw[me]
+    cycle_w = all_logw[((b - 1) % n_blk) * n_pair + p]
+    pair_w = all_logw[b * n_pair + (p + n_pair // 2) % n_pair]
+
+    source = (
+        ancestors.at[cycle_pick]
+        .set(rows_here + jnp.arange(n_cycle, dtype=jnp.int32))
+        .at[pair_pick]
+        .set(rows_here + n_cycle + jnp.arange(n_pairs, dtype=jnp.int32))
+    )
+    table = jnp.concatenate([state, cycle_in, pair_in], axis=0)
+    migrated = table[source]
+    group_logw = jnp.where(
+        source >= rows_here + n_cycle,
+        pair_w,
+        jnp.where(source >= rows_here, cycle_w, own_w),
+    )
     return (migrated, group_logw, mean_state)
 
 

time: 137 us -> 198 us (1.45)
  the two profiles are of different devices: /device:TPU:2 before, /device:TPU:1 now
where the time goes in v1:
time: 198 us; the launch traced here: 197 us
  blocking collectives  151 us (76%)
  local copies, waits for them, and re-layouts  16.1 us (8%)
  other arithmetic  13 us (7%)
  matrix products  9.96 us (5%)
  starting transfers between devices  4.74 us (2%)
    pmax x1, blocking collectives, per_device(): peak = lax.pmax(jnp.max(logw), BLK_PAIR)  78.8 us
    psum x1, blocking collectives, per_device(): summed = lax.psum(jnp.concatenate([slots, weighted]), BLK_PAIR)  72.6 us
    dot_general x4, matrix products, per_device(): jnp.dot(rounded, transition, preferred_element_type=jnp.float32)  5.14 us
    gather x1, local copies, waits for them, and re-layouts, per_device(): migrated = table[source]  4.87 us
    ppermute x2, starting transfers between devices, shifted(): return lax.ppermute(block, axis, route)  4.74 us
  transfers between devices with their start and end apart: 2, of which 0 were waited for; matrix products, arithmetic and copies ran while one was open for 9% of the time, Pallas kernels for 0%

profile of v1, /device:TPU:1, one launch (start us, length us, event | category | flops | bytes accessed | tf_op | source)
XLA Modules:
  0.0 196.9 jit_solution(11032729353253778405)
XLA Ops:
  0.6 0.0 copy-start
  0.6 0.7 copy.19
  1.4 0.7 compare_select_fusion.4
  2.0 1.5 fusion.21
  3.5 0.7 gather_fusion.2
  4.2 3.3 %broadcast_multiply_fusion = (f32[512]{0:T(512)S(1)}, f32[512]{0:T(512)S(1)}, f32[512]{0:T(512)S(1)}, f32[512]{0:T(512)S(1)}) fusion(f32[512]{0:T(512)} %param.17, f32[]{:T(128)} %bitcast.3, f32[]{:T(128)} %bitcast.1, f32[]{:T(128)} %bitcast, f32[]{:T(128)} %bitcast.2), kind=kLoop, calls=%fused_computation.49 | loop fusion | flops 2048 | bytes 10256 | tf_op jit(solution)/shard_map/mul | solution.py:41
  7.5 0.0 copy-done
  7.5 0.0 copy-start.12
  7.5 3.0 %tanh_add_fusion.3 = f32[1024,512]{1,0:T(8,128)S(1)} fusion(f32[1024,512]{1,0:T(8,128)} %param.14, bf16[512,512]{1,0:T(8,128)(2,1)S(1)} %copy-done, f32[512]{0:T(512)S(1)} %get-tuple-element.25, f32[512]{0:T(512)} %param.19), kind=kOutput, calls=%fused_computation.11 | convolution fusion | flops 538968064 | bytes 4722688 | tf_op jit(solution)/shard_map/dot_general | solution.py:40
  10.5 0.0 copy-start.7
  10.5 0.0 copy-done.12
  10.5 0.7 tanh_add_fusion.2
  11.3 0.6 copy-done.7
  11.9 0.0 copy-start.5
  11.9 0.7 tanh_add_fusion.1
  12.6 0.6 copy-done.5
  13.1 0.0 copy-start.3
  13.1 1.3 copy-done.3
  14.5 0.0 copy-start.11
  14.5 0.7 tanh_add_fusion
  15.2 0.0 copy-start.1
  15.2 0.6 gather_fusion.3
  15.8 2.2 %collective-permute-start.1 = (f32[32,512]{1,0:T(8,128)S(1)}, f32[32,512]{1,0:T(8,128)S(1)}, u32[]{:S(2)}, u32[]{:S(2)}) collective-permute-start(f32[32,512]{1,0:T(8,128)S(1)} %gather_fusion.3), channel_id=1, source_target_pairs={{4,0},{5,1},{6,2},{7,3},{0,4},{1,5},{2,6},{3,7},{12,8},{13,9},{14,... | collective-permute-start | bytes 196616 | tf_op jit(solution)/shard_map/ppermute | solution.py:18
  18.0 0.0 copy-done.11
  18.1 1.4 gather_fusion
  19.5 0.0 copy-start.10
  19.5 1.0 gather_fusion.1
  20.4 0.0 copy-start.2
  20.5 0.0 copy-start.8
  20.5 2.5 %collective-permute-start = (f32[256,512]{1,0:T(8,128)S(1)}, f32[256,512]{1,0:T(8,128)}, u32[]{:S(2)}, u32[]{:S(2)}) collective-permute-start(f32[256,512]{1,0:T(8,128)S(1)} %gather_fusion.1), channel_id=1, source_target_pairs={{248,0},{0,8},{8,16},{16,24},{24,32},{32,40},{40,48},{48,56},{56,6... | collective-permute-start | bytes 1572872 | tf_op jit(solution)/shard_map/ppermute | solution.py:18
  23.0 0.0 copy-done.10
  23.0 1.4 scatter_fusion
  24.4 0.7 scatter_fusion.1
  25.1 0.0 copy-start.6
  25.1 0.0 copy-done.2
  25.2 0.0 copy-done.8
  25.2 0.0 copy-start.4
  25.2 2.2 %fusion.9 = f32[1024]{0:T(1024)S(1)} fusion(bf16[512,128]{1,0:T(8,128)(2,1)S(1)} %copy-done.2, f32[1024,512]{1,0:T(8,128)} %copy-done.7, f32[128]{0:T(128)S(1)} %get-tuple-element.19, f32[128]{0:T(128)S(1)} %copy-done.8), kind=kOutput, calls=%fused_computation.25 | convolution fusion | flops 135265280 | bytes 2233344 | tf_op jit(solution)/shard_map/dot_general | solution.py:45
  27.4 0.0 copy-done.6
  27.4 0.5 fusion.8
  27.9 0.0 copy-done.4
  28.0 0.0 copy-start.9
  28.0 0.5 fusion.7
  28.5 0.5 fusion.4
  29.0 0.0 copy-done.9
  29.0 0.6 fusion.19
  29.6 78.8 %pmax.7 = f32[]{:T(128)} all-reduce(f32[]{:T(128)} %get-tuple-element.17), channel_id=1, replica_groups=mesh['blk_0'=2,'blk_1'=8,'blk_2'=2,'pair_0'=2,'pair_1'=4] {'blk_0','blk_..., use_global_device_ids=true, to_apply=%region_7.0 | all-reduce | flops 1 | bytes 8 | tf_op jit(solution)/shard_map/pmax | solution.py:58
  108.4 1.2 fusion.18
  109.7 0.0 copy-done.1
  109.7 1.1 fusion.22
  111.4 0.1 scatter.21
  111.6 72.6 %psum.7 = f32[768]{0:T(1024)S(1)} all-reduce(f32[768]{0:T(1024)S(1)} %pad_maximum_fusion.1), channel_id=1, replica_groups=mesh['blk_0'=2,'blk_1'=8,'blk_2'=2,'pair_0'=2,'pair_1'=4] {'blk_0','blk_..., use_global_device_ids=true, to_apply=%region_9.0 | all-reduce | flops 768 | bytes 6144 | tf_op jit(solution)/shard_map/psum | solution.py:64
  184.2 0.7 slice_reduce_fusion
  184.9 0.7 maximum_log_fusion
  185.6 0.6 fusion.20
  186.3 2.4 %select_select_fusion = f32[1024]{0:T(1024)} fusion(s32[1024]{0:T(1024)S(1)} %scatter_fusion.1, f32[]{:T(128)} %bitcast.17, f32[]{:T(128)} %bitcast.16, f32[]{:T(128)} %bitcast.15), kind=kLoop, calls=%fused_computation.40 | loop fusion | flops 4096 | bytes 8204 | tf_op jit(solution)/shard_map/jit(_where)/select_n | solution.py:84
  188.7 1.3 slice_divide_fusion
  190.0 0.0 collective-permute-done.1
  190.0 0.0 collective-permute-done
  190.0 2.0 %pad_maximum_fusion = f32[1312,512]{1,0:T(8,128)S(1)} fusion(f32[32,512]{1,0:T(8,128)S(1)} %collective-permute-done.1, f32[256,512]{1,0:T(8,128)} %collective-permute-done, f32[1024,512]{1,0:T(8,128)} %copy-done.1), kind=kLoop, calls=%fused_computation.7 | loop fusion | flops 1343488 | bytes 5373952 | tf_op jit(solution)/shard_map/concatenate | solution.py:82
  192.0 4.9 %gather_fusion.4 = f32[1024,512]{1,0:T(8,128)} fusion(f32[1312,512]{1,0:T(8,128)S(1)} %pad_maximum_fusion, s32[1024]{0:T(1024)S(1)} %fusion.16), kind=kCustom, calls=%fused_computation.4 | custom fusion | bytes 4198400 | tf_op jit(solution)/shard_map/gather | solution.py:83
  (11 shorter events, 0.1 us)
Async XLA Ops:
  0.6 6.9 %copy-start = (bf16[512,512]{1,0:T(8,128)(2,1)S(1)}, bf16[512,512]{1,0:T(8,128)(2,1)}, u32[]{:S(2)}) copy-start(bf16[512,512]{1,0:T(8,128)(2,1)} %param.16) | copy-start | bytes 1572868
  7.5 3.0 %copy-start.12 = (f32[512]{0:T(512)S(1)}, f32[512]{0:T(512)}, u32[]{:S(2)}) copy-start(f32[512]{0:T(512)} %param.19) | copy-start | bytes 6148
  10.5 1.3 copy-start.7
  11.9 1.3 copy-start.5
  13.1 1.4 copy-start.3
  14.5 3.6 %copy-start.11 = (s32[256]{0:T(256)S(1)}, s32[256]{0:T(256)}, u32[]{:S(2)}) copy-start(s32[256]{0:T(256)} %param.24) | copy-start | bytes 3076
  15.2 94.5 %copy-start.1 = (f32[1024,512]{1,0:T(8,128)}, f32[1024,512]{1,0:T(8,128)S(1)}, u32[]{:S(2)}) copy-start(f32[1024,512]{1,0:T(8,128)S(1)} %tanh_add_fusion) | copy-start | bytes 6291460
  15.8 174.1 %collective-permute-start.1 = (f32[32,512]{1,0:T(8,128)S(1)}, f32[32,512]{1,0:T(8,128)S(1)}, u32[]{:S(2)}, u32[]{:S(2)}) collective-permute-start(f32[32,512]{1,0:T(8,128)S(1)} %gather_fusion.3), channel_id=1, source_target_pairs={{4,0},{5,1},{6,2},{7,3},{0,4},{1,5},{2,6},{3,7},{12,8},{13,9},{14,... | collective-permute-start | bytes 196616 | tf_op jit(solution)/shard_map/ppermute | solution.py:18
  19.5 3.6 %copy-start.10 = (f32[4,128]{1,0:T(4,128)S(1)}, f32[4,128]{1,0:T(4,128)}, u32[]{:S(2)}) copy-start(f32[4,128]{1,0:T(4,128)} %param.22) | copy-start | bytes 6148
  20.4 4.7 %copy-start.2 = (bf16[512,128]{1,0:T(8,128)(2,1)S(1)}, bf16[512,128]{1,0:T(8,128)(2,1)}, u32[]{:S(2)}) copy-start(bf16[512,128]{1,0:T(8,128)(2,1)} %param.20) | copy-start | bytes 393220
  20.5 4.7 %copy-start.8 = (f32[128]{0:T(128)S(1)}, f32[128]{0:T(128)}, u32[]{:S(2)}) copy-start(f32[128]{0:T(128)} %param.21) | copy-start | bytes 1540
  20.5 169.5 %collective-permute-start = (f32[256,512]{1,0:T(8,128)S(1)}, f32[256,512]{1,0:T(8,128)}, u32[]{:S(2)}, u32[]{:S(2)}) collective-permute-start(f32[256,512]{1,0:T(8,128)S(1)} %gather_fusion.1), channel_id=1, source_target_pairs={{248,0},{0,8},{8,16},{16,24},{24,32},{32,40},{40,48},{48,56},{56,6... | collective-permute-start | bytes 1572872 | tf_op jit(solution)/shard_map/ppermute | solution.py:18
  25.1 2.3 %copy-start.6 = (f32[1024,512]{1,0:T(8,128)S(1)}, f32[1024,512]{1,0:T(8,128)}, u32[]{:S(2)}) copy-start(f32[1024,512]{1,0:T(8,128)} %copy-done.5) | copy-start | bytes 6291460
  25.2 2.8 %copy-start.4 = (f32[1024,512]{1,0:T(8,128)S(1)}, f32[1024,512]{1,0:T(8,128)}, u32[]{:S(2)}) copy-start(f32[1024,512]{1,0:T(8,128)} %copy-done.3) | copy-start | bytes 6291460
  28.0 1.0 copy-start.9

commit v2 on v1

--- a/solution.py
+++ b/solution.py
@@ -52,26 +52,36 @@
     n_cycle = cycle_pick.shape[0]
     n_pairs = pair_pick.shape[0]
 
-    cycle_in = shifted(state[ancestors[cycle_pick]], BLK, 1)
-    pair_in = shifted(state[ancestors[pair_pick]], PAIR, n_pair // 2)
-
-    peak = lax.pmax(jnp.max(logw), BLK_PAIR)
-    expw = jnp.exp(logw - peak)
+    local_peak = jnp.max(logw)
+    expw = jnp.exp(logw - local_peak)
     local_sum = jnp.sum(expw)
     weighted = jnp.dot(expw, state, precision=lax.Precision.HIGHEST)
-    me = lax.axis_index(BLK_PAIR)
-    slots = jnp.zeros((groups,), jnp.float32).at[me].set(local_sum)
-    summed = lax.psum(jnp.concatenate([slots, weighted]), BLK_PAIR)
-    sums = summed[:groups]
-    total = jnp.sum(sums)
-    mean_state = summed[groups:] / total
-    all_logw = jnp.log(jnp.maximum(groups * sums / total, 0.1))
+    width = state.shape[1]
+    stamp = jnp.zeros((1, width), jnp.float32).at[0, 0].set(local_peak).at[0, 1].set(local_sum)
 
-    b = lax.axis_index(BLK)
-    p = lax.axis_index(PAIR)
-    own_w = all_logw[me]
-    cycle_w = all_logw[((b - 1) % n_blk) * n_pair + p]
-    pair_w = all_logw[b * n_pair + (p + n_pair // 2) % n_pair]
+    cycle_in = shifted(jnp.concatenate([state[ancestors[cycle_pick]], stamp]), BLK, 1)
+    pair_in = shifted(jnp.concatenate([state[ancestors[pair_pick]], stamp]), PAIR, n_pair // 2)
+
+    packed = jnp.concatenate([local_peak[None], local_sum[None], weighted])
+    for axis, size in ((PAIR, n_pair), (BLK, n_blk)):
+        bit = 1
+        while bit < size:
+            other = lax.ppermute(packed, axis, [(i, i ^ bit) for i in range(size)])
+            peak = jnp.maximum(packed[0], other[0])
+            mine_scale = jnp.exp(packed[0] - peak)
+            other_scale = jnp.exp(other[0] - peak)
+            packed = jnp.concatenate([peak[None], packed[1:] * mine_scale + other[1:] * other_scale])
+            bit *= 2
+    peak = packed[0]
+    total = packed[1]
+    mean_state = packed[2:] / total
+
+    def group_weight(device_peak, device_sum):
+        return jnp.log(jnp.maximum(groups * (device_sum * jnp.exp(device_peak - peak)) / total, 0.1))
+
+    own_w = group_weight(local_peak, local_sum)
+    cycle_w = group_weight(cycle_in[n_cycle, 0], cycle_in[n_cycle, 1])
+    pair_w = group_weight(pair_in[n_pairs, 0], pair_in[n_pairs, 1])
 
     source = (
         ancestors.at[cycle_pick]
@@ -79,7 +89,7 @@
         .at[pair_pick]
         .set(rows_here + n_cycle + jnp.arange(n_pairs, dtype=jnp.int32))
     )
-    table = jnp.concatenate([state, cycle_in, pair_in], axis=0)
+    table = jnp.concatenate([state, cycle_in[:n_cycle], pair_in[:n_pairs]], axis=0)
     migrated = table[source]
     group_logw = jnp.where(
         source >= rows_here + n_cycle,

time: 198 us -> 99.4 us (0.50)
  blocking collectives: 151 us -> 0 us
  starting transfers between devices: 4.74 us -> 27.6 us
  between operations: 1.61 us -> 20.6 us
  local copies, waits for them, and re-layouts: 16.1 us -> 21.8 us
  waiting for transfers between devices: 0.01 us -> 4.46 us
  other arithmetic: 13 us -> 16.1 us
    pmax x1 -> x0, blocking collectives: 78.8 us -> none  [per_device(): peak = lax.pmax(jnp.max(logw), BLK_PAIR)]
    psum x1 -> x0, blocking collectives: 72.6 us -> none  [per_device(): summed = lax.psum(jnp.concatenate([slots, weighted]), BLK_PAIR)]
    ppermute x0 -> x8, starting transfers between devices: none -> 22.7 us  [per_device(): other = lax.ppermute(packed, axis, [(i, i ^ bit) for i in range(size)])]
    slice x0 -> x13, local copies, waits for them, and re-layouts: none -> 5.98 us  [the longest x8 4.1 us: per_device(): peak = jnp.maximum(packed[0], other[0])]
    ppermute x0 -> x8, waiting for transfers between devices: none -> 4.45 us  [per_device(): other = lax.ppermute(packed, axis, [(i, i ^ bit) for i in range(size)])]
    another operation x0 -> x3, other arithmetic: none -> 3.78 us
    unnamed x27 -> x17, local copies, waits for them, and re-layouts: 3.34 us -> 1.1 us
  transfers between devices with their start and end apart: 2 -> 10, of which waited for: 0 -> 4; matrix products, arithmetic and copies ran while one was open for 9% -> 19% of each run, Pallas kernels for 0% -> 0%
where the time goes in v2:
time: 99.4 us; the launch traced here: 98.7 us
  starting transfers between devices  27.6 us (28%)
  local copies, waits for them, and re-layouts  21.8 us (22%)
  between operations  20.6 us (21%)
  other arithmetic  16.1 us (16%)
  matrix products  8.21 us (8%)
  waiting for transfers between devices  4.46 us (4%)
    ppermute x8, starting transfers between devices, per_device(): other = lax.ppermute(packed, axis, [(i, i ^ bit) for i in range(size)])  22.7 us
    dot_general x4, matrix products, per_device(): jnp.dot(rounded, transition, preferred_element_type=jnp.float32)  5.14 us
    gather x1, local copies, waits for them, and re-layouts, per_device(): migrated = table[source]  4.87 us
    ppermute x2, starting transfers between devices, shifted(): return lax.ppermute(block, axis, route)  4.87 us
    ppermute x8, waiting for transfers between devices, per_device(): other = lax.ppermute(packed, axis, [(i, i ^ bit) for i in range(size)])  4.45 us
    slice x8, local copies, waits for them, and re-layouts, per_device(): peak = jnp.maximum(packed[0], other[0])  4.1 us
    another operation x3, other arithmetic  3.78 us
    mul x1, other arithmetic, per_device(): current[step_index] * drive_vector  3.31 us
  transfers between devices with their start and end apart: 10, of which 4 were waited for; matrix products, arithmetic and copies ran while one was open for 19% of the time, Pallas kernels for 0%

profile of v2, /device:TPU:1, one launch (start us, length us, event | category | flops | bytes accessed | tf_op | source)
XLA Modules:
  0.0 98.7 jit_solution(4664883999830700104)
XLA Ops:
  0.6 0.7 copy.19
  1.4 1.5 %fusion.23 = (f32[1]{0:T(128)}, f32[1]{0:T(128)}, f32[1]{0:T(128)}, f32[1]{0:T(128)}) fusion(f32[4]{0:T(128)} %param.20), kind=kLoop, calls=%fused_computation.84 | loop fusion | bytes 32 | tf_op jit(solution)/shard_map/slice | solution.py:41
  2.9 0.8 slice_bitcast_fusion.3
  3.7 3.3 %broadcast_multiply_fusion = (f32[512]{0:T(512)S(1)}, f32[512]{0:T(512)S(1)}, f32[512]{0:T(512)S(1)}, f32[512]{0:T(512)S(1)}) fusion(f32[512]{0:T(512)} %param.19, f32[]{:T(128)} %bitcast.3, f32[]{:T(128)} %bitcast.1, f32[]{:T(128)} %bitcast, f32[]{:T(128)} %bitcast.2), kind=kLoop, calls=%fused_computation.68 | loop fusion | flops 2048 | bytes 10256 | tf_op jit(solution)/shard_map/mul | solution.py:41
  7.0 3.0 %tanh_add_fusion.3 = f32[1024,512]{1,0:T(8,128)S(1)} fusion(f32[1024,512]{1,0:T(8,128)} %param.16, bf16[512,512]{1,0:T(8,128)(2,1)S(1)} %copy-done, f32[512]{0:T(512)S(1)} %get-tuple-element.41, f32[512]{0:T(512)} %param.21), kind=kOutput, calls=%fused_computation.11 | convolution fusion | flops 538968064 | bytes 4722688 | tf_op jit(solution)/shard_map/dot_general | solution.py:40
  10.0 0.7 tanh_add_fusion.2
  10.8 0.1 copy-done.2
  10.9 0.5 fusion.9
  11.4 0.5 fusion.8
  11.9 0.7 tanh_add_fusion.1
  12.6 0.5 fusion.7
  13.1 0.7 tanh_add_fusion
  13.9 0.5 fusion.4
  14.4 0.2 copy-done.4
  14.6 0.6 fusion.20
  15.2 1.3 %fusion.19 = (f32[]{:T(128)}, f32[1024]{0:T(1024)S(1)}) fusion(f32[1024]{0:T(1024)S(1)} %get-tuple-element.30, f32[]{:T(128)} %get-tuple-element.29), kind=kLoop, calls=%fused_computation.80 | loop fusion | flops 2047 | bytes 8200 | tf_op jit(solution)/shard_map/reduce_sum | solution.py:57
  16.5 1.1 %fusion.25 = f32[1,512]{1,0:T(1,128)S(1)} fusion(f32[1024,1]{0,1:T(1,128)S(1)} %bitcast.60, f32[1024,512]{1,0:T(8,128)S(1)} %tanh_add_fusion), kind=kOutput, calls=%fused_computation.86 | convolution fusion | flops 6291456 | bytes 2103296 | tf_op jit(solution)/shard_map/dot_general | solution.py:58
  17.6 1.4 %pad_maximum_fusion.3 = f32[514]{0:T(1024)S(1)} fusion(f32[512]{0:T(512)S(1)} %bitcast.58, f32[1]{0:T(128)} %bitcast.19, f32[1]{0:T(128)} %bitcast.18), kind=kLoop, calls=%fused_computation.41 | loop fusion | flops 1028 | bytes 4112 | tf_op jit(solution)/shard_map/concatenate | solution.py:65
  19.0 2.1 %collective-permute-start.2 = (f32[514]{0:T(1024)S(1)}, f32[514]{0:T(1024)S(1)}, u32[]{:S(2)}, u32[]{:S(2)}) collective-permute-start(f32[514]{0:T(1024)S(1)} %pad_maximum_fusion.3), channel_id=1, source_target_pairs={{0,1},{1,0},{2,3},{3,2},{4,5},{5,4},{6,7},{7,6},{8,9},{9,8},{10,11... | collective-permute-start | bytes 6176 | tf_op jit(solution)/shard_map/ppermute | solution.py:69
  21.1 0.7 gather_fusion.2
  21.8 0.6 slice.149
  22.4 0.6 compare_reduce_fusion.1
  24.4 0.6 gather_fusion.3
  25.0 0.6 compare_reduce_fusion
  25.6 2.5 %fusion.24 = f32[1,1]{1,0:T(1,128)} fusion(pred[1,1]{1,0:T(4,128)(4,1)} %bitcast.11, f32[1,1]{1,0:T(1,128)} %bitcast.12, s32[]{:T(128)} %bitcast.13, f32[1,1]{1,0:T(1,128)} %bitcast.10), kind=kLoop, calls=%fused_computation.85 | loop fusion | flops 1 | bytes 17 | tf_op jit(solution)/shard_map/select.3
  28.1 1.3 %scatter.25 = f32[1,512]{1,0:T(1,128)S(1)} dynamic-update-slice(f32[1,512]{1,0:T(1,128)S(1)} %scatter.24, f32[1,1]{1,0:T(1,128)} %fusion.24, s32[]{:T(128)} %constant.65.clone.1, s32[]{:T(128)} %bitcast.13) | dynamic-update-slice | bytes 12 | tf_op jit(solution)/shard_map/scatter | solution.py:60
  29.4 0.5 slice.154
  32.6 0.8 fusion.17
  33.4 2.4 %collective-permute-start.3 = (f32[514]{0:T(1024)S(1)}, f32[514]{0:T(1024)S(1)}, u32[]{:S(2)}, u32[]{:S(2)}) collective-permute-start(f32[514]{0:T(1024)S(1)} %pad_maximum_fusion.4), channel_id=1, source_target_pairs={{0,2},{1,3},{2,0},{3,1},{4,6},{5,7},{6,4},{7,5},{8,10},{9,11},{10,... | collective-permute-start | bytes 6176 | tf_op jit(solution)/shard_map/ppermute | solution.py:69
  35.9 1.4 %collective-permute-start.1 = (f32[33,512]{1,0:T(8,128)S(1)}, f32[33,512]{1,0:T(8,128)S(1)}, u32[]{:S(2)}, u32[]{:S(2)}) collective-permute-start(f32[33,512]{1,0:T(8,128)S(1)} %pad_maximum_fusion.2), channel_id=1, source_target_pairs={{4,0},{5,1},{6,2},{7,3},{0,4},{1,5},{2,6},{3,7},{12,8},{13,9},{14,... | collective-permute-start | bytes 202760 | tf_op jit(solution)/shard_map/ppermute | solution.py:18
  37.3 0.1 collective-permute-done.3
  37.4 0.5 slice.156
  39.4 0.1 pad_maximum_fusion.5
  39.5 1.3 %collective-permute-start.4 = (f32[514]{0:T(1024)S(1)}, f32[514]{0:T(1024)S(1)}, u32[]{:S(2)}, u32[]{:S(2)}) collective-permute-start(f32[514]{0:T(1024)S(1)} %pad_maximum_fusion.5), channel_id=1, source_target_pairs={{0,4},{1,5},{2,6},{3,7},{4,0},{5,1},{6,2},{7,3},{8,12},{9,13},{10,... | collective-permute-start | bytes 6176 | tf_op jit(solution)/shard_map/ppermute | solution.py:69
  40.8 1.2 %collective-permute-done.4 = f32[514]{0:T(1024)S(1)} collective-permute-done((f32[514]{0:T(1024)S(1)}, f32[514]{0:T(1024)S(1)}, u32[]{:S(2)}, u32[]{:S(2)}) %collective-permute-start.4) | collective-permute-done | bytes 2088 | tf_op jit(solution)/shard_map/ppermute | solution.py:69
  41.9 0.5 slice.158
  43.9 0.1 pad_maximum_fusion.6
  44.0 3.5 %collective-permute-start.5 = (f32[514]{0:T(1024)S(1)}, f32[514]{0:T(1024)S(1)}, u32[]{:S(2)}, u32[]{:S(2)}) collective-permute-start(f32[514]{0:T(1024)S(1)} %pad_maximum_fusion.6), channel_id=1, source_target_pairs={{0,8},{8,0},{16,24},{24,16},{32,40},{40,32},{48,56},{56,48},{64,72... | collective-permute-start | bytes 6176 | tf_op jit(solution)/shard_map/ppermute | solution.py:69
  47.5 1.4 %gather_fusion = s32[256]{0:T(256)S(1)} fusion(s32[1024]{0:T(1024)S(1)} %copy.19, s32[1024]{0:T(1024)S(1)} %pad_clamp_fusion.3), kind=kCustom, calls=%fused_computation | custom fusion | bytes 3072 | tf_op jit(solution)/shard_map/gather | solution.py:62
  48.9 0.5 slice.160
  50.8 0.1 pad_maximum_fusion.7
  50.9 1.4 %collective-permute-start.6 = (f32[514]{0:T(1024)S(1)}, f32[514]{0:T(1024)S(1)}, u32[]{:S(2)}, u32[]{:S(2)}) collective-permute-start(f32[514]{0:T(1024)S(1)} %pad_maximum_fusion.7), channel_id=1, source_target_pairs={{0,16},{8,24},{16,0},{24,8},{32,48},{40,56},{48,32},{56,40},{64,80... | collective-permute-start | bytes 6176 | tf_op jit(solution)/shard_map/ppermute | solution.py:69
  52.3 1.1 %collective-permute-done.6 = f32[514]{0:T(1024)S(1)} collective-permute-done((f32[514]{0:T(1024)S(1)}, f32[514]{0:T(1024)S(1)}, u32[]{:S(2)}, u32[]{:S(2)}) %collective-permute-start.6) | collective-permute-done | bytes 2088 | tf_op jit(solution)/shard_map/ppermute | solution.py:69
  53.4 0.5 slice.162
  55.4 2.9 %collective-permute-start.7 = (f32[514]{0:T(1024)S(1)}, f32[514]{0:T(1024)S(1)}, u32[]{:S(2)}, u32[]{:S(2)}) collective-permute-start(f32[514]{0:T(1024)S(1)} %pad_maximum_fusion.8), channel_id=1, source_target_pairs={{0,32},{8,40},{16,48},{24,56},{32,0},{40,8},{48,16},{56,24},{64,96... | collective-permute-start | bytes 6176 | tf_op jit(solution)/shard_map/ppermute | solution.py:69
  58.4 1.0 gather_fusion.1
  59.4 0.5 slice.164
  61.3 0.1 pad_maximum_fusion.9
  61.4 6.1 %collective-permute-start.8 = (f32[514]{0:T(1024)S(1)}, f32[514]{0:T(1024)S(1)}, u32[]{:S(2)}, u32[]{:S(2)}) collective-permute-start(f32[514]{0:T(1024)S(1)} %pad_maximum_fusion.9), channel_id=1, source_target_pairs={{0,64},{8,72},{16,80},{24,88},{32,96},{40,104},{48,112},{56,120},{... | collective-permute-start | bytes 6176 | tf_op jit(solution)/shard_map/ppermute | solution.py:69
  67.6 3.5 %collective-permute-start = (f32[257,512]{1,0:T(8,128)S(1)}, f32[257,512]{1,0:T(8,128)S(1)}, u32[]{:S(2)}, u32[]{:S(2)}) collective-permute-start(f32[257,512]{1,0:T(8,128)S(1)} %pad_maximum_fusion.1), channel_id=1, source_target_pairs={{248,0},{0,8},{8,16},{16,24},{24,32},{32,40},{40,48},{48,56},{56,6... | collective-permute-start | bytes 1579016 | tf_op jit(solution)/shard_map/ppermute | solution.py:18
  71.1 1.4 %scatter_fusion = s32[1024]{0:T(1024)S(1)} fusion(s32[1024]{0:T(1024)S(1)} %copy.19, s32[256]{0:T(256)S(1)} %get-tuple-element.47, s32[256]{0:T(256)S(1)} %get-tuple-element.48), kind=kCustom, calls=%fused_computation.5 | custom fusion | bytes 4096 | tf_op jit(solution)/shard_map/scatter | solution.py:88
  72.5 0.7 scatter_fusion.1
  73.2 0.5 slice.166
  75.2 0.1 pad_maximum_fusion.10
  75.2 2.9 %collective-permute-start.9 = (f32[514]{0:T(1024)S(1)}, f32[514]{0:T(1024)S(1)}, u32[]{:S(2)}, u32[]{:S(2)}) collective-permute-start(f32[514]{0:T(1024)S(1)} %pad_maximum_fusion.10), channel_id=1, source_target_pairs={{0,128},{8,136},{16,144},{24,152},{32,160},{40,168},{48,176},{56,1... | collective-permute-start | bytes 6176 | tf_op jit(solution)/shard_map/ppermute | solution.py:69
  78.2 2.0 %collective-permute-done.9 = f32[514]{0:T(1024)S(1)} collective-permute-done((f32[514]{0:T(1024)S(1)}, f32[514]{0:T(1024)S(1)}, u32[]{:S(2)}, u32[]{:S(2)}) %collective-permute-start.9) | collective-permute-done | bytes 2088 | tf_op jit(solution)/shard_map/ppermute | solution.py:69
  80.2 0.5 slice.168
  82.2 0.5 slice.170
  82.7 1.2 %slice_divide_fusion = f32[512]{0:T(512)} fusion(f32[513]{0:T(1024)S(1)} %multiply_add_fusion, f32[]{:T(128)} %bitcast.37), kind=kLoop, calls=%fused_computation.64 | loop fusion | flops 512 | bytes 4100 | tf_op jit(solution)/shard_map/div | solution.py:77
  85.9 0.7 fusion.22
  88.6 0.7 fusion.21
  91.4 1.9 %pad_maximum_fusion = f32[1312,512]{1,0:T(8,128)S(1)} fusion(f32[32,512]{1,0:T(8,128)S(1)} %slice.185, f32[256,512]{1,0:T(8,128)S(1)} %slice.184, f32[1024,512]{1,0:T(8,128)} %copy-done.1), kind=kLoop, calls=%fused_computation.7 | loop fusion | flops 1343488 | bytes 5373952 | tf_op jit(solution)/shard_map/concatenate | solution.py:92
  93.3 4.9 %gather_fusion.4 = f32[1024,512]{1,0:T(8,128)} fusion(f32[1312,512]{1,0:T(8,128)S(1)} %pad_maximum_fusion, s32[1024]{0:T(1024)S(1)} %fusion.16), kind=kCustom, calls=%fused_computation.4 | custom fusion | bytes 4198400 | tf_op jit(solution)/shard_map/gather | solution.py:93
  98.1 0.6 select_select_fusion
  (44 shorter events, 0.9 us)
Async XLA Ops:
  0.6 6.4 %copy-start = (bf16[512,512]{1,0:T(8,128)(2,1)S(1)}, bf16[512,512]{1,0:T(8,128)(2,1)}, u32[]{:S(2)}) copy-start(bf16[512,512]{1,0:T(8,128)(2,1)} %param.18) | copy-start | bytes 1572868
  7.0 3.0 %copy-start.6 = (f32[512]{0:T(512)S(1)}, f32[512]{0:T(512)}, u32[]{:S(2)}) copy-start(f32[512]{0:T(512)} %param.21) | copy-start | bytes 6148
  10.0 0.9 copy-start.2
  10.0 0.9 copy-start.3
  13.9 44.5 %copy-start.1 = (f32[1024,512]{1,0:T(8,128)}, f32[1024,512]{1,0:T(8,128)S(1)}, u32[]{:S(2)}) copy-start(f32[1024,512]{1,0:T(8,128)S(1)} %tanh_add_fusion) | copy-start | bytes 6291460
  13.9 0.7 copy-start.4
  13.9 7.2 %copy-start.7 = (s32[32]{0:T(128)S(1)}, s32[32]{0:T(128)}, u32[]{:S(2)}) copy-start(s32[32]{0:T(128)} %param.27) | copy-start | bytes 388
  14.6 26.2 %copy-start.5 = (s32[256]{0:T(256)S(1)}, s32[256]{0:T(256)}, u32[]{:S(2)}) copy-start(s32[256]{0:T(256)} %param.26) | copy-start | bytes 3076
  19.0 10.4 %collective-permute-start.2 = (f32[514]{0:T(1024)S(1)}, f32[514]{0:T(1024)S(1)}, u32[]{:S(2)}, u32[]{:S(2)}) collective-permute-start(f32[514]{0:T(1024)S(1)} %pad_maximum_fusion.3), channel_id=1, source_target_pairs={{0,1},{1,0},{2,3},{3,2},{4,5},{5,4},{6,7},{7,6},{8,9},{9,8},{10,11... | collective-permute-start | bytes 6176 | tf_op jit(solution)/shard_map/ppermute | solution.py:69
  33.4 4.0 %collective-permute-start.3 = (f32[514]{0:T(1024)S(1)}, f32[514]{0:T(1024)S(1)}, u32[]{:S(2)}, u32[]{:S(2)}) collective-permute-start(f32[514]{0:T(1024)S(1)} %pad_maximum_fusion.4), channel_id=1, source_target_pairs={{0,2},{1,3},{2,0},{3,1},{4,6},{5,7},{6,4},{7,5},{8,10},{9,11},{10,... | collective-permute-start | bytes 6176 | tf_op jit(solution)/shard_map/ppermute | solution.py:69
  35.9 50.0 %collective-permute-start.1 = (f32[33,512]{1,0:T(8,128)S(1)}, f32[33,512]{1,0:T(8,128)S(1)}, u32[]{:S(2)}, u32[]{:S(2)}) collective-permute-start(f32[33,512]{1,0:T(8,128)S(1)} %pad_maximum_fusion.2), channel_id=1, source_target_pairs={{4,0},{5,1},{6,2},{7,3},{0,4},{1,5},{2,6},{3,7},{12,8},{13,9},{14,... | collective-permute-start | bytes 202760 | tf_op jit(solution)/shard_map/ppermute | solution.py:18
  39.5 2.5 %collective-permute-start.4 = (f32[514]{0:T(1024)S(1)}, f32[514]{0:T(1024)S(1)}, u32[]{:S(2)}, u32[]{:S(2)}) collective-permute-start(f32[514]{0:T(1024)S(1)} %pad_maximum_fusion.5), channel_id=1, source_target_pairs={{0,4},{1,5},{2,6},{3,7},{4,0},{5,1},{6,2},{7,3},{8,12},{9,13},{10,... | collective-permute-start | bytes 6176 | tf_op jit(solution)/shard_map/ppermute | solution.py:69
  44.0 4.9 %collective-permute-start.5 = (f32[514]{0:T(1024)S(1)}, f32[514]{0:T(1024)S(1)}, u32[]{:S(2)}, u32[]{:S(2)}) collective-permute-start(f32[514]{0:T(1024)S(1)} %pad_maximum_fusion.6), channel_id=1, source_target_pairs={{0,8},{8,0},{16,24},{24,16},{32,40},{40,32},{48,56},{56,48},{64,72... | collective-permute-start | bytes 6176 | tf_op jit(solution)/shard_map/ppermute | solution.py:69
  50.9 2.5 %collective-permute-start.6 = (f32[514]{0:T(1024)S(1)}, f32[514]{0:T(1024)S(1)}, u32[]{:S(2)}, u32[]{:S(2)}) collective-permute-start(f32[514]{0:T(1024)S(1)} %pad_maximum_fusion.7), channel_id=1, source_target_pairs={{0,16},{8,24},{16,0},{24,8},{32,48},{40,56},{48,32},{56,40},{64,80... | collective-permute-start | bytes 6176 | tf_op jit(solution)/shard_map/ppermute | solution.py:69
  55.4 3.9 %collective-permute-start.7 = (f32[514]{0:T(1024)S(1)}, f32[514]{0:T(1024)S(1)}, u32[]{:S(2)}, u32[]{:S(2)}) collective-permute-start(f32[514]{0:T(1024)S(1)} %pad_maximum_fusion.8), channel_id=1, source_target_pairs={{0,32},{8,40},{16,48},{24,56},{32,0},{40,8},{48,16},{56,24},{64,96... | collective-permute-start | bytes 6176 | tf_op jit(solution)/shard_map/ppermute | solution.py:69
  61.4 11.8 %collective-permute-start.8 = (f32[514]{0:T(1024)S(1)}, f32[514]{0:T(1024)S(1)}, u32[]{:S(2)}, u32[]{:S(2)}) collective-permute-start(f32[514]{0:T(1024)S(1)} %pad_maximum_fusion.9), channel_id=1, source_target_pairs={{0,64},{8,72},{16,80},{24,88},{32,96},{40,104},{48,112},{56,120},{... | collective-permute-start | bytes 6176 | tf_op jit(solution)/shard_map/ppermute | solution.py:69
  67.6 21.0 %collective-permute-start = (f32[257,512]{1,0:T(8,128)S(1)}, f32[257,512]{1,0:T(8,128)S(1)}, u32[]{:S(2)}, u32[]{:S(2)}) collective-permute-start(f32[257,512]{1,0:T(8,128)S(1)} %pad_maximum_fusion.1), channel_id=1, source_target_pairs={{248,0},{0,8},{8,16},{16,24},{24,32},{32,40},{40,48},{48,56},{56,6... | collective-permute-start | bytes 1579016 | tf_op jit(solution)/shard_map/ppermute | solution.py:18
  75.2 5.0 %collective-permute-start.9 = (f32[514]{0:T(1024)S(1)}, f32[514]{0:T(1024)S(1)}, u32[]{:S(2)}, u32[]{:S(2)}) collective-permute-start(f32[514]{0:T(1024)S(1)} %pad_maximum_fusion.10), channel_id=1, source_target_pairs={{0,128},{8,136},{16,144},{24,152},{32,160},{40,168},{48,176},{56,1... | collective-permute-start | bytes 6176 | tf_op jit(solution)/shard_map/ppermute | solution.py:69

commit v3 on v2

--- a/solution.py
+++ b/solution.py
@@ -1,10 +1,9 @@
-import functools
-
 import jax
 import jax.numpy as jnp
 from jax import lax
 from jax.sharding import Mesh
 from jax.sharding import PartitionSpec as P
+
 
 STEPS = 4
 BLK = ("blk_0", "blk_1", "blk_2")
@@ -18,7 +17,7 @@
     return lax.ppermute(block, axis, route)
 
 
-def per_device(
+def window(
     particles,
     log_prior,
     transition,
@@ -48,7 +47,7 @@
     n_blk = lax.axis_size(BLK)
     n_pair = lax.axis_size(PAIR)
     groups = n_blk * n_pair
-    rows_here = state.shape[0]
+    rows_here, width = state.shape
     n_cycle = cycle_pick.shape[0]
     n_pairs = pair_pick.shape[0]
 
@@ -56,25 +55,35 @@
     expw = jnp.exp(logw - local_peak)
     local_sum = jnp.sum(expw)
     weighted = jnp.dot(expw, state, precision=lax.Precision.HIGHEST)
-    width = state.shape[1]
     stamp = jnp.zeros((1, width), jnp.float32).at[0, 0].set(local_peak).at[0, 1].set(local_sum)
 
     cycle_in = shifted(jnp.concatenate([state[ancestors[cycle_pick]], stamp]), BLK, 1)
     pair_in = shifted(jnp.concatenate([state[ancestors[pair_pick]], stamp]), PAIR, n_pair // 2)
 
-    packed = jnp.concatenate([local_peak[None], local_sum[None], weighted])
+    lanes = 128
+    k = width // lanes
+    message = jnp.concatenate(
+        [
+            weighted.reshape(k, lanes),
+            jnp.full((1, lanes), local_sum),
+            jnp.full((1, lanes), local_peak),
+            jnp.zeros((8 - (k + 2) % 8 if (k + 2) % 8 else 0, lanes), jnp.float32),
+        ]
+    )
+    pad = message.shape[0] - (k + 2)
     for axis, size in ((PAIR, n_pair), (BLK, n_blk)):
         bit = 1
         while bit < size:
-            other = lax.ppermute(packed, axis, [(i, i ^ bit) for i in range(size)])
-            peak = jnp.maximum(packed[0], other[0])
-            mine_scale = jnp.exp(packed[0] - peak)
-            other_scale = jnp.exp(other[0] - peak)
-            packed = jnp.concatenate([peak[None], packed[1:] * mine_scale + other[1:] * other_scale])
+            other = lax.ppermute(message, axis, [(i, i ^ bit) for i in range(size)])
+            peak_row = jnp.maximum(message[k + 1], other[k + 1])
+            mine_scale = jnp.exp(message[k + 1] - peak_row)
+            other_scale = jnp.exp(other[k + 1] - peak_row)
+            body = message[: k + 1] * mine_scale + other[: k + 1] * other_scale
+            message = jnp.concatenate([body, peak_row[None], jnp.zeros((pad, lanes), jnp.float32)])
             bit *= 2
-    peak = packed[0]
-    total = packed[1]
-    mean_state = packed[2:] / total
+    total = message[k, 0]
+    peak = message[k + 1, 0]
+    mean_state = message[:k].reshape(width) / total
 
     def group_weight(device_peak, device_sum):
         return jnp.log(jnp.maximum(groups * (device_sum * jnp.exp(device_peak - peak)) / total, 0.1))
@@ -119,5 +128,5 @@
     )
     out_specs = (P(BLK_PAIR, None), P(BLK_PAIR), P())
     return jax.shard_map(
-        per_device, mesh=torus, in_specs=in_specs, out_specs=out_specs, check_vma=False
+        window, mesh=torus, in_specs=in_specs, out_specs=out_specs, check_vma=False
     )

time: 99.4 us -> 82.9 us (0.83)
  between operations: 20.6 us -> 8.35 us
  local copies, waits for them, and re-layouts: 21.8 us -> 19.1 us
  other arithmetic: 16.1 us -> 14.6 us
    slice x14 -> x6, local copies, waits for them, and re-layouts: 7.45 us -> 3.18 us  [the longest x1 1.4 us: window(): current[step_index] * drive_vector]
    concatenate x11, other arithmetic: 3.91 us -> 2.52 us  [the longest x1 1.9 us: window(): jnp.concatenate([state, cycle_in[:n_cycle], pair_in[:n_pairs]], axis=0)]
    mul x1 -> x17, other arithmetic: 3.31 us -> 3.96 us  [the longest x1 3.18 us: window(): current[step_index] * drive_vector]
  transfers between devices with their start and end apart: 10 -> 10, of which waited for: 4 -> 4; matrix products, arithmetic and copies ran while one was open for 19% -> 18% of each run, Pallas kernels for 0% -> 0%
where the time goes in v3:
time: 82.9 us; the launch traced here: 82.4 us
  starting transfers between devices  27.7 us (33%)
  local copies, waits for them, and re-layouts  19.1 us (23%)
  other arithmetic  14.6 us (18%)
  between operations  8.35 us (10%)
  matrix products  8.19 us (10%)
  waiting for transfers between devices  4.4 us (5%)
    ppermute x8, starting transfers between devices, window(): other = lax.ppermute(message, axis, [(i, i ^ bit) for i in range(size)])  22.8 us
    dot_general x4, matrix products, window(): jnp.dot(rounded, transition, preferred_element_type=jnp.float32)  5.12 us
    ppermute x2, starting transfers between devices, shifted(): return lax.ppermute(block, axis, route)  4.88 us
    gather x1, local copies, waits for them, and re-layouts, window(): migrated = table[source]  4.87 us
    ppermute x8, waiting for transfers between devices, window(): other = lax.ppermute(message, axis, [(i, i ^ bit) for i in range(size)])  4.4 us
    another operation x3, other arithmetic  3.8 us
    mul x1, other arithmetic, window(): current[step_index] * drive_vector  3.18 us
    scatter x2, local copies, waits for them, and re-layouts, window(): source = ancestors.at[cycle_pick].set(rows_here + jnp.arange(n_cycle, dty...  2.09 us
  transfers between devices with their start and end apart: 10, of which 4 were waited for; matrix products, arithmetic and copies ran while one was open for 18% of the time, Pallas kernels for 0%

profile of v3, /device:TPU:1, one launch (start us, length us, event | category | flops | bytes accessed | tf_op | source)
XLA Modules:
  0.0 82.4 jit_solution(13683546037833228159)
XLA Ops:
  0.6 0.0 copy-start
  0.6 0.7 copy.19
  1.4 1.4 %fusion.22 = (f32[1]{0:T(128)}, f32[1]{0:T(128)}, f32[1]{0:T(128)}, f32[1]{0:T(128)}) fusion(f32[4]{0:T(128)} %param.20), kind=kLoop, calls=%fused_computation.107 | loop fusion | bytes 32 | tf_op jit(solution)/shard_map/slice | solution.py:40
  2.8 0.8 %slice_bitcast_fusion.3 = (f32[128]{0:T(128)S(1)}, f32[128]{0:T(128)S(1)}, f32[128]{0:T(128)S(1)}, f32[128]{0:T(128)S(1)}) fusion(f32[4,128]{1,0:T(4,128)} %param.24), kind=kLoop, calls=%fused_computation.92 | loop fusion | bytes 4096 | tf_op jit(solution)/shard_map/sub | solution.py:45
  3.6 3.2 %broadcast_multiply_fusion = (f32[512]{0:T(512)S(1)}, f32[512]{0:T(512)S(1)}, f32[512]{0:T(512)S(1)}, f32[512]{0:T(512)S(1)}) fusion(f32[512]{0:T(512)} %param.19, f32[]{:T(128)} %bitcast.3, f32[]{:T(128)} %bitcast.1, f32[]{:T(128)} %bitcast, f32[]{:T(128)} %bitcast.2), kind=kLoop, calls=%fused_computation.67 | loop fusion | flops 2048 | bytes 10256 | tf_op jit(solution)/shard_map/mul | solution.py:40
  6.8 3.0 %tanh_add_fusion.3 = f32[1024,512]{1,0:T(8,128)S(1)} fusion(f32[1024,512]{1,0:T(8,128)} %param.16, bf16[512,512]{1,0:T(8,128)(2,1)S(1)} %copy-done, f32[512]{0:T(512)S(1)} %get-tuple-element.57, f32[512]{0:T(512)} %param.21), kind=kOutput, calls=%fused_computation.11 | convolution fusion | flops 538968064 | bytes 4722688 | tf_op jit(solution)/shard_map/dot_general | solution.py:39
  9.8 0.7 tanh_add_fusion.2
  10.5 0.2 copy-done.2
  10.7 0.5 fusion.9
  11.2 0.5 fusion.8
  11.7 0.7 tanh_add_fusion.1
  12.4 0.5 fusion.7
  12.9 0.7 tanh_add_fusion
  13.7 0.5 fusion.4
  14.2 0.2 copy-done.4
  14.4 0.6 fusion.19
  15.0 1.2 %fusion.18 = (f32[]{:T(128)}, f32[1024]{0:T(1024)S(1)}) fusion(f32[1024]{0:T(1024)S(1)} %get-tuple-element.46, f32[]{:T(128)} %get-tuple-element.45), kind=kLoop, calls=%fused_computation.103 | loop fusion | flops 2047 | bytes 8200 | tf_op jit(solution)/shard_map/reduce_sum | solution.py:56
  16.2 1.1 %fusion.24 = f32[1,512]{1,0:T(1,128)S(1)} fusion(f32[1024,1]{0,1:T(1,128)S(1)} %bitcast.82, f32[1024,512]{1,0:T(8,128)S(1)} %tanh_add_fusion), kind=kOutput, calls=%fused_computation.109 | convolution fusion | flops 6291456 | bytes 2103296 | tf_op jit(solution)/shard_map/dot_general | solution.py:57
  17.3 0.1 pad.35.clone
  17.4 0.6 pad.33.clone
  18.0 0.6 squeeze.56
  18.7 0.1 maximum_maximum_fusion
  18.8 2.1 %collective-permute-start.2 = (f32[8,128]{1,0:T(8,128)S(1)}, f32[8,128]{1,0:T(8,128)S(1)}, u32[]{:S(2)}, u32[]{:S(2)}) collective-permute-start(f32[8,128]{1,0:T(8,128)S(1)} %maximum_maximum_fusion), channel_id=1, source_target_pairs={{0,1},{1,0},{2,3},{3,2},{4,5},{5,4},{6,7},{7,6},{8,9},{9,8},{10,11... | collective-permute-start | bytes 12296 | tf_op jit(solution)/shard_map/ppermute | solution.py:77
  20.8 0.7 gather_fusion.2
  21.5 0.7 slice.152
  22.2 0.6 compare_reduce_fusion.1
  24.1 0.6 gather_fusion.3
  24.8 0.6 compare_reduce_fusion
  25.4 2.5 %fusion.23 = f32[1,1]{1,0:T(1,128)} fusion(pred[1,1]{1,0:T(4,128)(4,1)} %bitcast.11, f32[1,1]{1,0:T(1,128)} %bitcast.12, s32[]{:T(128)} %bitcast.13, f32[1,1]{1,0:T(1,128)} %bitcast.10), kind=kLoop, calls=%fused_computation.108 | loop fusion | flops 1 | bytes 17 | tf_op jit(solution)/shard_map/select.3
  27.9 1.4 %scatter.25 = f32[1,512]{1,0:T(1,128)S(1)} dynamic-update-slice(f32[1,512]{1,0:T(1,128)S(1)} %scatter.24, f32[1,1]{1,0:T(1,128)} %fusion.23, s32[]{:T(128)} %constant.66.clone.1, s32[]{:T(128)} %bitcast.13) | dynamic-update-slice | bytes 12 | tf_op jit(solution)/shard_map/scatter | solution.py:58
  29.3 0.7 exponential_bitcast_fusion.15
  30.0 0.6 multiply_add_fusion.7
  30.6 0.1 maximum_maximum_fusion.1
  30.7 2.5 %collective-permute-start.3 = (f32[8,128]{1,0:T(8,128)S(1)}, f32[8,128]{1,0:T(8,128)S(1)}, u32[]{:S(2)}, u32[]{:S(2)}) collective-permute-start(f32[8,128]{1,0:T(8,128)S(1)} %maximum_maximum_fusion.1), channel_id=1, source_target_pairs={{0,2},{1,3},{2,0},{3,1},{4,6},{5,7},{6,4},{7,5},{8,10},{9,11},{10,... | collective-permute-start | bytes 12296 | tf_op jit(solution)/shard_map/ppermute | solution.py:77
  33.1 1.4 %collective-permute-start.1 = (f32[33,512]{1,0:T(8,128)S(1)}, f32[33,512]{1,0:T(8,128)S(1)}, u32[]{:S(2)}, u32[]{:S(2)}) collective-permute-start(f32[33,512]{1,0:T(8,128)S(1)} %pad_maximum_fusion.2), channel_id=1, source_target_pairs={{4,0},{5,1},{6,2},{7,3},{0,4},{1,5},{2,6},{3,7},{12,8},{13,9},{14,... | collective-permute-start | bytes 202760 | tf_op jit(solution)/shard_map/ppermute | solution.py:17
  34.5 0.1 collective-permute-done.3
  34.7 0.1 maximum_maximum_fusion.2
  34.7 1.3 %collective-permute-start.4 = (f32[8,128]{1,0:T(8,128)S(1)}, f32[8,128]{1,0:T(8,128)S(1)}, u32[]{:S(2)}, u32[]{:S(2)}) collective-permute-start(f32[8,128]{1,0:T(8,128)S(1)} %maximum_maximum_fusion.2), channel_id=1, source_target_pairs={{0,4},{1,5},{2,6},{3,7},{4,0},{5,1},{6,2},{7,3},{8,12},{9,13},{10,... | collective-permute-start | bytes 12296 | tf_op jit(solution)/shard_map/ppermute | solution.py:77
  36.1 1.2 %collective-permute-done.4 = f32[8,128]{1,0:T(8,128)S(1)} collective-permute-done((f32[8,128]{1,0:T(8,128)S(1)}, f32[8,128]{1,0:T(8,128)S(1)}, u32[]{:S(2)}, u32[]{:S(2)}) %collective-permute-start.4) | collective-permute-done | bytes 4128 | tf_op jit(solution)/shard_map/ppermute | solution.py:77
  37.3 0.1 maximum_maximum_fusion.3
  37.3 3.5 %collective-permute-start.5 = (f32[8,128]{1,0:T(8,128)S(1)}, f32[8,128]{1,0:T(8,128)S(1)}, u32[]{:S(2)}, u32[]{:S(2)}) collective-permute-start(f32[8,128]{1,0:T(8,128)S(1)} %maximum_maximum_fusion.3), channel_id=1, source_target_pairs={{0,8},{8,0},{16,24},{24,16},{32,40},{40,32},{48,56},{56,48},{64,72... | collective-permute-start | bytes 12296 | tf_op jit(solution)/shard_map/ppermute | solution.py:77
  40.9 1.4 %gather_fusion = s32[256]{0:T(256)S(1)} fusion(s32[1024]{0:T(1024)S(1)} %copy.19, s32[1024]{0:T(1024)S(1)} %pad_clamp_fusion.3), kind=kCustom, calls=%fused_computation | custom fusion | bytes 3072 | tf_op jit(solution)/shard_map/gather | solution.py:60
  42.3 0.1 maximum_maximum_fusion.4
  42.4 1.4 %collective-permute-start.6 = (f32[8,128]{1,0:T(8,128)S(1)}, f32[8,128]{1,0:T(8,128)S(1)}, u32[]{:S(2)}, u32[]{:S(2)}) collective-permute-start(f32[8,128]{1,0:T(8,128)S(1)} %maximum_maximum_fusion.4), channel_id=1, source_target_pairs={{0,16},{8,24},{16,0},{24,8},{32,48},{40,56},{48,32},{56,40},{64,80... | collective-permute-start | bytes 12296 | tf_op jit(solution)/shard_map/ppermute | solution.py:77
  43.8 1.1 %collective-permute-done.6 = f32[8,128]{1,0:T(8,128)S(1)} collective-permute-done((f32[8,128]{1,0:T(8,128)S(1)}, f32[8,128]{1,0:T(8,128)S(1)}, u32[]{:S(2)}, u32[]{:S(2)}) %collective-permute-start.6) | collective-permute-done | bytes 4128 | tf_op jit(solution)/shard_map/ppermute | solution.py:77
  44.9 0.1 maximum_maximum_fusion.5
  45.0 3.0 %collective-permute-start.7 = (f32[8,128]{1,0:T(8,128)S(1)}, f32[8,128]{1,0:T(8,128)S(1)}, u32[]{:S(2)}, u32[]{:S(2)}) collective-permute-start(f32[8,128]{1,0:T(8,128)S(1)} %maximum_maximum_fusion.5), channel_id=1, source_target_pairs={{0,32},{8,40},{16,48},{24,56},{32,0},{40,8},{48,16},{56,24},{64,96... | collective-permute-start | bytes 12296 | tf_op jit(solution)/shard_map/ppermute | solution.py:77
  47.9 1.0 %gather_fusion.1 = f32[256,512]{1,0:T(8,128)S(1)} fusion(f32[1024,512]{1,0:T(8,128)S(1)} %tanh_add_fusion, s32[1024]{0:T(1024)S(1)} %pad_clamp_fusion.2), kind=kCustom, calls=%fused_computation.1 | custom fusion | bytes 1049600 | tf_op jit(solution)/shard_map/gather | solution.py:60
  48.9 0.0 collective-permute-done.7
  49.0 0.1 maximum_maximum_fusion.6
  49.0 6.1 %collective-permute-start.8 = (f32[8,128]{1,0:T(8,128)S(1)}, f32[8,128]{1,0:T(8,128)S(1)}, u32[]{:S(2)}, u32[]{:S(2)}) collective-permute-start(f32[8,128]{1,0:T(8,128)S(1)} %maximum_maximum_fusion.6), channel_id=1, source_target_pairs={{0,64},{8,72},{16,80},{24,88},{32,96},{40,104},{48,112},{56,120},{... | collective-permute-start | bytes 12296 | tf_op jit(solution)/shard_map/ppermute | solution.py:77
  55.2 3.5 %collective-permute-start = (f32[257,512]{1,0:T(8,128)S(1)}, f32[257,512]{1,0:T(8,128)S(1)}, u32[]{:S(2)}, u32[]{:S(2)}) collective-permute-start(f32[257,512]{1,0:T(8,128)S(1)} %pad_maximum_fusion.1), channel_id=1, source_target_pairs={{248,0},{0,8},{8,16},{16,24},{24,32},{32,40},{40,48},{48,56},{56,6... | collective-permute-start | bytes 1579016 | tf_op jit(solution)/shard_map/ppermute | solution.py:17
  58.7 1.4 %scatter_fusion = s32[1024]{0:T(1024)S(1)} fusion(s32[1024]{0:T(1024)S(1)} %copy.19, s32[256]{0:T(256)S(1)} %get-tuple-element.63, s32[256]{0:T(256)S(1)} %get-tuple-element.64), kind=kCustom, calls=%fused_computation.5 | custom fusion | bytes 4096 | tf_op jit(solution)/shard_map/scatter | solution.py:97
  60.1 0.7 scatter_fusion.1
  60.9 0.1 maximum_maximum_fusion.7
  60.9 2.9 %collective-permute-start.9 = (f32[8,128]{1,0:T(8,128)S(1)}, f32[8,128]{1,0:T(8,128)S(1)}, u32[]{:S(2)}, u32[]{:S(2)}) collective-permute-start(f32[8,128]{1,0:T(8,128)S(1)} %maximum_maximum_fusion.7), channel_id=1, source_target_pairs={{0,128},{8,136},{16,144},{24,152},{32,160},{40,168},{48,176},{56,1... | collective-permute-start | bytes 12296 | tf_op jit(solution)/shard_map/ppermute | solution.py:77
  63.9 2.0 %collective-permute-done.9 = f32[8,128]{1,0:T(8,128)S(1)} collective-permute-done((f32[8,128]{1,0:T(8,128)S(1)}, f32[8,128]{1,0:T(8,128)S(1)}, u32[]{:S(2)}, u32[]{:S(2)}) %collective-permute-start.9) | collective-permute-done | bytes 4128 | tf_op jit(solution)/shard_map/ppermute | solution.py:77
  65.9 0.6 slice.174
  66.5 1.3 %divide_bitcast_fusion = f32[512]{0:T(512)} fusion(f32[5,128]{1,0:T(8,128)S(1)} %multiply_add_fusion, f32[]{:T(128)} %bitcast.39), kind=kLoop, calls=%fused_computation.63 | loop fusion | flops 512 | bytes 4100 | tf_op jit(solution)/shard_map/div | solution.py:86
  69.8 0.6 fusion.21
  72.4 0.6 fusion.20
  75.1 1.9 %pad_maximum_fusion = f32[1312,512]{1,0:T(8,128)S(1)} fusion(f32[32,512]{1,0:T(8,128)S(1)} %slice.189, f32[256,512]{1,0:T(8,128)S(1)} %slice.188, f32[1024,512]{1,0:T(8,128)} %copy-done.1), kind=kLoop, calls=%fused_computation.7 | loop fusion | flops 1343488 | bytes 5373952 | tf_op jit(solution)/shard_map/concatenate | solution.py:101
  77.0 4.9 %gather_fusion.4 = f32[1024,512]{1,0:T(8,128)} fusion(f32[1312,512]{1,0:T(8,128)S(1)} %pad_maximum_fusion, s32[1024]{0:T(1024)S(1)} %fusion.16), kind=kCustom, calls=%fused_computation.4 | custom fusion | bytes 4198400 | tf_op jit(solution)/shard_map/gather | solution.py:102
  81.8 0.6 select_select_fusion
  (56 shorter events, 0.4 us)
Async XLA Ops:
  0.6 6.2 %copy-start = (bf16[512,512]{1,0:T(8,128)(2,1)S(1)}, bf16[512,512]{1,0:T(8,128)(2,1)}, u32[]{:S(2)}) copy-start(bf16[512,512]{1,0:T(8,128)(2,1)} %param.18) | copy-start | bytes 1572868
  6.8 3.0 %copy-start.6 = (f32[512]{0:T(512)S(1)}, f32[512]{0:T(512)}, u32[]{:S(2)}) copy-start(f32[512]{0:T(512)} %param.21) | copy-start | bytes 6148
  9.8 0.9 %copy-start.2 = (bf16[512,128]{1,0:T(8,128)(2,1)S(1)}, bf16[512,128]{1,0:T(8,128)(2,1)}, u32[]{:S(2)}) copy-start(bf16[512,128]{1,0:T(8,128)(2,1)} %param.22) | copy-start | bytes 393220
  9.8 0.9 %copy-start.3 = (f32[128]{0:T(128)S(1)}, f32[128]{0:T(128)}, u32[]{:S(2)}) copy-start(f32[128]{0:T(128)} %param.23) | copy-start | bytes 1540
  13.7 34.3 %copy-start.1 = (f32[1024,512]{1,0:T(8,128)}, f32[1024,512]{1,0:T(8,128)S(1)}, u32[]{:S(2)}) copy-start(f32[1024,512]{1,0:T(8,128)S(1)} %tanh_add_fusion) | copy-start | bytes 6291460
  13.7 0.7 copy-start.4
  13.7 7.1 %copy-start.7 = (s32[32]{0:T(128)S(1)}, s32[32]{0:T(128)}, u32[]{:S(2)}) copy-start(s32[32]{0:T(128)} %param.27) | copy-start | bytes 388
  14.4 21.7 %copy-start.5 = (s32[256]{0:T(256)S(1)}, s32[256]{0:T(256)}, u32[]{:S(2)}) copy-start(s32[256]{0:T(256)} %param.26) | copy-start | bytes 3076
  18.8 10.6 %collective-permute-start.2 = (f32[8,128]{1,0:T(8,128)S(1)}, f32[8,128]{1,0:T(8,128)S(1)}, u32[]{:S(2)}, u32[]{:S(2)}) collective-permute-start(f32[8,128]{1,0:T(8,128)S(1)} %maximum_maximum_fusion), channel_id=1, source_target_pairs={{0,1},{1,0},{2,3},{3,2},{4,5},{5,4},{6,7},{7,6},{8,9},{9,8},{10,11... | collective-permute-start | bytes 12296 | tf_op jit(solution)/shard_map/ppermute | solution.py:77
  30.7 4.0 %collective-permute-start.3 = (f32[8,128]{1,0:T(8,128)S(1)}, f32[8,128]{1,0:T(8,128)S(1)}, u32[]{:S(2)}, u32[]{:S(2)}) collective-permute-start(f32[8,128]{1,0:T(8,128)S(1)} %maximum_maximum_fusion.1), channel_id=1, source_target_pairs={{0,2},{1,3},{2,0},{3,1},{4,6},{5,7},{6,4},{7,5},{8,10},{9,11},{10,... | collective-permute-start | bytes 12296 | tf_op jit(solution)/shard_map/ppermute | solution.py:77
  33.1 36.7 %collective-permute-start.1 = (f32[33,512]{1,0:T(8,128)S(1)}, f32[33,512]{1,0:T(8,128)S(1)}, u32[]{:S(2)}, u32[]{:S(2)}) collective-permute-start(f32[33,512]{1,0:T(8,128)S(1)} %pad_maximum_fusion.2), channel_id=1, source_target_pairs={{4,0},{5,1},{6,2},{7,3},{0,4},{1,5},{2,6},{3,7},{12,8},{13,9},{14,... | collective-permute-start | bytes 202760 | tf_op jit(solution)/shard_map/ppermute | solution.py:17
  34.7 2.5 %collective-permute-start.4 = (f32[8,128]{1,0:T(8,128)S(1)}, f32[8,128]{1,0:T(8,128)S(1)}, u32[]{:S(2)}, u32[]{:S(2)}) collective-permute-start(f32[8,128]{1,0:T(8,128)S(1)} %maximum_maximum_fusion.2), channel_id=1, source_target_pairs={{0,4},{1,5},{2,6},{3,7},{4,0},{5,1},{6,2},{7,3},{8,12},{9,13},{10,... | collective-permute-start | bytes 12296 | tf_op jit(solution)/shard_map/ppermute | solution.py:77
  37.3 4.9 %collective-permute-start.5 = (f32[8,128]{1,0:T(8,128)S(1)}, f32[8,128]{1,0:T(8,128)S(1)}, u32[]{:S(2)}, u32[]{:S(2)}) collective-permute-start(f32[8,128]{1,0:T(8,128)S(1)} %maximum_maximum_fusion.3), channel_id=1, source_target_pairs={{0,8},{8,0},{16,24},{24,16},{32,40},{40,32},{48,56},{56,48},{64,72... | collective-permute-start | bytes 12296 | tf_op jit(solution)/shard_map/ppermute | solution.py:77
  42.4 2.5 %collective-permute-start.6 = (f32[8,128]{1,0:T(8,128)S(1)}, f32[8,128]{1,0:T(8,128)S(1)}, u32[]{:S(2)}, u32[]{:S(2)}) collective-permute-start(f32[8,128]{1,0:T(8,128)S(1)} %maximum_maximum_fusion.4), channel_id=1, source_target_pairs={{0,16},{8,24},{16,0},{24,8},{32,48},{40,56},{48,32},{56,40},{64,80... | collective-permute-start | bytes 12296 | tf_op jit(solution)/shard_map/ppermute | solution.py:77
  45.0 3.9 %collective-permute-start.7 = (f32[8,128]{1,0:T(8,128)S(1)}, f32[8,128]{1,0:T(8,128)S(1)}, u32[]{:S(2)}, u32[]{:S(2)}) collective-permute-start(f32[8,128]{1,0:T(8,128)S(1)} %maximum_maximum_fusion.5), channel_id=1, source_target_pairs={{0,32},{8,40},{16,48},{24,56},{32,0},{40,8},{48,16},{56,24},{64,96... | collective-permute-start | bytes 12296 | tf_op jit(solution)/shard_map/ppermute | solution.py:77
  49.0 11.8 %collective-permute-start.8 = (f32[8,128]{1,0:T(8,128)S(1)}, f32[8,128]{1,0:T(8,128)S(1)}, u32[]{:S(2)}, u32[]{:S(2)}) collective-permute-start(f32[8,128]{1,0:T(8,128)S(1)} %maximum_maximum_fusion.6), channel_id=1, source_target_pairs={{0,64},{8,72},{16,80},{24,88},{32,96},{40,104},{48,112},{56,120},{... | collective-permute-start | bytes 12296 | tf_op jit(solution)/shard_map/ppermute | solution.py:77
  55.2 17.2 %collective-permute-start = (f32[257,512]{1,0:T(8,128)S(1)}, f32[257,512]{1,0:T(8,128)S(1)}, u32[]{:S(2)}, u32[]{:S(2)}) collective-permute-start(f32[257,512]{1,0:T(8,128)S(1)} %pad_maximum_fusion.1), channel_id=1, source_target_pairs={{248,0},{0,8},{8,16},{16,24},{24,32},{32,40},{40,48},{48,56},{56,6... | collective-permute-start | bytes 1579016 | tf_op jit(solution)/shard_map/ppermute | solution.py:17
  60.9 5.0 %collective-permute-start.9 = (f32[8,128]{1,0:T(8,128)S(1)}, f32[8,128]{1,0:T(8,128)S(1)}, u32[]{:S(2)}, u32[]{:S(2)}) collective-permute-start(f32[8,128]{1,0:T(8,128)S(1)} %maximum_maximum_fusion.7), channel_id=1, source_target_pairs={{0,128},{8,136},{16,144},{24,152},{32,160},{40,168},{48,176},{56,1... | collective-permute-start | bytes 12296 | tf_op jit(solution)/shard_map/ppermute | solution.py:77

commit v4 on v3

--- a/solution.py
+++ b/solution.py
@@ -1,6 +1,8 @@
 import jax
 import jax.numpy as jnp
 from jax import lax
+from jax.experimental import pallas as pl
+from jax.experimental.pallas import tpu as pltpu
 from jax.sharding import Mesh
 from jax.sharding import PartitionSpec as P
 
@@ -17,6 +19,77 @@
     return lax.ppermute(block, axis, route)
 
 
+def steps_kernel(
+    current_ref, state_ref, prior_ref, transition_ref, drive_ref, decay_ref,
+    obs_matrix_ref, obs_weight_ref, observed_ref, state_out, logw_out,
+):
+    state = state_ref[...]
+    logw = prior_ref[...]
+    drive = drive_ref[...]
+    decay = decay_ref[...]
+    obs_weight = obs_weight_ref[...]
+    rounded = state.astype(jnp.bfloat16)
+    for step_index in range(STEPS):
+        drift = (
+            jnp.dot(rounded, transition_ref[...], preferred_element_type=jnp.float32)
+            + current_ref[step_index] * drive
+        )
+        state = decay * state + jnp.tanh(drift)
+        rounded = state.astype(jnp.bfloat16)
+        predicted = jnp.dot(rounded, obs_matrix_ref[...], preferred_element_type=jnp.float32)
+        misfit = predicted - observed_ref[step_index : step_index + 1, :]
+        logw = logw - 0.5 * jnp.sum(obs_weight * misfit * misfit, axis=1, keepdims=True)
+    state_out[...] = state
+    logw_out[...] = logw
+
+
+def run_steps(particles, log_prior, transition, drive_vector, current, decay_rate, obs_matrix, obs_weight, observed):
+    rows, width = particles.shape
+    n_obs = obs_matrix.shape[1]
+    block = 256
+    whole = lambda i: (0, 0)
+    state, logw = pl.pallas_call(
+        steps_kernel,
+        grid=(rows // block,),
+        in_specs=[
+            pl.BlockSpec(memory_space=pltpu.SMEM),
+            pl.BlockSpec((block, width), lambda i: (i, 0)),
+            pl.BlockSpec((block, 1), lambda i: (i, 0)),
+            pl.BlockSpec((width, width), whole),
+            pl.BlockSpec((1, width), whole),
+            pl.BlockSpec((1, width), whole),
+            pl.BlockSpec((width, n_obs), whole),
+            pl.BlockSpec((1, n_obs), whole),
+            pl.BlockSpec(observed.shape, whole),
+        ],
+        out_specs=[
+            pl.BlockSpec((block, width), lambda i: (i, 0)),
+            pl.BlockSpec((block, 1), lambda i: (i, 0)),
+        ],
+        out_shape=[
+            jax.ShapeDtypeStruct((rows, width), jnp.float32),
+            jax.ShapeDtypeStruct((rows, 1), jnp.float32),
+        ],
+        compiler_params=pltpu.CompilerParams(dimension_semantics=("arbitrary",)),
+        cost_estimate=pl.CostEstimate(
+            flops=2 * STEPS * rows * width * (width + n_obs),
+            transcendentals=STEPS * rows * width,
+            bytes_accessed=2 * rows * width * 4 + width * width * 2,
+        ),
+    )(
+        current,
+        particles,
+        log_prior.reshape(rows, 1),
+        transition,
+        drive_vector.reshape(1, width),
+        decay_rate.reshape(1, width),
+        obs_matrix,
+        obs_weight.reshape(1, n_obs),
+        observed,
+    )
+    return state, logw.reshape(rows)
+
+
 def window(
     particles,
     log_prior,
@@ -31,19 +104,9 @@
     cycle_pick,
     pair_pick,
 ):
-    state = particles
-    logw = log_prior
-    rounded = state.astype(jnp.bfloat16)
-    for step_index in range(STEPS):
-        drift = (
-            jnp.dot(rounded, transition, preferred_element_type=jnp.float32)
-            + current[step_index] * drive_vector
-        )
-        state = decay_rate * state + jnp.tanh(drift)
-        rounded = state.astype(jnp.bfloat16)
-        predicted = jnp.dot(rounded, obs_matrix, preferred_element_type=jnp.float32)
-        misfit = predicted - observed[step_index]
-        logw = logw - 0.5 * jnp.sum(obs_weight * misfit * misfit, axis=1)
+    state, logw = run_steps(
+        particles, log_prior, transition, drive_vector, current, decay_rate, obs_matrix, obs_weight, observed
+    )
     n_blk = lax.axis_size(BLK)
     n_pair = lax.axis_size(PAIR)
     groups = n_blk * n_pair

time: 82.9 us -> 83.9 us (1.012)
  Pallas kernels: 0 us -> 7.75 us
  matrix products: 8.19 us -> 2.68 us
    pallas_call x0 -> x1, Pallas kernels: none -> 7.75 us  [run_steps(): pl.pallas_call(steps_kernel, grid=(rows // block,), in_specs=[pl.BlockSpe...]
    dot_general x8 -> x0, matrix products: 7.1 us -> none  [the longest x4 5.12 us: window(): jnp.dot(rounded, transition, preferred_element_type=jnp.float32)]
    mul x1 -> x0, other arithmetic: 3.18 us -> none  [window(): current[step_index] * drive_vector]
    exp x0 -> x1, other arithmetic: none -> 2.57 us  [window(): expw = jnp.exp(logw - local_peak)]
    reshape x0 -> x1, local copies, waits for them, and re-layouts: none -> 1.71 us  [run_steps(): log_prior.reshape(rows, 1)]
    dot_general x1, matrix products: 1.09 us -> 2.68 us  [window(): weighted = jnp.dot(expw, state, precision=lax.Precision.HIGHEST)]
    slice x1 -> x0, local copies, waits for them, and re-layouts: 1.4 us -> none  [window(): current[step_index] * drive_vector]
    reduce_max x1, other arithmetic: 0.6 us -> 1.93 us  [window(): local_peak = jnp.max(logw)]
where the time goes in v4:
time: 83.9 us; the launch traced here: 83.4 us
  starting transfers between devices  27.5 us (33%)
  local copies, waits for them, and re-layouts  18.4 us (22%)
  other arithmetic  14.2 us (17%)
  between operations  8.43 us (10%)
  Pallas kernels  7.75 us (9%)
  waiting for transfers between devices  4.4 us (5%)
  matrix products  2.68 us (3%)
    ppermute x8, starting transfers between devices, window(): other = lax.ppermute(message, axis, [(i, i ^ bit) for i in range(size)])  22.8 us
    pallas_call x1, Pallas kernels, run_steps(): pl.pallas_call(steps_kernel, grid=(rows // block,), in_specs=[pl.BlockSpe...  7.75 us
    gather x1, local copies, waits for them, and re-layouts, window(): migrated = table[source]  4.87 us
    ppermute x2, starting transfers between devices, shifted(): return lax.ppermute(block, axis, route)  4.71 us
    ppermute x8, waiting for transfers between devices, window(): other = lax.ppermute(message, axis, [(i, i ^ bit) for i in range(size)])  4.4 us
    another operation x3, other arithmetic  3.86 us
    dot_general x1, matrix products, window(): weighted = jnp.dot(expw, state, precision=lax.Precision.HIGHEST)  2.68 us
    exp x1, other arithmetic, window(): expw = jnp.exp(logw - local_peak)  2.57 us
  transfers between devices with their start and end apart: 10, of which 4 were waited for; matrix products, arithmetic and copies ran while one was open for 18% of the time, Pallas kernels for 0%

profile of v4, /device:TPU:1, one launch (start us, length us, event | category | flops | bytes accessed | tf_op | source)
XLA Modules:
  0.0 83.4 jit_solution(4092560466248082538)
XLA Ops:
  0.6 0.7 copy.27
  1.3 1.7 %copy.15.prior_ref = f32[1024,1]{1,0:T(8,128)} copy(f32[1024,1]{0,1:T(1,128)} %bitcast.73) | data formatting | bytes 8192 | tf_op jit(solution)/shard_map/reshape | solution.py:82
  3.0 0.1 pad.35.clone
  3.1 7.8 %shard_map.139 = (f32[1024,512]{1,0:T(8,128)}, f32[1024,1]{1,0:T(8,128)}) custom-call(f32[4]{0:T(128)} %current_ref.1, f32[1024,512]{1,0:T(8,128)} %state_ref.1, f32[1024,1]{1,0:T(8,128)} %copy.15.prior_ref, bf16[512,512]{1,0:T(8,128)(2,1)} %transition_ref.1, f32[1,512]{1,0:T(1,128)} %bitcast.79, f32[1,512]{1,0:T(1,128)} %bitcast.80, ...), custom_call_target="tpu_custom_call" | custom-call | flops 2684354560 | bytes 4718592 | tf_op jit(solution)/shard_map/pallas_call | solution.py:51
  10.9 0.0 copy-start.2
  10.9 0.0 copy-start
  10.9 1.9 %reduce_max.9 = f32[]{:T(128)} reduce(f32[1024,1]{1,0:T(8,128)} %get-tuple-element.30, f32[]{:T(128)} %constant.69.clone.1), dimensions={0,1}, to_apply=%region_1.0 | reduce | flops 1023 | bytes 4104 | tf_op jit(solution)/shard_map/reduce_max | solution.py:117
  12.8 0.0 copy-start.1
  12.8 2.6 %fusion.3 = (f32[1024]{0:T(1024)S(1)}, f32[]{:T(128)}) fusion(f32[1024,1]{1,0:T(8,128)} %get-tuple-element.30, f32[]{:T(128)} %reduce_max.9), kind=kLoop, calls=%fused_computation.13 | loop fusion | flops 2047 | bytes 8200 | tf_op jit(solution)/shard_map/exp | solution.py:118
  15.4 0.7 pad.33.clone
  16.1 2.7 %fusion = f32[1,4,128]{2,0,1:T(1,128)S(1)} fusion(f32[1024,1,1]{0,1,2:T(1,128)S(1)} %bitcast.72, f32[1024,512]{1,0:T(8,128)} %get-tuple-element.29), kind=kOutput, calls=%fused_computation.8 | convolution fusion | flops 6291456 | bytes 2103296 | tf_op jit(solution)/shard_map/dot_general | solution.py:120
  18.8 0.7 squeeze.16
  19.4 0.1 maximum_maximum_fusion
  19.5 2.1 %collective-permute-start.2 = (f32[8,128]{1,0:T(8,128)S(1)}, f32[8,128]{1,0:T(8,128)S(1)}, u32[]{:S(2)}, u32[]{:S(2)}) collective-permute-start(f32[8,128]{1,0:T(8,128)S(1)} %maximum_maximum_fusion), channel_id=1, source_target_pairs={{0,1},{1,0},{2,3},{3,2},{4,5},{5,4},{6,7},{7,6},{8,9},{9,8},{10,11... | collective-permute-start | bytes 12296 | tf_op jit(solution)/shard_map/ppermute | solution.py:140
  21.6 0.0 copy-done.2
  21.6 0.7 gather_fusion.2
  22.3 0.7 slice.120
  23.0 0.6 compare_reduce_fusion.1
  24.9 0.0 copy-done
  24.9 0.6 gather_fusion.3
  25.5 0.6 compare_reduce_fusion
  26.2 2.6 %fusion.9 = f32[1,1]{1,0:T(1,128)} fusion(pred[1,1]{1,0:T(4,128)(4,1)} %bitcast.7, f32[1,1]{1,0:T(1,128)} %bitcast.8, s32[]{:T(128)} %bitcast.9, f32[1,1]{1,0:T(1,128)} %bitcast.6), kind=kLoop, calls=%fused_computation.77 | loop fusion | flops 1 | bytes 17 | tf_op jit(solution)/shard_map/select.3
  28.7 1.4 %scatter.25 = f32[1,512]{1,0:T(1,128)S(1)} dynamic-update-slice(f32[1,512]{1,0:T(1,128)S(1)} %scatter.24, f32[1,1]{1,0:T(1,128)} %fusion.9, s32[]{:T(128)} %constant.65.clone.1, s32[]{:T(128)} %bitcast.9) | dynamic-update-slice | bytes 12 | tf_op jit(solution)/shard_map/scatter | solution.py:121
  30.2 0.0 collective-permute-done.2
  30.2 0.7 exponential_bitcast_fusion.15
  30.8 0.6 multiply_add_fusion.7
  31.5 0.1 maximum_maximum_fusion.1
  31.5 2.5 %collective-permute-start.3 = (f32[8,128]{1,0:T(8,128)S(1)}, f32[8,128]{1,0:T(8,128)S(1)}, u32[]{:S(2)}, u32[]{:S(2)}) collective-permute-start(f32[8,128]{1,0:T(8,128)S(1)} %maximum_maximum_fusion.1), channel_id=1, source_target_pairs={{0,2},{1,3},{2,0},{3,1},{4,6},{5,7},{6,4},{7,5},{8,10},{9,11},{10,... | collective-permute-start | bytes 12296 | tf_op jit(solution)/shard_map/ppermute | solution.py:140
  34.0 1.4 %collective-permute-start.1 = (f32[33,512]{1,0:T(8,128)S(1)}, f32[33,512]{1,0:T(8,128)S(1)}, u32[]{:S(2)}, u32[]{:S(2)}) collective-permute-start(f32[33,512]{1,0:T(8,128)S(1)} %pad_maximum_fusion.2), channel_id=1, source_target_pairs={{4,0},{5,1},{6,2},{7,3},{0,4},{1,5},{2,6},{3,7},{12,8},{13,9},{14,... | collective-permute-start | bytes 202760 | tf_op jit(solution)/shard_map/ppermute | solution.py:19
  35.4 0.1 collective-permute-done.3
  35.6 0.1 maximum_maximum_fusion.2
  35.6 1.3 %collective-permute-start.4 = (f32[8,128]{1,0:T(8,128)S(1)}, f32[8,128]{1,0:T(8,128)S(1)}, u32[]{:S(2)}, u32[]{:S(2)}) collective-permute-start(f32[8,128]{1,0:T(8,128)S(1)} %maximum_maximum_fusion.2), channel_id=1, source_target_pairs={{0,4},{1,5},{2,6},{3,7},{4,0},{5,1},{6,2},{7,3},{8,12},{9,13},{10,... | collective-permute-start | bytes 12296 | tf_op jit(solution)/shard_map/ppermute | solution.py:140
  37.0 0.0 copy-done.1
  37.0 1.2 %collective-permute-done.4 = f32[8,128]{1,0:T(8,128)S(1)} collective-permute-done((f32[8,128]{1,0:T(8,128)S(1)}, f32[8,128]{1,0:T(8,128)S(1)}, u32[]{:S(2)}, u32[]{:S(2)}) %collective-permute-start.4) | collective-permute-done | bytes 4128 | tf_op jit(solution)/shard_map/ppermute | solution.py:140
  38.2 0.1 maximum_maximum_fusion.3
  38.2 3.5 %collective-permute-start.5 = (f32[8,128]{1,0:T(8,128)S(1)}, f32[8,128]{1,0:T(8,128)S(1)}, u32[]{:S(2)}, u32[]{:S(2)}) collective-permute-start(f32[8,128]{1,0:T(8,128)S(1)} %maximum_maximum_fusion.3), channel_id=1, source_target_pairs={{0,8},{8,0},{16,24},{24,16},{32,40},{40,32},{48,56},{56,48},{64,72... | collective-permute-start | bytes 12296 | tf_op jit(solution)/shard_map/ppermute | solution.py:140
  41.8 1.4 %gather_fusion = s32[256]{0:T(256)S(1)} fusion(s32[1024]{0:T(1024)S(1)} %copy.27, s32[1024]{0:T(1024)S(1)} %pad_clamp_fusion.3), kind=kCustom, calls=%fused_computation | custom fusion | bytes 3072 | tf_op jit(solution)/shard_map/gather | solution.py:123
  43.1 0.0 collective-permute-done.5
  43.2 0.1 maximum_maximum_fusion.4
  43.3 1.4 %collective-permute-start.6 = (f32[8,128]{1,0:T(8,128)S(1)}, f32[8,128]{1,0:T(8,128)S(1)}, u32[]{:S(2)}, u32[]{:S(2)}) collective-permute-start(f32[8,128]{1,0:T(8,128)S(1)} %maximum_maximum_fusion.4), channel_id=1, source_target_pairs={{0,16},{8,24},{16,0},{24,8},{32,48},{40,56},{48,32},{56,40},{64,80... | collective-permute-start | bytes 12296 | tf_op jit(solution)/shard_map/ppermute | solution.py:140
  44.7 1.1 %collective-permute-done.6 = f32[8,128]{1,0:T(8,128)S(1)} collective-permute-done((f32[8,128]{1,0:T(8,128)S(1)}, f32[8,128]{1,0:T(8,128)S(1)}, u32[]{:S(2)}, u32[]{:S(2)}) %collective-permute-start.6) | collective-permute-done | bytes 4128 | tf_op jit(solution)/shard_map/ppermute | solution.py:140
  45.8 0.1 maximum_maximum_fusion.5
  45.8 3.0 %collective-permute-start.7 = (f32[8,128]{1,0:T(8,128)S(1)}, f32[8,128]{1,0:T(8,128)S(1)}, u32[]{:S(2)}, u32[]{:S(2)}) collective-permute-start(f32[8,128]{1,0:T(8,128)S(1)} %maximum_maximum_fusion.5), channel_id=1, source_target_pairs={{0,32},{8,40},{16,48},{24,56},{32,0},{40,8},{48,16},{56,24},{64,96... | collective-permute-start | bytes 12296 | tf_op jit(solution)/shard_map/ppermute | solution.py:140
  48.8 1.0 %gather_fusion.1 = f32[256,512]{1,0:T(8,128)S(1)} fusion(f32[1024,512]{1,0:T(8,128)S(1)} %copy-done, s32[1024]{0:T(1024)S(1)} %pad_clamp_fusion.2), kind=kCustom, calls=%fused_computation.1 | custom fusion | bytes 1049600 | tf_op jit(solution)/shard_map/gather | solution.py:123
  49.8 0.0 collective-permute-done.7
  49.8 0.1 maximum_maximum_fusion.6
  49.9 6.1 %collective-permute-start.8 = (f32[8,128]{1,0:T(8,128)S(1)}, f32[8,128]{1,0:T(8,128)S(1)}, u32[]{:S(2)}, u32[]{:S(2)}) collective-permute-start(f32[8,128]{1,0:T(8,128)S(1)} %maximum_maximum_fusion.6), channel_id=1, source_target_pairs={{0,64},{8,72},{16,80},{24,88},{32,96},{40,104},{48,112},{56,120},{... | collective-permute-start | bytes 12296 | tf_op jit(solution)/shard_map/ppermute | solution.py:140
  56.1 3.3 %collective-permute-start = (f32[257,512]{1,0:T(8,128)S(1)}, f32[257,512]{1,0:T(8,128)S(1)}, u32[]{:S(2)}, u32[]{:S(2)}) collective-permute-start(f32[257,512]{1,0:T(8,128)S(1)} %pad_maximum_fusion.1), channel_id=1, source_target_pairs={{248,0},{0,8},{8,16},{16,24},{24,32},{32,40},{40,48},{48,56},{56,6... | collective-permute-start | bytes 1579016 | tf_op jit(solution)/shard_map/ppermute | solution.py:19
  59.4 1.4 %scatter_fusion = s32[1024]{0:T(1024)S(1)} fusion(s32[1024]{0:T(1024)S(1)} %copy.27, s32[256]{0:T(256)S(1)} %get-tuple-element.53, s32[256]{0:T(256)S(1)} %get-tuple-element.54), kind=kCustom, calls=%fused_computation.5 | custom fusion | bytes 4096 | tf_op jit(solution)/shard_map/scatter | solution.py:160
  60.8 0.7 scatter_fusion.1
  61.5 0.0 collective-permute-done.8
  61.5 0.1 maximum_maximum_fusion.7
  61.6 3.0 %collective-permute-start.9 = (f32[8,128]{1,0:T(8,128)S(1)}, f32[8,128]{1,0:T(8,128)S(1)}, u32[]{:S(2)}, u32[]{:S(2)}) collective-permute-start(f32[8,128]{1,0:T(8,128)S(1)} %maximum_maximum_fusion.7), channel_id=1, source_target_pairs={{0,128},{8,136},{16,144},{24,152},{32,160},{40,168},{48,176},{56,1... | collective-permute-start | bytes 12296 | tf_op jit(solution)/shard_map/ppermute | solution.py:140
  64.6 2.0 %collective-permute-done.9 = f32[8,128]{1,0:T(8,128)S(1)} collective-permute-done((f32[8,128]{1,0:T(8,128)S(1)}, f32[8,128]{1,0:T(8,128)S(1)}, u32[]{:S(2)}, u32[]{:S(2)}) %collective-permute-start.9) | collective-permute-done | bytes 4128 | tf_op jit(solution)/shard_map/ppermute | solution.py:140
  66.6 0.6 slice.142
  67.2 1.3 %divide_bitcast_fusion = f32[512]{0:T(512)} fusion(f32[5,128]{1,0:T(8,128)S(1)} %multiply_add_fusion, f32[]{:T(128)} %bitcast.34), kind=kLoop, calls=%fused_computation.43 | loop fusion | flops 512 | bytes 4100 | tf_op jit(solution)/shard_map/div | solution.py:149
  70.5 0.0 collective-permute-done.1
  70.5 0.6 fusion.8
  73.3 0.0 collective-permute-done
  73.3 0.6 fusion.7
  76.0 1.9 %pad_maximum_fusion = f32[1312,512]{1,0:T(8,128)S(1)} fusion(f32[32,512]{1,0:T(8,128)S(1)} %slice.157, f32[256,512]{1,0:T(8,128)S(1)} %slice.156, f32[1024,512]{1,0:T(8,128)} %get-tuple-element.29), kind=kLoop, calls=%fused_computation.7 | loop fusion | flops 1343488 | bytes 5373952 | tf_op jit(solution)/shard_map/concatenate | solution.py:164
  78.0 4.9 %gather_fusion.4 = f32[1024,512]{1,0:T(8,128)} fusion(f32[1312,512]{1,0:T(8,128)S(1)} %pad_maximum_fusion, s32[1024]{0:T(1024)S(1)} %fusion.5), kind=kCustom, calls=%fused_computation.4 | custom fusion | bytes 4198400 | tf_op jit(solution)/shard_map/gather | solution.py:165
  82.8 0.6 select_select_fusion
  (38 shorter events, 0.3 us)
Async XLA Ops:
  10.9 10.7 %copy-start.2 = (s32[32]{0:T(128)S(1)}, s32[32]{0:T(128)}, u32[]{:S(2)}) copy-start(s32[32]{0:T(128)} %param.27) | copy-start | bytes 388
  10.9 14.0 %copy-start = (f32[1024,512]{1,0:T(8,128)S(1)}, f32[1024,512]{1,0:T(8,128)}, u32[]{:S(2)}) copy-start(f32[1024,512]{1,0:T(8,128)} %get-tuple-element.29) | copy-start | bytes 6291460
  12.8 24.2 %copy-start.1 = (s32[256]{0:T(256)S(1)}, s32[256]{0:T(256)}, u32[]{:S(2)}) copy-start(s32[256]{0:T(256)} %param.26) | copy-start | bytes 3076
  19.5 10.7 %collective-permute-start.2 = (f32[8,128]{1,0:T(8,128)S(1)}, f32[8,128]{1,0:T(8,128)S(1)}, u32[]{:S(2)}, u32[]{:S(2)}) collective-permute-start(f32[8,128]{1,0:T(8,128)S(1)} %maximum_maximum_fusion), channel_id=1, source_target_pairs={{0,1},{1,0},{2,3},{3,2},{4,5},{5,4},{6,7},{7,6},{8,9},{9,8},{10,11... | collective-permute-start | bytes 12296 | tf_op jit(solution)/shard_map/ppermute | solution.py:140
  31.5 4.0 %collective-permute-start.3 = (f32[8,128]{1,0:T(8,128)S(1)}, f32[8,128]{1,0:T(8,128)S(1)}, u32[]{:S(2)}, u32[]{:S(2)}) collective-permute-start(f32[8,128]{1,0:T(8,128)S(1)} %maximum_maximum_fusion.1), channel_id=1, source_target_pairs={{0,2},{1,3},{2,0},{3,1},{4,6},{5,7},{6,4},{7,5},{8,10},{9,11},{10,... | collective-permute-start | bytes 12296 | tf_op jit(solution)/shard_map/ppermute | solution.py:140
  34.0 36.5 %collective-permute-start.1 = (f32[33,512]{1,0:T(8,128)S(1)}, f32[33,512]{1,0:T(8,128)S(1)}, u32[]{:S(2)}, u32[]{:S(2)}) collective-permute-start(f32[33,512]{1,0:T(8,128)S(1)} %pad_maximum_fusion.2), channel_id=1, source_target_pairs={{4,0},{5,1},{6,2},{7,3},{0,4},{1,5},{2,6},{3,7},{12,8},{13,9},{14,... | collective-permute-start | bytes 202760 | tf_op jit(solution)/shard_map/ppermute | solution.py:19
  35.6 2.5 %collective-permute-start.4 = (f32[8,128]{1,0:T(8,128)S(1)}, f32[8,128]{1,0:T(8,128)S(1)}, u32[]{:S(2)}, u32[]{:S(2)}) collective-permute-start(f32[8,128]{1,0:T(8,128)S(1)} %maximum_maximum_fusion.2), channel_id=1, source_target_pairs={{0,4},{1,5},{2,6},{3,7},{4,0},{5,1},{6,2},{7,3},{8,12},{9,13},{10,... | collective-permute-start | bytes 12296 | tf_op jit(solution)/shard_map/ppermute | solution.py:140
  38.2 4.9 %collective-permute-start.5 = (f32[8,128]{1,0:T(8,128)S(1)}, f32[8,128]{1,0:T(8,128)S(1)}, u32[]{:S(2)}, u32[]{:S(2)}) collective-permute-start(f32[8,128]{1,0:T(8,128)S(1)} %maximum_maximum_fusion.3), channel_id=1, source_target_pairs={{0,8},{8,0},{16,24},{24,16},{32,40},{40,32},{48,56},{56,48},{64,72... | collective-permute-start | bytes 12296 | tf_op jit(solution)/shard_map/ppermute | solution.py:140
  43.3 2.5 %collective-permute-start.6 = (f32[8,128]{1,0:T(8,128)S(1)}, f32[8,128]{1,0:T(8,128)S(1)}, u32[]{:S(2)}, u32[]{:S(2)}) collective-permute-start(f32[8,128]{1,0:T(8,128)S(1)} %maximum_maximum_fusion.4), channel_id=1, source_target_pairs={{0,16},{8,24},{16,0},{24,8},{32,48},{40,56},{48,32},{56,40},{64,80... | collective-permute-start | bytes 12296 | tf_op jit(solution)/shard_map/ppermute | solution.py:140
  45.8 3.9 %collective-permute-start.7 = (f32[8,128]{1,0:T(8,128)S(1)}, f32[8,128]{1,0:T(8,128)S(1)}, u32[]{:S(2)}, u32[]{:S(2)}) collective-permute-start(f32[8,128]{1,0:T(8,128)S(1)} %maximum_maximum_fusion.5), channel_id=1, source_target_pairs={{0,32},{8,40},{16,48},{24,56},{32,0},{40,8},{48,16},{56,24},{64,96... | collective-permute-start | bytes 12296 | tf_op jit(solution)/shard_map/ppermute | solution.py:140
  49.9 11.6 %collective-permute-start.8 = (f32[8,128]{1,0:T(8,128)S(1)}, f32[8,128]{1,0:T(8,128)S(1)}, u32[]{:S(2)}, u32[]{:S(2)}) collective-permute-start(f32[8,128]{1,0:T(8,128)S(1)} %maximum_maximum_fusion.6), channel_id=1, source_target_pairs={{0,64},{8,72},{16,80},{24,88},{32,96},{40,104},{48,112},{56,120},{... | collective-permute-start | bytes 12296 | tf_op jit(solution)/shard_map/ppermute | solution.py:140
  56.1 17.2 %collective-permute-start = (f32[257,512]{1,0:T(8,128)S(1)}, f32[257,512]{1,0:T(8,128)S(1)}, u32[]{:S(2)}, u32[]{:S(2)}) collective-permute-start(f32[257,512]{1,0:T(8,128)S(1)} %pad_maximum_fusion.1), channel_id=1, source_target_pairs={{248,0},{0,8},{8,16},{16,24},{24,32},{32,40},{40,48},{48,56},{56,6... | collective-permute-start | bytes 1579016 | tf_op jit(solution)/shard_map/ppermute | solution.py:19
  61.6 5.0 %collective-permute-start.9 = (f32[8,128]{1,0:T(8,128)S(1)}, f32[8,128]{1,0:T(8,128)S(1)}, u32[]{:S(2)}, u32[]{:S(2)}) collective-permute-start(f32[8,128]{1,0:T(8,128)S(1)} %maximum_maximum_fusion.7), channel_id=1, source_target_pairs={{0,128},{8,136},{16,144},{24,152},{32,160},{40,168},{48,176},{56,1... | collective-permute-start | bytes 12296 | tf_op jit(solution)/shard_map/ppermute | solution.py:140

commit v5 on v4

--- a/solution.py
+++ b/solution.py
@@ -21,8 +21,10 @@
 
 def steps_kernel(
     current_ref, state_ref, prior_ref, transition_ref, drive_ref, decay_ref,
-    obs_matrix_ref, obs_weight_ref, observed_ref, state_out, logw_out,
+    obs_matrix_ref, obs_weight_ref, observed_ref, state_out, message_out,
+    peak_acc, sum_acc, weighted_acc,
 ):
+    block = pl.program_id(0)
     state = state_ref[...]
     logw = prior_ref[...]
     drive = drive_ref[...]
@@ -40,15 +42,43 @@
         misfit = predicted - observed_ref[step_index : step_index + 1, :]
         logw = logw - 0.5 * jnp.sum(obs_weight * misfit * misfit, axis=1, keepdims=True)
     state_out[...] = state
-    logw_out[...] = logw
+
+    @pl.when(block == 0)
+    def _():
+        peak_acc[...] = jnp.full(peak_acc.shape, -jnp.inf, jnp.float32)
+        sum_acc[...] = jnp.zeros(sum_acc.shape, jnp.float32)
+        weighted_acc[...] = jnp.zeros(weighted_acc.shape, jnp.float32)
+
+    old_peak = peak_acc[...]
+    new_peak = jnp.maximum(old_peak, jnp.max(logw, axis=0, keepdims=True))
+    scale = jnp.exp(old_peak - new_peak)
+    expw = jnp.exp(logw - new_peak[:, :1])
+    sum_acc[...] = sum_acc[...] * scale + jnp.sum(expw, axis=0, keepdims=True)
+    weighted_acc[...] = weighted_acc[...] * scale[:, :1] + jnp.sum(expw * state, axis=0, keepdims=True)
+    peak_acc[...] = new_peak
+
+    @pl.when(block == pl.num_programs(0) - 1)
+    def _():
+        lanes = peak_acc.shape[1]
+        k = weighted_acc.shape[1] // lanes
+        for row in range(k):
+            message_out[row : row + 1, :] = weighted_acc[:, row * lanes : (row + 1) * lanes]
+        message_out[k : k + 1, :] = sum_acc[...]
+        message_out[k + 1 : k + 2, :] = peak_acc[...]
+        rest = message_out.shape[0] - (k + 2)
+        if rest:
+            message_out[k + 2 :, :] = jnp.zeros((rest, lanes), jnp.float32)
 
 
 def run_steps(particles, log_prior, transition, drive_vector, current, decay_rate, obs_matrix, obs_weight, observed):
     rows, width = particles.shape
     n_obs = obs_matrix.shape[1]
     block = 256
+    lanes = 128
+    k = width // lanes
+    message_rows = max(-(-(k + 2) // 8) * 8, 2 * k)
     whole = lambda i: (0, 0)
-    state, logw = pl.pallas_call(
+    return pl.pallas_call(
         steps_kernel,
         grid=(rows // block,),
         in_specs=[
@@ -64,11 +94,16 @@
         ],
         out_specs=[
             pl.BlockSpec((block, width), lambda i: (i, 0)),
-            pl.BlockSpec((block, 1), lambda i: (i, 0)),
+            pl.BlockSpec((message_rows, lanes), whole),
         ],
         out_shape=[
             jax.ShapeDtypeStruct((rows, width), jnp.float32),
-            jax.ShapeDtypeStruct((rows, 1), jnp.float32),
+            jax.ShapeDtypeStruct((message_rows, lanes), jnp.float32),
+        ],
+        scratch_shapes=[
+            pltpu.VMEM((1, lanes), jnp.float32),
+            pltpu.VMEM((1, lanes), jnp.float32),
+            pltpu.VMEM((1, width), jnp.float32),
         ],
         compiler_params=pltpu.CompilerParams(dimension_semantics=("arbitrary",)),
         cost_estimate=pl.CostEstimate(
@@ -87,7 +122,6 @@
         obs_weight.reshape(1, n_obs),
         observed,
     )
-    return state, logw.reshape(rows)
 
 
 def window(
@@ -104,7 +138,7 @@
     cycle_pick,
     pair_pick,
 ):
-    state, logw = run_steps(
+    state, message = run_steps(
         particles, log_prior, transition, drive_vector, current, decay_rate, obs_matrix, obs_weight, observed
     )
     n_blk = lax.axis_size(BLK)
@@ -113,26 +147,15 @@
     rows_here, width = state.shape
     n_cycle = cycle_pick.shape[0]
     n_pairs = pair_pick.shape[0]
-
-    local_peak = jnp.max(logw)
-    expw = jnp.exp(logw - local_peak)
-    local_sum = jnp.sum(expw)
-    weighted = jnp.dot(expw, state, precision=lax.Precision.HIGHEST)
-    stamp = jnp.zeros((1, width), jnp.float32).at[0, 0].set(local_peak).at[0, 1].set(local_sum)
+    lanes = message.shape[1]
+    k = width // lanes
+    local_sum = message[k, 0]
+    local_peak = message[k + 1, 0]
+    stamp = message[k : 2 * k].reshape(1, width)
 
     cycle_in = shifted(jnp.concatenate([state[ancestors[cycle_pick]], stamp]), BLK, 1)
     pair_in = shifted(jnp.concatenate([state[ancestors[pair_pick]], stamp]), PAIR, n_pair // 2)
 
-    lanes = 128
-    k = width // lanes
-    message = jnp.concatenate(
-        [
-            weighted.reshape(k, lanes),
-            jnp.full((1, lanes), local_sum),
-            jnp.full((1, lanes), local_peak),
-            jnp.zeros((8 - (k + 2) % 8 if (k + 2) % 8 else 0, lanes), jnp.float32),
-        ]
-    )
     pad = message.shape[0] - (k + 2)
     for axis, size in ((PAIR, n_pair), (BLK, n_blk)):
         bit = 1
@@ -152,8 +175,8 @@
         return jnp.log(jnp.maximum(groups * (device_sum * jnp.exp(device_peak - peak)) / total, 0.1))
 
     own_w = group_weight(local_peak, local_sum)
-    cycle_w = group_weight(cycle_in[n_cycle, 0], cycle_in[n_cycle, 1])
-    pair_w = group_weight(pair_in[n_pairs, 0], pair_in[n_pairs, 1])
+    cycle_w = group_weight(cycle_in[n_cycle, lanes], cycle_in[n_cycle, 0])
+    pair_w = group_weight(pair_in[n_pairs, lanes], pair_in[n_pairs, 0])
 
     source = (
         ancestors.at[cycle_pick]

time: 83.9 us -> 72.8 us (0.87)
  other arithmetic: 14.2 us -> 5.85 us
  waiting for transfers between devices: 4.4 us -> 7.81 us
  starting transfers between devices: 27.5 us -> 24.5 us
  matrix products: 2.68 us -> 0 us
  between operations: 8.43 us -> 6.94 us
  Pallas kernels: 7.75 us -> 8.79 us
    another operation x3 -> x0, other arithmetic: 3.86 us -> none
    ppermute x8, waiting for transfers between devices: 4.4 us -> 7.81 us  [window(): other = lax.ppermute(message, axis, [(i, i ^ bit) for i in range(size)])]
    ppermute x8, starting transfers between devices: 22.8 us -> 20 us  [window(): other = lax.ppermute(message, axis, [(i, i ^ bit) for i in range(size)])]
    dot_general x1 -> x0, matrix products: 2.68 us -> none  [window(): weighted = jnp.dot(expw, state, precision=lax.Precision.HIGHEST)]
    exp x1 -> x0, other arithmetic: 2.57 us -> none  [window(): expw = jnp.exp(logw - local_peak)]
    reduce_max x1 -> x0, other arithmetic: 1.93 us -> none  [window(): local_peak = jnp.max(logw)]
    slice x2 -> x4, local copies, waits for them, and re-layouts: 1.27 us -> 3.14 us  [the longest x1 1.36 us: window(): local_peak = message[k + 1, 0]]
    gather x1, local copies, waits for them, and re-layouts: 0.6 us -> 2.22 us  [window(): state[ancestors[pair_pick]]]
  transfers between devices with their start and end apart: 10 -> 10, of which waited for: 4 -> 4; matrix products, arithmetic and copies ran while one was open for 18% -> 19% of each run, Pallas kernels for 0% -> 0%
where the time goes in v5:
time: 72.8 us; the launch traced here: 72.4 us
  starting transfers between devices  24.5 us (34%)
  local copies, waits for them, and re-layouts  18.4 us (25%)
  Pallas kernels  8.79 us (12%)
  waiting for transfers between devices  7.81 us (11%)
  between operations  6.94 us (10%)
  other arithmetic  5.85 us (8%)
    ppermute x8, starting transfers between devices, window(): other = lax.ppermute(message, axis, [(i, i ^ bit) for i in range(size)])  20 us
    pallas_call x1, Pallas kernels, run_steps(): pl.pallas_call(steps_kernel, grid=(rows // block,), in_specs=[pl.BlockSpe...  8.79 us
    ppermute x8, waiting for transfers between devices, window(): other = lax.ppermute(message, axis, [(i, i ^ bit) for i in range(size)])  7.81 us
    gather x1, local copies, waits for them, and re-layouts, window(): migrated = table[source]  4.87 us
    ppermute x2, starting transfers between devices, shifted(): return lax.ppermute(block, axis, route)  4.56 us
    gather x1, local copies, waits for them, and re-layouts, window(): state[ancestors[pair_pick]]  2.22 us
    scatter x2, local copies, waits for them, and re-layouts, window(): source = ancestors.at[cycle_pick].set(rows_here + jnp.arange(n_cycle, dty...  2.09 us
    concatenate x1, other arithmetic, window(): jnp.concatenate([state, cycle_in[:n_cycle], pair_in[:n_pairs]], axis=0)  1.9 us
  transfers between devices with their start and end apart: 10, of which 4 were waited for; matrix products, arithmetic and copies ran while one was open for 19% of the time, Pallas kernels for 0%

profile of v5, /device:TPU:1, one launch (start us, length us, event | category | flops | bytes accessed | tf_op | source)
XLA Modules:
  0.0 72.4 jit_solution(15770745592505207094)
XLA Ops:
  0.6 0.7 copy.19
  1.3 1.7 %copy.15.prior_ref = f32[1024,1]{1,0:T(8,128)} copy(f32[1024,1]{0,1:T(1,128)} %bitcast.54) | data formatting | bytes 8192 | tf_op jit(solution)/shard_map/reshape | solution.py:117
  3.0 0.0 copy-start.2
  3.0 0.0 copy-start.1
  3.0 8.8 %shard_map.139 = (f32[1024,512]{1,0:T(8,128)}, f32[8,128]{1,0:T(8,128)}) custom-call(f32[4]{0:T(128)} %current_ref.1, f32[1024,512]{1,0:T(8,128)} %state_ref.1, f32[1024,1]{1,0:T(8,128)} %copy.15.prior_ref, bf16[512,512]{1,0:T(8,128)(2,1)} %transition_ref.1, f32[1,512]{1,0:T(1,128)} %bitcast.60, f32[1,512]{1,0:T(1,128)} %bitcast.61, ...), custom_call_target="tpu_custom_call" | custom-call | flops 2684354560 | bytes 4718592 | tf_op jit(solution)/shard_map/pallas_call | solution.py:81
  11.8 0.0 copy-start
  11.8 2.1 %collective-permute-start.2 = (f32[8,128]{1,0:T(8,128)}, f32[8,128]{1,0:T(8,128)S(1)}, u32[]{:S(2)}, u32[]{:S(2)}) collective-permute-start(f32[8,128]{1,0:T(8,128)} %get-tuple-element.6), channel_id=1, source_target_pairs={{0,1},{1,0},{2,3},{3,2},{4,5},{5,4},{6,7},{7,6},{8,9},{9,8},{10,11... | collective-permute-start | bytes 12296 | tf_op jit(solution)/shard_map/ppermute | solution.py:163
  14.0 0.7 slice.99
  14.7 0.0 copy-done.2
  14.7 0.7 gather_fusion.2
  15.4 2.2 %gather_fusion.3 = f32[32,512]{1,0:T(8,128)S(1)} fusion(f32[1024,512]{1,0:T(8,128)} %get-tuple-element.5, s32[1024]{0:T(1024)S(1)} %pad_clamp_fusion), kind=kCustom, calls=%fused_computation.3 | custom fusion | bytes 131200 | tf_op jit(solution)/shard_map/gather | solution.py:157
  17.6 1.4 %collective-permute-start.1 = (f32[33,512]{1,0:T(8,128)S(1)}, f32[33,512]{1,0:T(8,128)S(1)}, u32[]{:S(2)}, u32[]{:S(2)}) collective-permute-start(f32[33,512]{1,0:T(8,128)S(1)} %pad_maximum_fusion.2), channel_id=1, source_target_pairs={{4,0},{5,1},{6,2},{7,3},{0,4},{1,5},{2,6},{3,7},{12,8},{13,9},{14,... | collective-permute-start | bytes 202760 | tf_op jit(solution)/shard_map/ppermute | solution.py:19
  19.0 0.1 pad.20.clone
  19.1 0.0 collective-permute-done.2
  19.1 0.7 exponential_bitcast_fusion.15
  19.8 0.7 multiply_add_fusion.7
  20.5 0.1 maximum_maximum_fusion
  20.6 2.5 %collective-permute-start.3 = (f32[8,128]{1,0:T(8,128)S(1)}, f32[8,128]{1,0:T(8,128)S(1)}, u32[]{:S(2)}, u32[]{:S(2)}) collective-permute-start(f32[8,128]{1,0:T(8,128)S(1)} %maximum_maximum_fusion), channel_id=1, source_target_pairs={{0,2},{1,3},{2,0},{3,1},{4,6},{5,7},{6,4},{7,5},{8,10},{9,11},{10,... | collective-permute-start | bytes 12296 | tf_op jit(solution)/shard_map/ppermute | solution.py:163
  23.0 0.0 copy-done.1
  23.0 1.5 %collective-permute-done.3 = f32[8,128]{1,0:T(8,128)S(1)} collective-permute-done((f32[8,128]{1,0:T(8,128)S(1)}, f32[8,128]{1,0:T(8,128)S(1)}, u32[]{:S(2)}, u32[]{:S(2)}) %collective-permute-start.3) | collective-permute-done | bytes 4128 | tf_op jit(solution)/shard_map/ppermute | solution.py:163
  24.6 0.1 maximum_maximum_fusion.1
  24.6 0.2 collective-permute-start.4
  24.9 1.4 %gather_fusion = s32[256]{0:T(256)S(1)} fusion(s32[1024]{0:T(1024)S(1)} %copy.19, s32[1024]{0:T(1024)S(1)} %pad_clamp_fusion.3), kind=kCustom, calls=%fused_computation | custom fusion | bytes 3072 | tf_op jit(solution)/shard_map/gather | solution.py:156
  26.2 0.9 %collective-permute-done.4 = f32[8,128]{1,0:T(8,128)S(1)} collective-permute-done((f32[8,128]{1,0:T(8,128)S(1)}, f32[8,128]{1,0:T(8,128)S(1)}, u32[]{:S(2)}, u32[]{:S(2)}) %collective-permute-start.4) | collective-permute-done | bytes 4128 | tf_op jit(solution)/shard_map/ppermute | solution.py:163
  27.2 0.1 maximum_maximum_fusion.2
  27.2 3.6 %collective-permute-start.5 = (f32[8,128]{1,0:T(8,128)S(1)}, f32[8,128]{1,0:T(8,128)S(1)}, u32[]{:S(2)}, u32[]{:S(2)}) collective-permute-start(f32[8,128]{1,0:T(8,128)S(1)} %maximum_maximum_fusion.2), channel_id=1, source_target_pairs={{0,8},{8,0},{16,24},{24,16},{32,40},{40,32},{48,56},{56,48},{64,72... | collective-permute-start | bytes 12296 | tf_op jit(solution)/shard_map/ppermute | solution.py:163
  30.8 0.8 %collective-permute-done.5 = f32[8,128]{1,0:T(8,128)S(1)} collective-permute-done((f32[8,128]{1,0:T(8,128)S(1)}, f32[8,128]{1,0:T(8,128)S(1)}, u32[]{:S(2)}, u32[]{:S(2)}) %collective-permute-start.5) | collective-permute-done | bytes 4128 | tf_op jit(solution)/shard_map/ppermute | solution.py:163
  31.7 0.1 maximum_maximum_fusion.3
  31.7 1.7 %collective-permute-start.6 = (f32[8,128]{1,0:T(8,128)S(1)}, f32[8,128]{1,0:T(8,128)S(1)}, u32[]{:S(2)}, u32[]{:S(2)}) collective-permute-start(f32[8,128]{1,0:T(8,128)S(1)} %maximum_maximum_fusion.3), channel_id=1, source_target_pairs={{0,16},{8,24},{16,0},{24,8},{32,48},{40,56},{48,32},{56,40},{64,80... | collective-permute-start | bytes 12296 | tf_op jit(solution)/shard_map/ppermute | solution.py:163
  33.4 0.0 copy-done
  33.4 1.0 %gather_fusion.1 = f32[256,512]{1,0:T(8,128)S(1)} fusion(f32[1024,512]{1,0:T(8,128)S(1)} %copy-done, s32[1024]{0:T(1024)S(1)} %pad_clamp_fusion.2), kind=kCustom, calls=%fused_computation.1 | custom fusion | bytes 1049600 | tf_op jit(solution)/shard_map/gather | solution.py:156
  34.4 0.0 collective-permute-done.6
  34.4 0.1 maximum_maximum_fusion.4
  34.5 3.0 %collective-permute-start.7 = (f32[8,128]{1,0:T(8,128)S(1)}, f32[8,128]{1,0:T(8,128)S(1)}, u32[]{:S(2)}, u32[]{:S(2)}) collective-permute-start(f32[8,128]{1,0:T(8,128)S(1)} %maximum_maximum_fusion.4), channel_id=1, source_target_pairs={{0,32},{8,40},{16,48},{24,56},{32,0},{40,8},{48,16},{56,24},{64,96... | collective-permute-start | bytes 12296 | tf_op jit(solution)/shard_map/ppermute | solution.py:163
  37.6 3.2 %collective-permute-start = (f32[257,512]{1,0:T(8,128)S(1)}, f32[257,512]{1,0:T(8,128)S(1)}, u32[]{:S(2)}, u32[]{:S(2)}) collective-permute-start(f32[257,512]{1,0:T(8,128)S(1)} %pad_maximum_fusion.1), channel_id=1, source_target_pairs={{248,0},{0,8},{8,16},{16,24},{24,32},{32,40},{40,48},{48,56},{56,6... | collective-permute-start | bytes 1579016 | tf_op jit(solution)/shard_map/ppermute | solution.py:19
  40.8 1.4 %scatter_fusion = s32[1024]{0:T(1024)S(1)} fusion(s32[1024]{0:T(1024)S(1)} %copy.19, s32[256]{0:T(256)S(1)} %get-tuple-element.29, s32[256]{0:T(256)S(1)} %get-tuple-element.30), kind=kCustom, calls=%fused_computation.5 | custom fusion | bytes 4096 | tf_op jit(solution)/shard_map/scatter | solution.py:183
  42.2 0.7 scatter_fusion.1
  42.9 0.0 collective-permute-done.7
  42.9 0.1 maximum_maximum_fusion.5
  43.0 4.2 %collective-permute-start.8 = (f32[8,128]{1,0:T(8,128)S(1)}, f32[8,128]{1,0:T(8,128)S(1)}, u32[]{:S(2)}, u32[]{:S(2)}) collective-permute-start(f32[8,128]{1,0:T(8,128)S(1)} %maximum_maximum_fusion.5), channel_id=1, source_target_pairs={{0,64},{8,72},{16,80},{24,88},{32,96},{40,104},{48,112},{56,120},{... | collective-permute-start | bytes 12296 | tf_op jit(solution)/shard_map/ppermute | solution.py:163
  47.2 4.6 %collective-permute-done.8 = f32[8,128]{1,0:T(8,128)S(1)} collective-permute-done((f32[8,128]{1,0:T(8,128)S(1)}, f32[8,128]{1,0:T(8,128)S(1)}, u32[]{:S(2)}, u32[]{:S(2)}) %collective-permute-start.8) | collective-permute-done | bytes 4128 | tf_op jit(solution)/shard_map/ppermute | solution.py:163
  51.8 0.1 maximum_maximum_fusion.6
  51.9 2.7 %collective-permute-start.9 = (f32[8,128]{1,0:T(8,128)S(1)}, f32[8,128]{1,0:T(8,128)S(1)}, u32[]{:S(2)}, u32[]{:S(2)}) collective-permute-start(f32[8,128]{1,0:T(8,128)S(1)} %maximum_maximum_fusion.6), channel_id=1, source_target_pairs={{0,128},{8,136},{16,144},{24,152},{32,160},{40,168},{48,176},{56,1... | collective-permute-start | bytes 12296 | tf_op jit(solution)/shard_map/ppermute | solution.py:163
  54.6 1.4 %fusion.4 = (f32[1,1]{1,0:T(1,128)}, f32[1,1]{1,0:T(1,128)}) fusion(f32[8,128]{1,0:T(8,128)} %get-tuple-element.6), kind=kLoop, calls=%fused_computation.66 | loop fusion | bytes 16 | tf_op jit(solution)/shard_map/slice | solution.py:153
  55.9 0.0 collective-permute-done.9
  56.0 0.6 slice.123
  56.5 1.2 %divide_bitcast_fusion = f32[512]{0:T(512)} fusion(f32[5,128]{1,0:T(8,128)S(1)} %multiply_add_fusion, f32[]{:T(128)} %bitcast.26), kind=kLoop, calls=%fused_computation.36 | loop fusion | flops 512 | bytes 4100 | tf_op jit(solution)/shard_map/div | solution.py:172
  59.8 0.0 collective-permute-done.1
  59.8 0.5 fusion.3
  62.4 0.0 collective-permute-done
  62.4 0.5 fusion.2
  65.0 1.9 %pad_maximum_fusion = f32[1312,512]{1,0:T(8,128)S(1)} fusion(f32[32,512]{1,0:T(8,128)S(1)} %slice.140, f32[256,512]{1,0:T(8,128)S(1)} %slice.139, f32[1024,512]{1,0:T(8,128)} %get-tuple-element.5), kind=kLoop, calls=%fused_computation.7 | loop fusion | flops 1343488 | bytes 5373952 | tf_op jit(solution)/shard_map/concatenate | solution.py:187
  66.9 4.9 %gather_fusion.4 = f32[1024,512]{1,0:T(8,128)} fusion(f32[1312,512]{1,0:T(8,128)S(1)} %pad_maximum_fusion, s32[1024]{0:T(1024)S(1)} %fusion), kind=kCustom, calls=%fused_computation.4 | custom fusion | bytes 4198400 | tf_op jit(solution)/shard_map/gather | solution.py:188
  71.8 0.6 select_select_fusion
  (36 shorter events, 0.3 us)
Async XLA Ops:
  3.0 11.6 %copy-start.2 = (s32[32]{0:T(128)S(1)}, s32[32]{0:T(128)}, u32[]{:S(2)}) copy-start(s32[32]{0:T(128)} %param.23) | copy-start | bytes 388
  3.0 20.0 %copy-start.1 = (s32[256]{0:T(256)S(1)}, s32[256]{0:T(256)}, u32[]{:S(2)}) copy-start(s32[256]{0:T(256)} %param.22) | copy-start | bytes 3076
  11.8 21.6 %copy-start = (f32[1024,512]{1,0:T(8,128)S(1)}, f32[1024,512]{1,0:T(8,128)}, u32[]{:S(2)}) copy-start(f32[1024,512]{1,0:T(8,128)} %get-tuple-element.5) | copy-start | bytes 6291460
  11.8 7.3 %collective-permute-start.2 = (f32[8,128]{1,0:T(8,128)}, f32[8,128]{1,0:T(8,128)S(1)}, u32[]{:S(2)}, u32[]{:S(2)}) collective-permute-start(f32[8,128]{1,0:T(8,128)} %get-tuple-element.6), channel_id=1, source_target_pairs={{0,1},{1,0},{2,3},{3,2},{4,5},{5,4},{6,7},{7,6},{8,9},{9,8},{10,11... | collective-permute-start | bytes 12296 | tf_op jit(solution)/shard_map/ppermute | solution.py:163
  17.6 42.2 %collective-permute-start.1 = (f32[33,512]{1,0:T(8,128)S(1)}, f32[33,512]{1,0:T(8,128)S(1)}, u32[]{:S(2)}, u32[]{:S(2)}) collective-permute-start(f32[33,512]{1,0:T(8,128)S(1)} %pad_maximum_fusion.2), channel_id=1, source_target_pairs={{4,0},{5,1},{6,2},{7,3},{0,4},{1,5},{2,6},{3,7},{12,8},{13,9},{14,... | collective-permute-start | bytes 202760 | tf_op jit(solution)/shard_map/ppermute | solution.py:19
  20.6 4.0 %collective-permute-start.3 = (f32[8,128]{1,0:T(8,128)S(1)}, f32[8,128]{1,0:T(8,128)S(1)}, u32[]{:S(2)}, u32[]{:S(2)}) collective-permute-start(f32[8,128]{1,0:T(8,128)S(1)} %maximum_maximum_fusion), channel_id=1, source_target_pairs={{0,2},{1,3},{2,0},{3,1},{4,6},{5,7},{6,4},{7,5},{8,10},{9,11},{10,... | collective-permute-start | bytes 12296 | tf_op jit(solution)/shard_map/ppermute | solution.py:163
  24.6 2.5 %collective-permute-start.4 = (f32[8,128]{1,0:T(8,128)S(1)}, f32[8,128]{1,0:T(8,128)S(1)}, u32[]{:S(2)}, u32[]{:S(2)}) collective-permute-start(f32[8,128]{1,0:T(8,128)S(1)} %maximum_maximum_fusion.1), channel_id=1, source_target_pairs={{0,4},{1,5},{2,6},{3,7},{4,0},{5,1},{6,2},{7,3},{8,12},{9,13},{10,... | collective-permute-start | bytes 12296 | tf_op jit(solution)/shard_map/ppermute | solution.py:163
  27.2 4.4 %collective-permute-start.5 = (f32[8,128]{1,0:T(8,128)S(1)}, f32[8,128]{1,0:T(8,128)S(1)}, u32[]{:S(2)}, u32[]{:S(2)}) collective-permute-start(f32[8,128]{1,0:T(8,128)S(1)} %maximum_maximum_fusion.2), channel_id=1, source_target_pairs={{0,8},{8,0},{16,24},{24,16},{32,40},{40,32},{48,56},{56,48},{64,72... | collective-permute-start | bytes 12296 | tf_op jit(solution)/shard_map/ppermute | solution.py:163
  31.7 2.7 %collective-permute-start.6 = (f32[8,128]{1,0:T(8,128)S(1)}, f32[8,128]{1,0:T(8,128)S(1)}, u32[]{:S(2)}, u32[]{:S(2)}) collective-permute-start(f32[8,128]{1,0:T(8,128)S(1)} %maximum_maximum_fusion.3), channel_id=1, source_target_pairs={{0,16},{8,24},{16,0},{24,8},{32,48},{40,56},{48,32},{56,40},{64,80... | collective-permute-start | bytes 12296 | tf_op jit(solution)/shard_map/ppermute | solution.py:163
  34.5 8.4 %collective-permute-start.7 = (f32[8,128]{1,0:T(8,128)S(1)}, f32[8,128]{1,0:T(8,128)S(1)}, u32[]{:S(2)}, u32[]{:S(2)}) collective-permute-start(f32[8,128]{1,0:T(8,128)S(1)} %maximum_maximum_fusion.4), channel_id=1, source_target_pairs={{0,32},{8,40},{16,48},{24,56},{32,0},{40,8},{48,16},{56,24},{64,96... | collective-permute-start | bytes 12296 | tf_op jit(solution)/shard_map/ppermute | solution.py:163
  37.6 24.8 %collective-permute-start = (f32[257,512]{1,0:T(8,128)S(1)}, f32[257,512]{1,0:T(8,128)S(1)}, u32[]{:S(2)}, u32[]{:S(2)}) collective-permute-start(f32[257,512]{1,0:T(8,128)S(1)} %pad_maximum_fusion.1), channel_id=1, source_target_pairs={{248,0},{0,8},{8,16},{16,24},{24,32},{32,40},{40,48},{48,56},{56,6... | collective-permute-start | bytes 1579016 | tf_op jit(solution)/shard_map/ppermute | solution.py:19
  43.0 8.8 %collective-permute-start.8 = (f32[8,128]{1,0:T(8,128)S(1)}, f32[8,128]{1,0:T(8,128)S(1)}, u32[]{:S(2)}, u32[]{:S(2)}) collective-permute-start(f32[8,128]{1,0:T(8,128)S(1)} %maximum_maximum_fusion.5), channel_id=1, source_target_pairs={{0,64},{8,72},{16,80},{24,88},{32,96},{40,104},{48,112},{56,120},{... | collective-permute-start | bytes 12296 | tf_op jit(solution)/shard_map/ppermute | solution.py:163
  51.9 4.0 %collective-permute-start.9 = (f32[8,128]{1,0:T(8,128)S(1)}, f32[8,128]{1,0:T(8,128)S(1)}, u32[]{:S(2)}, u32[]{:S(2)}) collective-permute-start(f32[8,128]{1,0:T(8,128)S(1)} %maximum_maximum_fusion.6), channel_id=1, source_target_pairs={{0,128},{8,136},{16,144},{24,152},{32,160},{40,168},{48,176},{56,1... | collective-permute-start | bytes 12296 | tf_op jit(solution)/shard_map/ppermute | solution.py:163

commit v6 on v5

--- a/solution.py
+++ b/solution.py
@@ -153,8 +153,10 @@
     local_peak = message[k + 1, 0]
     stamp = message[k : 2 * k].reshape(1, width)
 
-    cycle_in = shifted(jnp.concatenate([state[ancestors[cycle_pick]], stamp]), BLK, 1)
-    pair_in = shifted(jnp.concatenate([state[ancestors[pair_pick]], stamp]), PAIR, n_pair // 2)
+    cycle_out = jnp.concatenate([state[ancestors[cycle_pick]], stamp])
+    pair_out = jnp.concatenate([state[ancestors[pair_pick]], stamp])
+    cycle_in = shifted(cycle_out, BLK, 1)
+    pair_in = shifted(pair_out, PAIR, n_pair // 2)
 
     pad = message.shape[0] - (k + 2)
     for axis, size in ((PAIR, n_pair), (BLK, n_blk)):

time: 72.8 us -> 72.8 us (level)
  no operation moved by 1% of the time
where the time goes in v6:
time: 72.8 us; the launch traced here: 72.4 us
  starting transfers between devices  24.5 us (34%)
  local copies, waits for them, and re-layouts  18.4 us (25%)
  Pallas kernels  8.79 us (12%)
  waiting for transfers between devices  7.81 us (11%)
  between operations  6.94 us (10%)
  other arithmetic  5.85 us (8%)
    ppermute x8, starting transfers between devices, window(): other = lax.ppermute(message, axis, [(i, i ^ bit) for i in range(size)])  20 us
    pallas_call x1, Pallas kernels, run_steps(): pl.pallas_call(steps_kernel, grid=(rows // block,), in_specs=[pl.BlockSpe...  8.79 us
    ppermute x8, waiting for transfers between devices, window(): other = lax.ppermute(message, axis, [(i, i ^ bit) for i in range(size)])  7.81 us
    gather x1, local copies, waits for them, and re-layouts, window(): migrated = table[source]  4.87 us
    ppermute x2, starting transfers between devices, shifted(): return lax.ppermute(block, axis, route)  4.56 us
    gather x2, local copies, waits for them, and re-layouts, window(): pair_out = jnp.concatenate([state[ancestors[pair_pick]], stamp])  2.89 us
    gather x2, local copies, waits for them, and re-layouts, window(): cycle_out = jnp.concatenate([state[ancestors[cycle_pick]], stamp])  2.34 us
    scatter x2, local copies, waits for them, and re-layouts, window(): source = ancestors.at[cycle_pick].set(rows_here + jnp.arange(n_cycle, dty...  2.09 us
  transfers between devices with their start and end apart: 10, of which 4 were waited for; matrix products, arithmetic and copies ran while one was open for 19% of the time, Pallas kernels for 0%

profile of v6, /device:TPU:1, one launch (start us, length us, event | category | flops | bytes accessed | tf_op | source)
XLA Modules:
  0.0 72.4 jit_solution(15770745592505207094)
XLA Ops:
  0.6 0.7 copy.19
  1.3 1.7 %copy.15.prior_ref = f32[1024,1]{1,0:T(8,128)} copy(f32[1024,1]{0,1:T(1,128)} %bitcast.54) | data formatting | bytes 8192 | tf_op jit(solution)/shard_map/reshape | solution.py:117
  3.0 0.0 copy-start.2
  3.0 0.0 copy-start.1
  3.0 8.8 %shard_map.139 = (f32[1024,512]{1,0:T(8,128)}, f32[8,128]{1,0:T(8,128)}) custom-call(f32[4]{0:T(128)} %current_ref.1, f32[1024,512]{1,0:T(8,128)} %state_ref.1, f32[1024,1]{1,0:T(8,128)} %copy.15.prior_ref, bf16[512,512]{1,0:T(8,128)(2,1)} %transition_ref.1, f32[1,512]{1,0:T(1,128)} %bitcast.60, f32[1,512]{1,0:T(1,128)} %bitcast.61, ...), custom_call_target="tpu_custom_call" | custom-call | flops 2684354560 | bytes 4718592 | tf_op jit(solution)/shard_map/pallas_call | solution.py:81
  11.8 0.0 copy-start
  11.8 2.1 %collective-permute-start.2 = (f32[8,128]{1,0:T(8,128)}, f32[8,128]{1,0:T(8,128)S(1)}, u32[]{:S(2)}, u32[]{:S(2)}) collective-permute-start(f32[8,128]{1,0:T(8,128)} %get-tuple-element.6), channel_id=1, source_target_pairs={{0,1},{1,0},{2,3},{3,2},{4,5},{5,4},{6,7},{7,6},{8,9},{9,8},{10,11... | collective-permute-start | bytes 12296 | tf_op jit(solution)/shard_map/ppermute | solution.py:165
  14.0 0.7 slice.99
  14.7 0.0 copy-done.2
  14.7 0.7 gather_fusion.2
  15.4 2.2 %gather_fusion.3 = f32[32,512]{1,0:T(8,128)S(1)} fusion(f32[1024,512]{1,0:T(8,128)} %get-tuple-element.5, s32[1024]{0:T(1024)S(1)} %pad_clamp_fusion), kind=kCustom, calls=%fused_computation.3 | custom fusion | bytes 131200 | tf_op jit(solution)/shard_map/gather | solution.py:157
  17.6 1.4 %collective-permute-start.1 = (f32[33,512]{1,0:T(8,128)S(1)}, f32[33,512]{1,0:T(8,128)S(1)}, u32[]{:S(2)}, u32[]{:S(2)}) collective-permute-start(f32[33,512]{1,0:T(8,128)S(1)} %pad_maximum_fusion.2), channel_id=1, source_target_pairs={{4,0},{5,1},{6,2},{7,3},{0,4},{1,5},{2,6},{3,7},{12,8},{13,9},{14,... | collective-permute-start | bytes 202760 | tf_op jit(solution)/shard_map/ppermute | solution.py:19
  19.0 0.1 pad.20.clone
  19.1 0.0 collective-permute-done.2
  19.1 0.7 exponential_bitcast_fusion.15
  19.8 0.7 multiply_add_fusion.7
  20.5 0.1 maximum_maximum_fusion
  20.6 2.5 %collective-permute-start.3 = (f32[8,128]{1,0:T(8,128)S(1)}, f32[8,128]{1,0:T(8,128)S(1)}, u32[]{:S(2)}, u32[]{:S(2)}) collective-permute-start(f32[8,128]{1,0:T(8,128)S(1)} %maximum_maximum_fusion), channel_id=1, source_target_pairs={{0,2},{1,3},{2,0},{3,1},{4,6},{5,7},{6,4},{7,5},{8,10},{9,11},{10,... | collective-permute-start | bytes 12296 | tf_op jit(solution)/shard_map/ppermute | solution.py:165
  23.0 0.0 copy-done.1
  23.0 1.5 %collective-permute-done.3 = f32[8,128]{1,0:T(8,128)S(1)} collective-permute-done((f32[8,128]{1,0:T(8,128)S(1)}, f32[8,128]{1,0:T(8,128)S(1)}, u32[]{:S(2)}, u32[]{:S(2)}) %collective-permute-start.3) | collective-permute-done | bytes 4128 | tf_op jit(solution)/shard_map/ppermute | solution.py:165
  24.6 0.1 maximum_maximum_fusion.1
  24.6 0.2 collective-permute-start.4
  24.9 1.4 %gather_fusion = s32[256]{0:T(256)S(1)} fusion(s32[1024]{0:T(1024)S(1)} %copy.19, s32[1024]{0:T(1024)S(1)} %pad_clamp_fusion.3), kind=kCustom, calls=%fused_computation | custom fusion | bytes 3072 | tf_op jit(solution)/shard_map/gather | solution.py:156
  26.2 0.9 %collective-permute-done.4 = f32[8,128]{1,0:T(8,128)S(1)} collective-permute-done((f32[8,128]{1,0:T(8,128)S(1)}, f32[8,128]{1,0:T(8,128)S(1)}, u32[]{:S(2)}, u32[]{:S(2)}) %collective-permute-start.4) | collective-permute-done | bytes 4128 | tf_op jit(solution)/shard_map/ppermute | solution.py:165
  27.2 0.1 maximum_maximum_fusion.2
  27.2 3.6 %collective-permute-start.5 = (f32[8,128]{1,0:T(8,128)S(1)}, f32[8,128]{1,0:T(8,128)S(1)}, u32[]{:S(2)}, u32[]{:S(2)}) collective-permute-start(f32[8,128]{1,0:T(8,128)S(1)} %maximum_maximum_fusion.2), channel_id=1, source_target_pairs={{0,8},{8,0},{16,24},{24,16},{32,40},{40,32},{48,56},{56,48},{64,72... | collective-permute-start | bytes 12296 | tf_op jit(solution)/shard_map/ppermute | solution.py:165
  30.8 0.8 %collective-permute-done.5 = f32[8,128]{1,0:T(8,128)S(1)} collective-permute-done((f32[8,128]{1,0:T(8,128)S(1)}, f32[8,128]{1,0:T(8,128)S(1)}, u32[]{:S(2)}, u32[]{:S(2)}) %collective-permute-start.5) | collective-permute-done | bytes 4128 | tf_op jit(solution)/shard_map/ppermute | solution.py:165
  31.7 0.1 maximum_maximum_fusion.3
  31.7 1.7 %collective-permute-start.6 = (f32[8,128]{1,0:T(8,128)S(1)}, f32[8,128]{1,0:T(8,128)S(1)}, u32[]{:S(2)}, u32[]{:S(2)}) collective-permute-start(f32[8,128]{1,0:T(8,128)S(1)} %maximum_maximum_fusion.3), channel_id=1, source_target_pairs={{0,16},{8,24},{16,0},{24,8},{32,48},{40,56},{48,32},{56,40},{64,80... | collective-permute-start | bytes 12296 | tf_op jit(solution)/shard_map/ppermute | solution.py:165
  33.4 0.0 copy-done
  33.4 1.0 %gather_fusion.1 = f32[256,512]{1,0:T(8,128)S(1)} fusion(f32[1024,512]{1,0:T(8,128)S(1)} %copy-done, s32[1024]{0:T(1024)S(1)} %pad_clamp_fusion.2), kind=kCustom, calls=%fused_computation.1 | custom fusion | bytes 1049600 | tf_op jit(solution)/shard_map/gather | solution.py:156
  34.4 0.0 collective-permute-done.6
  34.4 0.1 maximum_maximum_fusion.4
  34.5 3.0 %collective-permute-start.7 = (f32[8,128]{1,0:T(8,128)S(1)}, f32[8,128]{1,0:T(8,128)S(1)}, u32[]{:S(2)}, u32[]{:S(2)}) collective-permute-start(f32[8,128]{1,0:T(8,128)S(1)} %maximum_maximum_fusion.4), channel_id=1, source_target_pairs={{0,32},{8,40},{16,48},{24,56},{32,0},{40,8},{48,16},{56,24},{64,96... | collective-permute-start | bytes 12296 | tf_op jit(solution)/shard_map/ppermute | solution.py:165
  37.6 3.2 %collective-permute-start = (f32[257,512]{1,0:T(8,128)S(1)}, f32[257,512]{1,0:T(8,128)S(1)}, u32[]{:S(2)}, u32[]{:S(2)}) collective-permute-start(f32[257,512]{1,0:T(8,128)S(1)} %pad_maximum_fusion.1), channel_id=1, source_target_pairs={{248,0},{0,8},{8,16},{16,24},{24,32},{32,40},{40,48},{48,56},{56,6... | collective-permute-start | bytes 1579016 | tf_op jit(solution)/shard_map/ppermute | solution.py:19
  40.8 1.4 %scatter_fusion = s32[1024]{0:T(1024)S(1)} fusion(s32[1024]{0:T(1024)S(1)} %copy.19, s32[256]{0:T(256)S(1)} %get-tuple-element.29, s32[256]{0:T(256)S(1)} %get-tuple-element.30), kind=kCustom, calls=%fused_computation.5 | custom fusion | bytes 4096 | tf_op jit(solution)/shard_map/scatter | solution.py:185
  42.2 0.7 scatter_fusion.1
  42.9 0.0 collective-permute-done.7
  42.9 0.1 maximum_maximum_fusion.5
  43.0 4.2 %collective-permute-start.8 = (f32[8,128]{1,0:T(8,128)S(1)}, f32[8,128]{1,0:T(8,128)S(1)}, u32[]{:S(2)}, u32[]{:S(2)}) collective-permute-start(f32[8,128]{1,0:T(8,128)S(1)} %maximum_maximum_fusion.5), channel_id=1, source_target_pairs={{0,64},{8,72},{16,80},{24,88},{32,96},{40,104},{48,112},{56,120},{... | collective-permute-start | bytes 12296 | tf_op jit(solution)/shard_map/ppermute | solution.py:165
  47.2 4.6 %collective-permute-done.8 = f32[8,128]{1,0:T(8,128)S(1)} collective-permute-done((f32[8,128]{1,0:T(8,128)S(1)}, f32[8,128]{1,0:T(8,128)S(1)}, u32[]{:S(2)}, u32[]{:S(2)}) %collective-permute-start.8) | collective-permute-done | bytes 4128 | tf_op jit(solution)/shard_map/ppermute | solution.py:165
  51.8 0.1 maximum_maximum_fusion.6
  51.9 2.7 %collective-permute-start.9 = (f32[8,128]{1,0:T(8,128)S(1)}, f32[8,128]{1,0:T(8,128)S(1)}, u32[]{:S(2)}, u32[]{:S(2)}) collective-permute-start(f32[8,128]{1,0:T(8,128)S(1)} %maximum_maximum_fusion.6), channel_id=1, source_target_pairs={{0,128},{8,136},{16,144},{24,152},{32,160},{40,168},{48,176},{56,1... | collective-permute-start | bytes 12296 | tf_op jit(solution)/shard_map/ppermute | solution.py:165
  54.6 1.4 %fusion.4 = (f32[1,1]{1,0:T(1,128)}, f32[1,1]{1,0:T(1,128)}) fusion(f32[8,128]{1,0:T(8,128)} %get-tuple-element.6), kind=kLoop, calls=%fused_computation.66 | loop fusion | bytes 16 | tf_op jit(solution)/shard_map/slice | solution.py:153
  55.9 0.0 collective-permute-done.9
  56.0 0.6 slice.123
  56.5 1.2 %divide_bitcast_fusion = f32[512]{0:T(512)} fusion(f32[5,128]{1,0:T(8,128)S(1)} %multiply_add_fusion, f32[]{:T(128)} %bitcast.26), kind=kLoop, calls=%fused_computation.36 | loop fusion | flops 512 | bytes 4100 | tf_op jit(solution)/shard_map/div | solution.py:174
  59.8 0.0 collective-permute-done.1
  59.8 0.5 fusion.3
  62.4 0.0 collective-permute-done
  62.4 0.5 fusion.2
  65.0 1.9 %pad_maximum_fusion = f32[1312,512]{1,0:T(8,128)S(1)} fusion(f32[32,512]{1,0:T(8,128)S(1)} %slice.140, f32[256,512]{1,0:T(8,128)S(1)} %slice.139, f32[1024,512]{1,0:T(8,128)} %get-tuple-element.5), kind=kLoop, calls=%fused_computation.7 | loop fusion | flops 1343488 | bytes 5373952 | tf_op jit(solution)/shard_map/concatenate | solution.py:189
  66.9 4.9 %gather_fusion.4 = f32[1024,512]{1,0:T(8,128)} fusion(f32[1312,512]{1,0:T(8,128)S(1)} %pad_maximum_fusion, s32[1024]{0:T(1024)S(1)} %fusion), kind=kCustom, calls=%fused_computation.4 | custom fusion | bytes 4198400 | tf_op jit(solution)/shard_map/gather | solution.py:190
  71.8 0.6 select_select_fusion
  (36 shorter events, 0.3 us)
Async XLA Ops:
  3.0 11.6 %copy-start.2 = (s32[32]{0:T(128)S(1)}, s32[32]{0:T(128)}, u32[]{:S(2)}) copy-start(s32[32]{0:T(128)} %param.23) | copy-start | bytes 388
  3.0 20.0 %copy-start.1 = (s32[256]{0:T(256)S(1)}, s32[256]{0:T(256)}, u32[]{:S(2)}) copy-start(s32[256]{0:T(256)} %param.22) | copy-start | bytes 3076
  11.8 21.6 %copy-start = (f32[1024,512]{1,0:T(8,128)S(1)}, f32[1024,512]{1,0:T(8,128)}, u32[]{:S(2)}) copy-start(f32[1024,512]{1,0:T(8,128)} %get-tuple-element.5) | copy-start | bytes 6291460
  11.8 7.3 %collective-permute-start.2 = (f32[8,128]{1,0:T(8,128)}, f32[8,128]{1,0:T(8,128)S(1)}, u32[]{:S(2)}, u32[]{:S(2)}) collective-permute-start(f32[8,128]{1,0:T(8,128)} %get-tuple-element.6), channel_id=1, source_target_pairs={{0,1},{1,0},{2,3},{3,2},{4,5},{5,4},{6,7},{7,6},{8,9},{9,8},{10,11... | collective-permute-start | bytes 12296 | tf_op jit(solution)/shard_map/ppermute | solution.py:165
  17.6 42.2 %collective-permute-start.1 = (f32[33,512]{1,0:T(8,128)S(1)}, f32[33,512]{1,0:T(8,128)S(1)}, u32[]{:S(2)}, u32[]{:S(2)}) collective-permute-start(f32[33,512]{1,0:T(8,128)S(1)} %pad_maximum_fusion.2), channel_id=1, source_target_pairs={{4,0},{5,1},{6,2},{7,3},{0,4},{1,5},{2,6},{3,7},{12,8},{13,9},{14,... | collective-permute-start | bytes 202760 | tf_op jit(solution)/shard_map/ppermute | solution.py:19
  20.6 4.0 %collective-permute-start.3 = (f32[8,128]{1,0:T(8,128)S(1)}, f32[8,128]{1,0:T(8,128)S(1)}, u32[]{:S(2)}, u32[]{:S(2)}) collective-permute-start(f32[8,128]{1,0:T(8,128)S(1)} %maximum_maximum_fusion), channel_id=1, source_target_pairs={{0,2},{1,3},{2,0},{3,1},{4,6},{5,7},{6,4},{7,5},{8,10},{9,11},{10,... | collective-permute-start | bytes 12296 | tf_op jit(solution)/shard_map/ppermute | solution.py:165
  24.6 2.5 %collective-permute-start.4 = (f32[8,128]{1,0:T(8,128)S(1)}, f32[8,128]{1,0:T(8,128)S(1)}, u32[]{:S(2)}, u32[]{:S(2)}) collective-permute-start(f32[8,128]{1,0:T(8,128)S(1)} %maximum_maximum_fusion.1), channel_id=1, source_target_pairs={{0,4},{1,5},{2,6},{3,7},{4,0},{5,1},{6,2},{7,3},{8,12},{9,13},{10,... | collective-permute-start | bytes 12296 | tf_op jit(solution)/shard_map/ppermute | solution.py:165
  27.2 4.4 %collective-permute-start.5 = (f32[8,128]{1,0:T(8,128)S(1)}, f32[8,128]{1,0:T(8,128)S(1)}, u32[]{:S(2)}, u32[]{:S(2)}) collective-permute-start(f32[8,128]{1,0:T(8,128)S(1)} %maximum_maximum_fusion.2), channel_id=1, source_target_pairs={{0,8},{8,0},{16,24},{24,16},{32,40},{40,32},{48,56},{56,48},{64,72... | collective-permute-start | bytes 12296 | tf_op jit(solution)/shard_map/ppermute | solution.py:165
  31.7 2.7 %collective-permute-start.6 = (f32[8,128]{1,0:T(8,128)S(1)}, f32[8,128]{1,0:T(8,128)S(1)}, u32[]{:S(2)}, u32[]{:S(2)}) collective-permute-start(f32[8,128]{1,0:T(8,128)S(1)} %maximum_maximum_fusion.3), channel_id=1, source_target_pairs={{0,16},{8,24},{16,0},{24,8},{32,48},{40,56},{48,32},{56,40},{64,80... | collective-permute-start | bytes 12296 | tf_op jit(solution)/shard_map/ppermute | solution.py:165
  34.5 8.4 %collective-permute-start.7 = (f32[8,128]{1,0:T(8,128)S(1)}, f32[8,128]{1,0:T(8,128)S(1)}, u32[]{:S(2)}, u32[]{:S(2)}) collective-permute-start(f32[8,128]{1,0:T(8,128)S(1)} %maximum_maximum_fusion.4), channel_id=1, source_target_pairs={{0,32},{8,40},{16,48},{24,56},{32,0},{40,8},{48,16},{56,24},{64,96... | collective-permute-start | bytes 12296 | tf_op jit(solution)/shard_map/ppermute | solution.py:165
  37.6 24.8 %collective-permute-start = (f32[257,512]{1,0:T(8,128)S(1)}, f32[257,512]{1,0:T(8,128)S(1)}, u32[]{:S(2)}, u32[]{:S(2)}) collective-permute-start(f32[257,512]{1,0:T(8,128)S(1)} %pad_maximum_fusion.1), channel_id=1, source_target_pairs={{248,0},{0,8},{8,16},{16,24},{24,32},{32,40},{40,48},{48,56},{56,6... | collective-permute-start | bytes 1579016 | tf_op jit(solution)/shard_map/ppermute | solution.py:19
  43.0 8.8 %collective-permute-start.8 = (f32[8,128]{1,0:T(8,128)S(1)}, f32[8,128]{1,0:T(8,128)S(1)}, u32[]{:S(2)}, u32[]{:S(2)}) collective-permute-start(f32[8,128]{1,0:T(8,128)S(1)} %maximum_maximum_fusion.5), channel_id=1, source_target_pairs={{0,64},{8,72},{16,80},{24,88},{32,96},{40,104},{48,112},{56,120},{... | collective-permute-start | bytes 12296 | tf_op jit(solution)/shard_map/ppermute | solution.py:165
  51.9 4.0 %collective-permute-start.9 = (f32[8,128]{1,0:T(8,128)S(1)}, f32[8,128]{1,0:T(8,128)S(1)}, u32[]{:S(2)}, u32[]{:S(2)}) collective-permute-start(f32[8,128]{1,0:T(8,128)S(1)} %maximum_maximum_fusion.6), channel_id=1, source_target_pairs={{0,128},{8,136},{16,144},{24,152},{32,160},{40,168},{48,176},{56,1... | collective-permute-start | bytes 12296 | tf_op jit(solution)/shard_map/ppermute | solution.py:165

commit v7 on v6

--- a/solution.py
+++ b/solution.py
@@ -124,6 +124,80 @@
     )
 
 
+def pick_rows_kernel(ancestors_ref, pick_ref, state_hbm, stamp_ref, rows_out, sem):
+    count = pick_ref.shape[0]
+
+    def issue(i, carry):
+        row = ancestors_ref[pick_ref[i]]
+        pltpu.make_async_copy(state_hbm.at[pl.ds(row, 1)], rows_out.at[pl.ds(i, 1)], sem.at[0]).start()
+        return carry
+
+    lax.fori_loop(0, count, issue, 0)
+    pltpu.make_async_copy(state_hbm.at[pl.ds(0, count)], rows_out.at[pl.ds(0, count)], sem.at[0]).wait()
+    rows_out[count : count + 1, :] = stamp_ref[...]
+
+
+def pick_rows(state, ancestors, pick, stamp):
+    _, width = state.shape
+    count = pick.shape[0]
+    return pl.pallas_call(
+        pick_rows_kernel,
+        in_specs=[
+            pl.BlockSpec(memory_space=pltpu.SMEM),
+            pl.BlockSpec(memory_space=pltpu.SMEM),
+            pl.BlockSpec(memory_space=pl.ANY),
+            pl.BlockSpec(memory_space=pltpu.VMEM),
+        ],
+        out_specs=pl.BlockSpec(memory_space=pltpu.VMEM),
+        out_shape=jax.ShapeDtypeStruct((count + 1, width), jnp.float32),
+        scratch_shapes=[pltpu.SemaphoreType.DMA((1,))],
+        cost_estimate=pl.CostEstimate(flops=0, transcendentals=0, bytes_accessed=2 * count * width * 4),
+    )(ancestors, pick, state, stamp)
+
+
+def assemble_kernel(
+    ancestors_ref, cycle_pick_ref, pair_pick_ref, state_hbm, cycle_hbm, pair_hbm, migrated_out, sem
+):
+    rows = ancestors_ref.shape[0]
+    n_cycle = cycle_pick_ref.shape[0]
+    n_pairs = pair_pick_ref.shape[0]
+
+    def resample(i, carry):
+        row = ancestors_ref[i]
+        pltpu.make_async_copy(state_hbm.at[pl.ds(row, 1)], migrated_out.at[pl.ds(i, 1)], sem.at[0]).start()
+        return carry
+
+    lax.fori_loop(0, rows, resample, 0)
+    pltpu.make_async_copy(state_hbm, migrated_out, sem.at[0]).wait()
+
+    def arrive_cycle(j, carry):
+        row = cycle_pick_ref[j]
+        pltpu.make_async_copy(cycle_hbm.at[pl.ds(j, 1)], migrated_out.at[pl.ds(row, 1)], sem.at[1]).start()
+        return carry
+
+    def arrive_pair(j, carry):
+        row = pair_pick_ref[j]
+        pltpu.make_async_copy(pair_hbm.at[pl.ds(j, 1)], migrated_out.at[pl.ds(row, 1)], sem.at[1]).start()
+        return carry
+
+    lax.fori_loop(0, n_cycle, arrive_cycle, 0)
+    lax.fori_loop(0, n_pairs, arrive_pair, 0)
+    pltpu.make_async_copy(cycle_hbm.at[pl.ds(0, n_cycle)], migrated_out.at[pl.ds(0, n_cycle)], sem.at[1]).wait()
+    pltpu.make_async_copy(pair_hbm.at[pl.ds(0, n_pairs)], migrated_out.at[pl.ds(0, n_pairs)], sem.at[1]).wait()
+
+
+def assemble(state, ancestors, cycle_pick, pair_pick, cycle_in, pair_in):
+    rows, width = state.shape
+    return pl.pallas_call(
+        assemble_kernel,
+        in_specs=[pl.BlockSpec(memory_space=pltpu.SMEM)] * 3 + [pl.BlockSpec(memory_space=pl.ANY)] * 3,
+        out_specs=pl.BlockSpec(memory_space=pltpu.VMEM),
+        out_shape=jax.ShapeDtypeStruct((rows, width), jnp.float32),
+        scratch_shapes=[pltpu.SemaphoreType.DMA((2,))],
+        cost_estimate=pl.CostEstimate(flops=0, transcendentals=0, bytes_accessed=4 * rows * width * 4),
+    )(ancestors, cycle_pick, pair_pick, state, cycle_in, pair_in)
+
+
 def window(
     particles,
     log_prior,
@@ -149,12 +223,10 @@
     n_pairs = pair_pick.shape[0]
     lanes = message.shape[1]
     k = width // lanes
-    local_sum = message[k, 0]
-    local_peak = message[k + 1, 0]
     stamp = message[k : 2 * k].reshape(1, width)
 
-    cycle_out = jnp.concatenate([state[ancestors[cycle_pick]], stamp])
-    pair_out = jnp.concatenate([state[ancestors[pair_pick]], stamp])
+    cycle_out = pick_rows(state, ancestors, cycle_pick, stamp)
+    pair_out = pick_rows(state, ancestors, pair_pick, stamp)
     cycle_in = shifted(cycle_out, BLK, 1)
     pair_in = shifted(pair_out, PAIR, n_pair // 2)
 
@@ -169,30 +241,32 @@
             body = message[: k + 1] * mine_scale + other[: k + 1] * other_scale
             message = jnp.concatenate([body, peak_row[None], jnp.zeros((pad, lanes), jnp.float32)])
             bit *= 2
-    total = message[k, 0]
-    peak = message[k + 1, 0]
-    mean_state = message[:k].reshape(width) / total
-
-    def group_weight(device_peak, device_sum):
+    total = message[k : k + 1]
+    peak = message[k + 1 : k + 2]
+    mean_state = (message[:k] / total).reshape(width)
+
+    def group_weight(row):
+        device_sum = row[:, :lanes]
+        device_peak = row[:, lanes : 2 * lanes]
         return jnp.log(jnp.maximum(groups * (device_sum * jnp.exp(device_peak - peak)) / total, 0.1))
 
-    own_w = group_weight(local_peak, local_sum)
-    cycle_w = group_weight(cycle_in[n_cycle, lanes], cycle_in[n_cycle, 0])
-    pair_w = group_weight(pair_in[n_pairs, lanes], pair_in[n_pairs, 0])
-
+    own_w = group_weight(stamp)
+    cycle_w = group_weight(cycle_in[n_cycle : n_cycle + 1])
+    pair_w = group_weight(pair_in[n_pairs : n_pairs + 1])
+
+    migrated = assemble(state, ancestors, cycle_pick, pair_pick, cycle_in, pair_in)
     source = (
         ancestors.at[cycle_pick]
         .set(rows_here + jnp.arange(n_cycle, dtype=jnp.int32))
         .at[pair_pick]
         .set(rows_here + n_cycle + jnp.arange(n_pairs, dtype=jnp.int32))
     )
-    table = jnp.concatenate([state, cycle_in[:n_cycle], pair_in[:n_pairs]], axis=0)
-    migrated = table[source]
+    tiles = source.reshape(rows_here // lanes, lanes)
     group_logw = jnp.where(
-        source >= rows_here + n_cycle,
+        tiles >= rows_here + n_cycle,
         pair_w,
-        jnp.where(source >= rows_here, cycle_w, own_w),
-    )
+        jnp.where(tiles >= rows_here, cycle_w, own_w),
+    ).reshape(rows_here)
     return (migrated, group_logw, mean_state)
 
 
@@ -215,6 +289,4 @@
         P(BLK_PAIR),
     )
     out_specs = (P(BLK_PAIR, None), P(BLK_PAIR), P())
-    return jax.shard_map(
-        window, mesh=torus, in_specs=in_specs, out_specs=out_specs, check_vma=False
-    )
+    return jax.shard_map(window, mesh=torus, in_specs=in_specs, out_specs=out_specs, check_vma=False)

time: 72.8 us -> 78.6 us (1.080)
  Pallas kernels: 8.79 us -> 30.3 us
  local copies, waits for them, and re-layouts: 18.4 us -> 6.54 us
  between operations: 6.94 us -> 0.81 us
  starting transfers between devices: 24.5 us -> 27.3 us
  other arithmetic: 5.85 us -> 3.33 us
  waiting for transfers between devices: 7.81 us -> 9.93 us
    pallas_call x0 -> x3, Pallas kernels: none -> 21.5 us  [the longest x1 14.3 us: assemble(): pl.pallas_call(assemble_kernel, in_specs=[pl.BlockSpec(memory_space=pltpu...]
    gather x5 -> x0, local copies, waits for them, and re-layouts: 10.1 us -> none  [the longest x1 4.87 us: window(): migrated = table[source]]
    ppermute x8, starting transfers between devices: 20 us -> 25.1 us  [window(): other = lax.ppermute(message, axis, [(i, i ^ bit) for i in range(size)])]
    slice x6 -> x0, local copies, waits for them, and re-layouts: 3.04 us -> none  [the longest x1 1.36 us: window(): local_peak = message[k + 1, 0]]
    ppermute x2, starting transfers between devices: 4.56 us -> 2.14 us  [shifted(): return lax.ppermute(block, axis, route)]
    ppermute x8, waiting for transfers between devices: 7.81 us -> 9.92 us  [window(): other = lax.ppermute(message, axis, [(i, i ^ bit) for i in range(size)])]
    concatenate x3 -> x0, other arithmetic: 1.95 us -> none  [the longest x1 1.9 us: window(): jnp.concatenate([state, cycle_in[:n_cycle], pair_in[:n_pairs]], axis=0)]
    div x1 -> x0, other arithmetic: 1.21 us -> none  [window(): mean_state = message[:k].reshape(width) / total]
  transfers between devices with their start and end apart: 10 -> 10, of which waited for: 4 -> 7; matrix products, arithmetic and copies ran while one was open for 19% -> 2% of each run, Pallas kernels for 0% -> 9%
where the time goes in v7:
time: 78.6 us; the launch traced here: 78.1 us
  Pallas kernels  30.3 us (39%)
  starting transfers between devices  27.3 us (35%)
  waiting for transfers between devices  9.93 us (13%)
  local copies, waits for them, and re-layouts  6.54 us (8%)
  other arithmetic  3.33 us (4%)
  between operations  0.81 us (1%)
    ppermute x8, starting transfers between devices, window(): other = lax.ppermute(message, axis, [(i, i ^ bit) for i in range(size)])  25.1 us
    pallas_call x1, Pallas kernels, assemble(): pl.pallas_call(assemble_kernel, in_specs=[pl.BlockSpec(memory_space=pltpu...  14.3 us
    ppermute x8, waiting for transfers between devices, window(): other = lax.ppermute(message, axis, [(i, i ^ bit) for i in range(size)])  9.92 us
    pallas_call x1, Pallas kernels, run_steps(): pl.pallas_call(steps_kernel, grid=(rows // block,), in_specs=[pl.BlockSpe...  8.78 us
    pallas_call x2, Pallas kernels, pick_rows(): pl.pallas_call(pick_rows_kernel, in_specs=[pl.BlockSpec(memory_space=pltp...  7.15 us
    ppermute x2, starting transfers between devices, shifted(): return lax.ppermute(block, axis, route)  2.14 us
    scatter x2, local copies, waits for them, and re-layouts, window(): source = ancestors.at[cycle_pick].set(rows_here + jnp.arange(n_cycle, dty...  2.09 us
    reshape x1, local copies, waits for them, and re-layouts, run_steps(): log_prior.reshape(rows, 1)  1.71 us
  transfers between devices with their start and end apart: 10, of which 7 were waited for; matrix products, arithmetic and copies ran while one was open for 2% of the time, Pallas kernels for 9%

profile of v7, /device:TPU:1, one launch (start us, length us, event | category | flops | bytes accessed | tf_op | source)
XLA Modules:
  0.0 78.1 jit_solution(9208948321505466359)
XLA Ops:
  0.6 1.3 %copy.19.ancestors_ref = s32[1024]{0:T(1024)} copy(s32[1024]{0:T(1024)} %param.21) | data formatting | bytes 8192
  1.9 1.7 %copy.15.prior_ref = f32[1024,1]{1,0:T(8,128)} copy(f32[1024,1]{0,1:T(1,128)} %bitcast.58) | data formatting | bytes 8192 | tf_op jit(solution)/shard_map/reshape | solution.py:117
  3.6 8.8 %shard_map.139 = (f32[1024,512]{1,0:T(8,128)}, f32[8,128]{1,0:T(8,128)}) custom-call(f32[4]{0:T(128)} %current_ref.1, f32[1024,512]{1,0:T(8,128)} %state_ref.1, f32[1024,1]{1,0:T(8,128)} %copy.15.prior_ref, bf16[512,512]{1,0:T(8,128)(2,1)} %transition_ref.1, f32[1,512]{1,0:T(1,128)} %bitcast.59, f32[1,512]{1,0:T(1,128)} %bitcast.60, ...), custom_call_target="tpu_custom_call" | custom-call | flops 2684354560 | bytes 4718592 | tf_op jit(solution)/shard_map/pallas_call | solution.py:81
  12.4 2.1 %collective-permute-start.2 = (f32[8,128]{1,0:T(8,128)}, f32[8,128]{1,0:T(8,128)S(1)}, u32[]{:S(2)}, u32[]{:S(2)}) collective-permute-start(f32[8,128]{1,0:T(8,128)} %get-tuple-element.6), channel_id=1, source_target_pairs={{0,1},{1,0},{2,3},{3,2},{4,5},{5,4},{6,7},{7,6},{8,9},{9,8},{10,11... | collective-permute-start | bytes 12296 | tf_op jit(solution)/shard_map/ppermute | solution.py:237
  14.5 0.1 pad.20.clone
  14.6 1.1 %collective-permute-done.2 = f32[8,128]{1,0:T(8,128)S(1)} collective-permute-done((f32[8,128]{1,0:T(8,128)}, f32[8,128]{1,0:T(8,128)S(1)}, u32[]{:S(2)}, u32[]{:S(2)}) %collective-permute-start.2) | collective-permute-done | bytes 4128 | tf_op jit(solution)/shard_map/ppermute | solution.py:237
  15.7 0.7 exponential_bitcast_fusion.15
  16.4 0.7 multiply_add_fusion.7
  17.1 0.1 maximum_maximum_fusion
  17.2 3.0 %collective-permute-start.3 = (f32[8,128]{1,0:T(8,128)S(1)}, f32[8,128]{1,0:T(8,128)S(1)}, u32[]{:S(2)}, u32[]{:S(2)}) collective-permute-start(f32[8,128]{1,0:T(8,128)S(1)} %maximum_maximum_fusion), channel_id=1, source_target_pairs={{0,2},{1,3},{2,0},{3,1},{4,6},{5,7},{6,4},{7,5},{8,10},{9,11},{10,... | collective-permute-start | bytes 12296 | tf_op jit(solution)/shard_map/ppermute | solution.py:237
  20.2 1.0 %collective-permute-done.3 = f32[8,128]{1,0:T(8,128)S(1)} collective-permute-done((f32[8,128]{1,0:T(8,128)S(1)}, f32[8,128]{1,0:T(8,128)S(1)}, u32[]{:S(2)}, u32[]{:S(2)}) %collective-permute-start.3) | collective-permute-done | bytes 4128 | tf_op jit(solution)/shard_map/ppermute | solution.py:237
  21.2 0.1 maximum_maximum_fusion.1
  21.3 1.5 %collective-permute-start.4 = (f32[8,128]{1,0:T(8,128)S(1)}, f32[8,128]{1,0:T(8,128)S(1)}, u32[]{:S(2)}, u32[]{:S(2)}) collective-permute-start(f32[8,128]{1,0:T(8,128)S(1)} %maximum_maximum_fusion.1), channel_id=1, source_target_pairs={{0,4},{1,5},{2,6},{3,7},{4,0},{5,1},{6,2},{7,3},{8,12},{9,13},{10,... | collective-permute-start | bytes 12296 | tf_op jit(solution)/shard_map/ppermute | solution.py:237
  22.8 1.0 %collective-permute-done.4 = f32[8,128]{1,0:T(8,128)S(1)} collective-permute-done((f32[8,128]{1,0:T(8,128)S(1)}, f32[8,128]{1,0:T(8,128)S(1)}, u32[]{:S(2)}, u32[]{:S(2)}) %collective-permute-start.4) | collective-permute-done | bytes 4128 | tf_op jit(solution)/shard_map/ppermute | solution.py:237
  23.9 0.1 maximum_maximum_fusion.2
  23.9 6.0 %collective-permute-start.5 = (f32[8,128]{1,0:T(8,128)S(1)}, f32[8,128]{1,0:T(8,128)S(1)}, u32[]{:S(2)}, u32[]{:S(2)}) collective-permute-start(f32[8,128]{1,0:T(8,128)S(1)} %maximum_maximum_fusion.2), channel_id=1, source_target_pairs={{0,8},{8,0},{16,24},{24,16},{32,40},{40,32},{48,56},{56,48},{64,72... | collective-permute-start | bytes 12296 | tf_op jit(solution)/shard_map/ppermute | solution.py:237
  29.9 0.8 %collective-permute-done.5 = f32[8,128]{1,0:T(8,128)S(1)} collective-permute-done((f32[8,128]{1,0:T(8,128)S(1)}, f32[8,128]{1,0:T(8,128)S(1)}, u32[]{:S(2)}, u32[]{:S(2)}) %collective-permute-start.5) | collective-permute-done | bytes 4128 | tf_op jit(solution)/shard_map/ppermute | solution.py:237
  30.8 0.1 maximum_maximum_fusion.3
  30.9 0.0 collective-permute-start.6
  30.9 1.3 %slice.96 = f32[4,128]{1,0:T(4,128)} slice(f32[8,128]{1,0:T(8,128)} %get-tuple-element.6), slice={[4:8], [0:128]} | slice | bytes 4096 | tf_op jit(solution)/shard_map/slice | solution.py:226
  32.2 0.0 copy-start.4
  32.2 0.0 copy-start.5
  32.2 0.0 copy-start.3
  32.2 2.5 %shard_map.141 = f32[33,512]{1,0:T(8,128)} custom-call(s32[1024]{0:T(1024)} %copy.19.ancestors_ref, s32[32]{0:T(128)} %pair_pick_ref.1, f32[1024,512]{1,0:T(8,128)} %get-tuple-element.5.state_hbm, f32[1,512]{1,0:T(1,128)} %bitcast.55), custom_call_target="tpu_custom_call" | custom-call | bytes 131072 | tf_op jit(solution)/shard_map/pallas_call | solution.py:143
  34.7 1.3 %collective-permute-start.1 = (f32[33,512]{1,0:T(8,128)}, f32[33,512]{1,0:T(8,128)S(1)}, u32[]{:S(2)}, u32[]{:S(2)}) collective-permute-start(f32[33,512]{1,0:T(8,128)} %shard_map.141), channel_id=1, source_target_pairs={{4,0},{5,1},{6,2},{7,3},{0,4},{1,5},{2,6},{3,7},{12,8},{13,9},{14,... | collective-permute-start | bytes 202760 | tf_op jit(solution)/shard_map/ppermute | solution.py:19
  36.0 4.7 %shard_map.140 = f32[257,512]{1,0:T(8,128)} custom-call(s32[1024]{0:T(1024)} %copy.19.ancestors_ref, s32[256]{0:T(256)} %cycle_pick_ref.1, f32[1024,512]{1,0:T(8,128)} %get-tuple-element.5.state_hbm, f32[1,512]{1,0:T(1,128)} %bitcast.56), custom_call_target="tpu_custom_call" | custom-call | bytes 1048576 | tf_op jit(solution)/shard_map/pallas_call | solution.py:143
  40.7 0.8 %collective-permute-start = (f32[257,512]{1,0:T(8,128)}, f32[257,512]{1,0:T(8,128)S(1)}, u32[]{:S(2)}, u32[]{:S(2)}) collective-permute-start(f32[257,512]{1,0:T(8,128)} %shard_map.140), channel_id=1, source_target_pairs={{248,0},{0,8},{8,16},{16,24},{24,32},{32,40},{40,48},{48,56},{56,6... | collective-permute-start | bytes 1579016 | tf_op jit(solution)/shard_map/ppermute | solution.py:19
  41.5 0.0 collective-permute-done.6
  41.5 0.1 maximum_maximum_fusion.4
  41.6 2.9 %collective-permute-start.7 = (f32[8,128]{1,0:T(8,128)S(1)}, f32[8,128]{1,0:T(8,128)S(1)}, u32[]{:S(2)}, u32[]{:S(2)}) collective-permute-start(f32[8,128]{1,0:T(8,128)S(1)} %maximum_maximum_fusion.4), channel_id=1, source_target_pairs={{0,32},{8,40},{16,48},{24,56},{32,0},{40,8},{48,16},{56,24},{64,96... | collective-permute-start | bytes 12296 | tf_op jit(solution)/shard_map/ppermute | solution.py:237
  44.5 0.0 copy-done.4
  44.5 3.7 %collective-permute-done.7 = f32[8,128]{1,0:T(8,128)S(1)} collective-permute-done((f32[8,128]{1,0:T(8,128)S(1)}, f32[8,128]{1,0:T(8,128)S(1)}, u32[]{:S(2)}, u32[]{:S(2)}) %collective-permute-start.7) | collective-permute-done | bytes 4128 | tf_op jit(solution)/shard_map/ppermute | solution.py:237
  48.2 0.1 maximum_maximum_fusion.5
  48.3 6.8 %collective-permute-start.8 = (f32[8,128]{1,0:T(8,128)S(1)}, f32[8,128]{1,0:T(8,128)S(1)}, u32[]{:S(2)}, u32[]{:S(2)}) collective-permute-start(f32[8,128]{1,0:T(8,128)S(1)} %maximum_maximum_fusion.5), channel_id=1, source_target_pairs={{0,64},{8,72},{16,80},{24,88},{32,96},{40,104},{48,112},{56,120},{... | collective-permute-start | bytes 12296 | tf_op jit(solution)/shard_map/ppermute | solution.py:237
  55.1 0.0 copy-done.5
  55.1 1.0 %collective-permute-done.8 = f32[8,128]{1,0:T(8,128)S(1)} collective-permute-done((f32[8,128]{1,0:T(8,128)S(1)}, f32[8,128]{1,0:T(8,128)S(1)}, u32[]{:S(2)}, u32[]{:S(2)}) %collective-permute-start.8) | collective-permute-done | bytes 4128 | tf_op jit(solution)/shard_map/ppermute | solution.py:237
  56.1 0.1 maximum_maximum_fusion.6
  56.2 2.7 %collective-permute-start.9 = (f32[8,128]{1,0:T(8,128)S(1)}, f32[8,128]{1,0:T(8,128)S(1)}, u32[]{:S(2)}, u32[]{:S(2)}) collective-permute-start(f32[8,128]{1,0:T(8,128)S(1)} %maximum_maximum_fusion.6), channel_id=1, source_target_pairs={{0,128},{8,136},{16,144},{24,152},{32,160},{40,168},{48,176},{56,1... | collective-permute-start | bytes 12296 | tf_op jit(solution)/shard_map/ppermute | solution.py:237
  58.9 1.3 %collective-permute-done.9 = f32[8,128]{1,0:T(8,128)S(1)} collective-permute-done((f32[8,128]{1,0:T(8,128)S(1)}, f32[8,128]{1,0:T(8,128)S(1)}, u32[]{:S(2)}, u32[]{:S(2)}) %collective-permute-start.9) | collective-permute-done | bytes 4128 | tf_op jit(solution)/shard_map/ppermute | solution.py:237
  60.2 0.0 collective-permute-done.1.pair_hbm
  60.2 0.0 copy-start.2
  60.2 0.0 collective-permute-done.cycle_hbm
  60.3 0.0 copy-done.3
  60.3 0.0 copy-start.1
  60.3 0.7 divide_bitcast_fusion
  61.0 0.0 copy-done.2
  61.0 0.1 copy-done.1
  61.1 0.0 copy-start
  61.1 14.3 %shard_map.142 = f32[1024,512]{1,0:T(8,128)} custom-call(s32[1024]{0:T(1024)} %copy.19.ancestors_ref, s32[256]{0:T(256)} %cycle_pick_ref.1, s32[32]{0:T(128)} %pair_pick_ref.1, f32[1024,512]{1,0:T(8,128)} %get-tuple-element.5.state_hbm, f32[257,512]{1,0:T(8,128)} %copy-done.1, f32[33,512]{1,0:T(8,128)} %copy-done.2), custom_call_target="tpu_custom_call" | custom-call | bytes 8388608 | tf_op jit(solution)/shard_map/pallas_call | solution.py:191
  75.4 0.0 copy-done
  75.4 1.4 %scatter_fusion = s32[1024]{0:T(1024)S(1)} fusion(s32[1024]{0:T(1024)S(1)} %copy-done, s32[256]{0:T(256)S(1)} %compare_select_fusion, s32[256]{0:T(256)S(1)} %iota_add_fusion), kind=kCustom, calls=%fused_computation | custom fusion | bytes 4096 | tf_op jit(solution)/shard_map/scatter | solution.py:260
  76.8 0.7 scatter_fusion.1
  77.5 0.6 fusion
  (27 shorter events, 0.2 us)
Async XLA Ops:
  12.4 3.3 %collective-permute-start.2 = (f32[8,128]{1,0:T(8,128)}, f32[8,128]{1,0:T(8,128)S(1)}, u32[]{:S(2)}, u32[]{:S(2)}) collective-permute-start(f32[8,128]{1,0:T(8,128)} %get-tuple-element.6), channel_id=1, source_target_pairs={{0,1},{1,0},{2,3},{3,2},{4,5},{5,4},{6,7},{7,6},{8,9},{9,8},{10,11... | collective-permute-start | bytes 12296 | tf_op jit(solution)/shard_map/ppermute | solution.py:237
  17.2 4.0 %collective-permute-start.3 = (f32[8,128]{1,0:T(8,128)S(1)}, f32[8,128]{1,0:T(8,128)S(1)}, u32[]{:S(2)}, u32[]{:S(2)}) collective-permute-start(f32[8,128]{1,0:T(8,128)S(1)} %maximum_maximum_fusion), channel_id=1, source_target_pairs={{0,2},{1,3},{2,0},{3,1},{4,6},{5,7},{6,4},{7,5},{8,10},{9,11},{10,... | collective-permute-start | bytes 12296 | tf_op jit(solution)/shard_map/ppermute | solution.py:237
  21.3 2.5 %collective-permute-start.4 = (f32[8,128]{1,0:T(8,128)S(1)}, f32[8,128]{1,0:T(8,128)S(1)}, u32[]{:S(2)}, u32[]{:S(2)}) collective-permute-start(f32[8,128]{1,0:T(8,128)S(1)} %maximum_maximum_fusion.1), channel_id=1, source_target_pairs={{0,4},{1,5},{2,6},{3,7},{4,0},{5,1},{6,2},{7,3},{8,12},{9,13},{10,... | collective-permute-start | bytes 12296 | tf_op jit(solution)/shard_map/ppermute | solution.py:237
  23.9 6.8 %collective-permute-start.5 = (f32[8,128]{1,0:T(8,128)S(1)}, f32[8,128]{1,0:T(8,128)S(1)}, u32[]{:S(2)}, u32[]{:S(2)}) collective-permute-start(f32[8,128]{1,0:T(8,128)S(1)} %maximum_maximum_fusion.2), channel_id=1, source_target_pairs={{0,8},{8,0},{16,24},{24,16},{32,40},{40,32},{48,56},{56,48},{64,72... | collective-permute-start | bytes 12296 | tf_op jit(solution)/shard_map/ppermute | solution.py:237
  30.9 10.6 %collective-permute-start.6 = (f32[8,128]{1,0:T(8,128)S(1)}, f32[8,128]{1,0:T(8,128)S(1)}, u32[]{:S(2)}, u32[]{:S(2)}) collective-permute-start(f32[8,128]{1,0:T(8,128)S(1)} %maximum_maximum_fusion.3), channel_id=1, source_target_pairs={{0,16},{8,24},{16,0},{24,8},{32,48},{40,56},{48,32},{56,40},{64,80... | collective-permute-start | bytes 12296 | tf_op jit(solution)/shard_map/ppermute | solution.py:237
  32.2 12.3 %copy-start.4 = (s32[256]{0:T(256)S(1)}, s32[256]{0:T(256)}, u32[]{:S(2)}) copy-start(s32[256]{0:T(256)} %cycle_pick_ref.1) | copy-start | bytes 3076
  32.2 22.9 %copy-start.5 = (s32[32]{0:T(128)S(1)}, s32[32]{0:T(128)}, u32[]{:S(2)}) copy-start(s32[32]{0:T(128)} %pair_pick_ref.1) | copy-start | bytes 388
  32.2 28.1 %copy-start.3 = (f32[4,128]{1,0:T(4,128)S(1)}, f32[4,128]{1,0:T(4,128)}, u32[]{:S(2)}) copy-start(f32[4,128]{1,0:T(4,128)} %slice.96) | copy-start | bytes 6148
  34.7 25.5 %collective-permute-start.1 = (f32[33,512]{1,0:T(8,128)}, f32[33,512]{1,0:T(8,128)S(1)}, u32[]{:S(2)}, u32[]{:S(2)}) collective-permute-start(f32[33,512]{1,0:T(8,128)} %shard_map.141), channel_id=1, source_target_pairs={{4,0},{5,1},{6,2},{7,3},{0,4},{1,5},{2,6},{3,7},{12,8},{13,9},{14,... | collective-permute-start | bytes 202760 | tf_op jit(solution)/shard_map/ppermute | solution.py:19
  40.7 19.6 %collective-permute-start = (f32[257,512]{1,0:T(8,128)}, f32[257,512]{1,0:T(8,128)S(1)}, u32[]{:S(2)}, u32[]{:S(2)}) collective-permute-start(f32[257,512]{1,0:T(8,128)} %shard_map.140), channel_id=1, source_target_pairs={{248,0},{0,8},{8,16},{16,24},{24,32},{32,40},{40,48},{48,56},{56,6... | collective-permute-start | bytes 1579016 | tf_op jit(solution)/shard_map/ppermute | solution.py:19
  41.6 6.5 %collective-permute-start.7 = (f32[8,128]{1,0:T(8,128)S(1)}, f32[8,128]{1,0:T(8,128)S(1)}, u32[]{:S(2)}, u32[]{:S(2)}) collective-permute-start(f32[8,128]{1,0:T(8,128)S(1)} %maximum_maximum_fusion.4), channel_id=1, source_target_pairs={{0,32},{8,40},{16,48},{24,56},{32,0},{40,8},{48,16},{56,24},{64,96... | collective-permute-start | bytes 12296 | tf_op jit(solution)/shard_map/ppermute | solution.py:237
  48.3 7.8 %collective-permute-start.8 = (f32[8,128]{1,0:T(8,128)S(1)}, f32[8,128]{1,0:T(8,128)S(1)}, u32[]{:S(2)}, u32[]{:S(2)}) collective-permute-start(f32[8,128]{1,0:T(8,128)S(1)} %maximum_maximum_fusion.5), channel_id=1, source_target_pairs={{0,64},{8,72},{16,80},{24,88},{32,96},{40,104},{48,112},{56,120},{... | collective-permute-start | bytes 12296 | tf_op jit(solution)/shard_map/ppermute | solution.py:237
  56.2 4.0 %collective-permute-start.9 = (f32[8,128]{1,0:T(8,128)S(1)}, f32[8,128]{1,0:T(8,128)S(1)}, u32[]{:S(2)}, u32[]{:S(2)}) collective-permute-start(f32[8,128]{1,0:T(8,128)S(1)} %maximum_maximum_fusion.6), channel_id=1, source_target_pairs={{0,128},{8,136},{16,144},{24,152},{32,160},{40,168},{48,176},{56,1... | collective-permute-start | bytes 12296 | tf_op jit(solution)/shard_map/ppermute | solution.py:237
  60.2 0.7 copy-start.2
  60.3 0.8 %copy-start.1 = (f32[257,512]{1,0:T(8,128)}, f32[257,512]{1,0:T(8,128)S(1)}, u32[]{:S(2)}) copy-start(f32[257,512]{1,0:T(8,128)S(1)} %collective-permute-done.cycle_hbm) | copy-start | bytes 1579012
  61.1 14.3 %copy-start = (s32[1024]{0:T(1024)S(1)}, s32[1024]{0:T(1024)}, u32[]{:S(2)}) copy-start(s32[1024]{0:T(1024)} %copy.19.ancestors_ref) | copy-start | bytes 12292

commit v8 on v6

--- a/solution.py
+++ b/solution.py
@@ -20,9 +20,10 @@
 
 
 def steps_kernel(
-    current_ref, state_ref, prior_ref, transition_ref, drive_ref, decay_ref,
-    obs_matrix_ref, obs_weight_ref, observed_ref, state_out, message_out,
-    peak_acc, sum_acc, weighted_acc,
+    current_ref, ancestors_ref, cycle_pick_ref, pair_pick_ref, state_ref, prior_ref, transition_ref,
+    drive_ref, decay_ref, obs_matrix_ref, obs_weight_ref, observed_ref,
+    state_out, message_out, cycle_out, pair_out,
+    peak_acc, sum_acc, weighted_acc, full_state,
 ):
     block = pl.program_id(0)
     state = state_ref[...]
@@ -42,6 +43,8 @@
         misfit = predicted - observed_ref[step_index : step_index + 1, :]
         logw = logw - 0.5 * jnp.sum(obs_weight * misfit * misfit, axis=1, keepdims=True)
     state_out[...] = state
+    rows_per_block = state.shape[0]
+    full_state[pl.ds(pl.multiple_of(block * rows_per_block, rows_per_block), rows_per_block), :] = state
 
     @pl.when(block == 0)
     def _():
@@ -69,19 +72,44 @@
         if rest:
             message_out[k + 2 :, :] = jnp.zeros((rest, lanes), jnp.float32)
 
-
-def run_steps(particles, log_prior, transition, drive_vector, current, decay_rate, obs_matrix, obs_weight, observed):
+        for pick_ref, rows_out in ((cycle_pick_ref, cycle_out), (pair_pick_ref, pair_out)):
+            count = pick_ref.shape[0]
+
+            def copy_row(j, carry, pick_ref=pick_ref, rows_out=rows_out):
+                row = ancestors_ref[pick_ref[j]]
+                rows_out[pl.ds(j, 1), :] = full_state[pl.ds(row, 1), :]
+                return carry
+
+            lax.fori_loop(0, count, copy_row, 0)
+            rows_out[count : count + 1, 0:lanes] = sum_acc[...]
+            rows_out[count : count + 1, lanes : 2 * lanes] = peak_acc[...]
+            rows_out[count : count + 1, 2 * lanes :] = jnp.zeros((1, width_of(rows_out) - 2 * lanes), jnp.float32)
+
+
+def width_of(ref):
+    return ref.shape[1]
+
+
+def run_steps(
+    particles, log_prior, transition, drive_vector, current, decay_rate, obs_matrix, obs_weight, observed,
+    ancestors, cycle_pick, pair_pick,
+):
     rows, width = particles.shape
     n_obs = obs_matrix.shape[1]
     block = 256
     lanes = 128
     k = width // lanes
     message_rows = max(-(-(k + 2) // 8) * 8, 2 * k)
+    n_cycle = cycle_pick.shape[0]
+    n_pairs = pair_pick.shape[0]
     whole = lambda i: (0, 0)
     return pl.pallas_call(
         steps_kernel,
         grid=(rows // block,),
         in_specs=[
+            pl.BlockSpec(memory_space=pltpu.SMEM),
+            pl.BlockSpec(memory_space=pltpu.SMEM),
+            pl.BlockSpec(memory_space=pltpu.SMEM),
             pl.BlockSpec(memory_space=pltpu.SMEM),
             pl.BlockSpec((block, width), lambda i: (i, 0)),
             pl.BlockSpec((block, 1), lambda i: (i, 0)),
@@ -95,15 +123,20 @@
         out_specs=[
             pl.BlockSpec((block, width), lambda i: (i, 0)),
             pl.BlockSpec((message_rows, lanes), whole),
+            pl.BlockSpec((n_cycle + 1, width), whole),
+            pl.BlockSpec((n_pairs + 1, width), whole),
         ],
         out_shape=[
             jax.ShapeDtypeStruct((rows, width), jnp.float32),
             jax.ShapeDtypeStruct((message_rows, lanes), jnp.float32),
+            jax.ShapeDtypeStruct((n_cycle + 1, width), jnp.float32),
+            jax.ShapeDtypeStruct((n_pairs + 1, width), jnp.float32),
         ],
         scratch_shapes=[
             pltpu.VMEM((1, lanes), jnp.float32),
             pltpu.VMEM((1, lanes), jnp.float32),
             pltpu.VMEM((1, width), jnp.float32),
+            pltpu.VMEM((rows, width), jnp.float32),
         ],
         compiler_params=pltpu.CompilerParams(dimension_semantics=("arbitrary",)),
         cost_estimate=pl.CostEstimate(
@@ -113,6 +146,9 @@
         ),
     )(
         current,
+        ancestors,
+        cycle_pick,
+        pair_pick,
         particles,
         log_prior.reshape(rows, 1),
         transition,
@@ -138,8 +174,9 @@
     cycle_pick,
     pair_pick,
 ):
-    state, message = run_steps(
-        particles, log_prior, transition, drive_vector, current, decay_rate, obs_matrix, obs_weight, observed
+    state, message, cycle_out, pair_out = run_steps(
+        particles, log_prior, transition, drive_vector, current, decay_rate, obs_matrix, obs_weight, observed,
+        ancestors, cycle_pick, pair_pick,
     )
     n_blk = lax.axis_size(BLK)
     n_pair = lax.axis_size(PAIR)
@@ -149,12 +186,8 @@
     n_pairs = pair_pick.shape[0]
     lanes = message.shape[1]
     k = width // lanes
-    local_sum = message[k, 0]
-    local_peak = message[k + 1, 0]
-    stamp = message[k : 2 * k].reshape(1, width)
-
-    cycle_out = jnp.concatenate([state[ancestors[cycle_pick]], stamp])
-    pair_out = jnp.concatenate([state[ancestors[pair_pick]], stamp])
+    stamp = cycle_out[n_cycle : n_cycle + 1]
+
     cycle_in = shifted(cycle_out, BLK, 1)
     pair_in = shifted(pair_out, PAIR, n_pair // 2)
 
@@ -169,16 +202,18 @@
             body = message[: k + 1] * mine_scale + other[: k + 1] * other_scale
             message = jnp.concatenate([body, peak_row[None], jnp.zeros((pad, lanes), jnp.float32)])
             bit *= 2
-    total = message[k, 0]
-    peak = message[k + 1, 0]
-    mean_state = message[:k].reshape(width) / total
-
-    def group_weight(device_peak, device_sum):
+    total = message[k : k + 1]
+    peak = message[k + 1 : k + 2]
+    mean_state = (message[:k] / total).reshape(width)
+
+    def group_weight(row):
+        device_sum = row[:, :lanes]
+        device_peak = row[:, lanes : 2 * lanes]
         return jnp.log(jnp.maximum(groups * (device_sum * jnp.exp(device_peak - peak)) / total, 0.1))
 
-    own_w = group_weight(local_peak, local_sum)
-    cycle_w = group_weight(cycle_in[n_cycle, lanes], cycle_in[n_cycle, 0])
-    pair_w = group_weight(pair_in[n_pairs, lanes], pair_in[n_pairs, 0])
+    own_w = group_weight(stamp)
+    cycle_w = group_weight(cycle_in[n_cycle : n_cycle + 1])
+    pair_w = group_weight(pair_in[n_pairs : n_pairs + 1])
 
     source = (
         ancestors.at[cycle_pick]
@@ -188,11 +223,12 @@
     )
     table = jnp.concatenate([state, cycle_in[:n_cycle], pair_in[:n_pairs]], axis=0)
     migrated = table[source]
+    tiles = source.reshape(rows_here // lanes, lanes)
     group_logw = jnp.where(
-        source >= rows_here + n_cycle,
+        tiles >= rows_here + n_cycle,
         pair_w,
-        jnp.where(source >= rows_here, cycle_w, own_w),
-    )
+        jnp.where(tiles >= rows_here, cycle_w, own_w),
+    ).reshape(rows_here)
     return (migrated, group_logw, mean_state)
 
 
@@ -215,6 +251,4 @@
         P(BLK_PAIR),
     )
     out_specs = (P(BLK_PAIR, None), P(BLK_PAIR), P())
-    return jax.shard_map(
-        window, mesh=torus, in_specs=in_specs, out_specs=out_specs, check_vma=False
-    )
+    return jax.shard_map(window, mesh=torus, in_specs=in_specs, out_specs=out_specs, check_vma=False)

time: 72.8 us -> 63.2 us (0.87); the launches traced: 72.4 us -> 62 us
  local copies, waits for them, and re-layouts: 18.4 us -> 10.1 us
  between operations: 6.94 us -> 0.81 us
  Pallas kernels: 8.79 us -> 11.9 us
  waiting for transfers between devices: 7.81 us -> 8.76 us
    gather x4 -> x0, local copies, waits for them, and re-layouts: 5.23 us -> none  [the longest x2 2.89 us: window(): pair_out = jnp.concatenate([state[ancestors[pair_pick]], stamp])]
    slice x5 -> x0, local copies, waits for them, and re-layouts: 3.72 us -> none  [the longest x1 1.36 us: window(): local_peak = message[k + 1, 0]]
    pallas_call x1, Pallas kernels: 8.79 us -> 11.9 us  [run_steps(): pl.pallas_call(steps_kernel, grid=(rows // block,), in_specs=[pl.BlockSpe...]
    div x1 -> x0, other arithmetic: 1.21 us -> none  [window(): mean_state = message[:k].reshape(width) / total]
    ppermute x8, waiting for transfers between devices: 7.81 us -> 8.76 us  [window(): other = lax.ppermute(message, axis, [(i, i ^ bit) for i in range(size)])]
  transfers between devices with their start and end apart: 10 -> 10, of which waited for: 4 -> 6; matrix products, arithmetic and copies ran while one was open for 19% -> 4% of each run, Pallas kernels for 0% -> 0%
where the time goes in v8:
time: 63.2 us; the launch traced here: 62 us
  starting transfers between devices  24.7 us (39%)
  Pallas kernels  11.9 us (19%)
  local copies, waits for them, and re-layouts  10.1 us (16%)
  waiting for transfers between devices  8.76 us (14%)
  other arithmetic  5.85 us (9%)
  between operations  0.81 us (1%)
    ppermute x8, starting transfers between devices, window(): other = lax.ppermute(message, axis, [(i, i ^ bit) for i in range(size)])  19.7 us
    pallas_call x1, Pallas kernels, run_steps(): pl.pallas_call(steps_kernel, grid=(rows // block,), in_specs=[pl.BlockSpe...  11.9 us
    ppermute x8, waiting for transfers between devices, window(): other = lax.ppermute(message, axis, [(i, i ^ bit) for i in range(size)])  8.76 us
    ppermute x2, starting transfers between devices, shifted(): return lax.ppermute(block, axis, route)  4.93 us
    gather x1, local copies, waits for them, and re-layouts, window(): migrated = table[source]  4.87 us
    scatter x2, local copies, waits for them, and re-layouts, window(): source = ancestors.at[cycle_pick].set(rows_here + jnp.arange(n_cycle, dty...  2.09 us
    concatenate x1, other arithmetic, window(): jnp.concatenate([state, cycle_in[:n_cycle], pair_in[:n_pairs]], axis=0)  1.9 us
    reshape x1, local copies, waits for them, and re-layouts, run_steps(): log_prior.reshape(rows, 1)  1.71 us
  transfers between devices with their start and end apart: 10, of which 6 were waited for; matrix products, arithmetic and copies ran while one was open for 4% of the time, Pallas kernels for 0%

profile of v8, /device:TPU:1, one launch (start us, length us, event | category | flops | bytes accessed | tf_op | source)
XLA Modules:
  0.0 62.0 jit_solution(5910673402440993651)
XLA Ops:
  0.6 1.3 %copy.19.ancestors_ref = s32[1024]{0:T(1024)} copy(s32[1024]{0:T(1024)} %param.21) | data formatting | bytes 8192
  1.9 1.7 %copy.15.prior_ref = f32[1024,1]{1,0:T(8,128)} copy(f32[1024,1]{0,1:T(1,128)} %bitcast.54) | data formatting | bytes 8192 | tf_op jit(solution)/shard_map/reshape | solution.py:153
  3.6 0.0 copy-start.1
  3.6 0.0 copy-start.2
  3.6 0.0 copy-start
  3.6 11.9 %shard_map.139 = (f32[1024,512]{1,0:T(8,128)}, f32[8,128]{1,0:T(8,128)}, f32[257,512]{1,0:T(8,128)}, f32[33,512]{1,0:T(8,128)}) custom-call(f32[4]{0:T(128)} %current_ref.1, s32[1024]{0:T(1024)} %copy.19.ancestors_ref, s32[256]{0:T(256)} %cycle_pick_ref.1, s32[32]{0:T(128)} %pair_pick_ref.1, f32[1024,512]{1,0:T(8,128)} %state_ref.1, ...), custom_call_target="tpu_custom_call" | custom-call | flops 2684354560 | bytes 4718592 | tf_op jit(solution)/shard_map/pallas_call | solution.py:106
  15.5 2.1 %collective-permute-start.2 = (f32[8,128]{1,0:T(8,128)}, f32[8,128]{1,0:T(8,128)S(1)}, u32[]{:S(2)}, u32[]{:S(2)}) collective-permute-start(f32[8,128]{1,0:T(8,128)} %get-tuple-element.10), channel_id=1, source_target_pairs={{0,1},{1,0},{2,3},{3,2},{4,5},{5,4},{6,7},{7,6},{8,9},{9,8},{10,11... | collective-permute-start | bytes 12296 | tf_op jit(solution)/shard_map/ppermute | solution.py:198
  17.6 0.1 pad.20.clone
  17.7 1.1 %collective-permute-done.2 = f32[8,128]{1,0:T(8,128)S(1)} collective-permute-done((f32[8,128]{1,0:T(8,128)}, f32[8,128]{1,0:T(8,128)S(1)}, u32[]{:S(2)}, u32[]{:S(2)}) %collective-permute-start.2) | collective-permute-done | bytes 4128 | tf_op jit(solution)/shard_map/ppermute | solution.py:198
  18.8 0.7 %exponential_bitcast_fusion.15 = (f32[128]{0:T(128)S(1)}, f32[1,128]{1,0:T(1,128)S(1)}) fusion(f32[8,128]{1,0:T(8,128)} %get-tuple-element.10, f32[8,128]{1,0:T(8,128)S(1)} %collective-permute-done.2), kind=kLoop, calls=%fused_computation.54 | loop fusion | flops 256 | bytes 2048 | tf_op jit(solution)/shard_map/mul | solution.py:202
  19.5 0.7 %multiply_add_fusion.7 = f32[5,128]{1,0:T(8,128)S(1)} fusion(f32[8,128]{1,0:T(8,128)S(1)} %collective-permute-done.2, f32[8,128]{1,0:T(8,128)} %get-tuple-element.10, f32[128]{0:T(128)S(1)} %exponential_bitcast_fusion.14, f32[128]{0:T(128)S(1)} %get-tuple-element.25), kind=kLoop, calls=%fused_computation.22 | loop fusion | flops 1920 | bytes 8704 | tf_op jit(solution)/shard_map/add | solution.py:202
  20.2 0.1 maximum_maximum_fusion
  20.3 3.0 %collective-permute-start.3 = (f32[8,128]{1,0:T(8,128)S(1)}, f32[8,128]{1,0:T(8,128)S(1)}, u32[]{:S(2)}, u32[]{:S(2)}) collective-permute-start(f32[8,128]{1,0:T(8,128)S(1)} %maximum_maximum_fusion), channel_id=1, source_target_pairs={{0,2},{1,3},{2,0},{3,1},{4,6},{5,7},{6,4},{7,5},{8,10},{9,11},{10,... | collective-permute-start | bytes 12296 | tf_op jit(solution)/shard_map/ppermute | solution.py:198
  23.3 1.0 %collective-permute-done.3 = f32[8,128]{1,0:T(8,128)S(1)} collective-permute-done((f32[8,128]{1,0:T(8,128)S(1)}, f32[8,128]{1,0:T(8,128)S(1)}, u32[]{:S(2)}, u32[]{:S(2)}) %collective-permute-start.3) | collective-permute-done | bytes 4128 | tf_op jit(solution)/shard_map/ppermute | solution.py:198
  24.3 0.1 maximum_maximum_fusion.1
  24.4 1.5 %collective-permute-start.4 = (f32[8,128]{1,0:T(8,128)S(1)}, f32[8,128]{1,0:T(8,128)S(1)}, u32[]{:S(2)}, u32[]{:S(2)}) collective-permute-start(f32[8,128]{1,0:T(8,128)S(1)} %maximum_maximum_fusion.1), channel_id=1, source_target_pairs={{0,4},{1,5},{2,6},{3,7},{4,0},{5,1},{6,2},{7,3},{8,12},{9,13},{10,... | collective-permute-start | bytes 12296 | tf_op jit(solution)/shard_map/ppermute | solution.py:198
  25.9 4.8 %collective-permute-start = (f32[257,512]{1,0:T(8,128)}, f32[257,512]{1,0:T(8,128)S(1)}, u32[]{:S(2)}, u32[]{:S(2)}) collective-permute-start(f32[257,512]{1,0:T(8,128)} %get-tuple-element.8), channel_id=1, source_target_pairs={{248,0},{0,8},{8,16},{16,24},{24,32},{32,40},{40,48},{48,56},{56,6... | collective-permute-start | bytes 1579016 | tf_op jit(solution)/shard_map/ppermute | solution.py:19
  30.7 0.1 collective-permute-start.1
  30.9 0.0 collective-permute-done.4
  30.9 0.1 maximum_maximum_fusion.2
  31.0 2.1 %collective-permute-start.5 = (f32[8,128]{1,0:T(8,128)S(1)}, f32[8,128]{1,0:T(8,128)S(1)}, u32[]{:S(2)}, u32[]{:S(2)}) collective-permute-start(f32[8,128]{1,0:T(8,128)S(1)} %maximum_maximum_fusion.2), channel_id=1, source_target_pairs={{0,8},{8,0},{16,24},{24,16},{32,40},{40,32},{48,56},{56,48},{64,72... | collective-permute-start | bytes 12296 | tf_op jit(solution)/shard_map/ppermute | solution.py:198
  33.1 0.0 copy-done.1
  33.1 0.8 %collective-permute-done.5 = f32[8,128]{1,0:T(8,128)S(1)} collective-permute-done((f32[8,128]{1,0:T(8,128)S(1)}, f32[8,128]{1,0:T(8,128)S(1)}, u32[]{:S(2)}, u32[]{:S(2)}) %collective-permute-start.5) | collective-permute-done | bytes 4128 | tf_op jit(solution)/shard_map/ppermute | solution.py:198
  33.9 0.1 maximum_maximum_fusion.3
  34.0 0.0 collective-permute-start.6
  34.0 0.0 copy-done.2
  34.1 3.3 %collective-permute-done.6 = f32[8,128]{1,0:T(8,128)S(1)} collective-permute-done((f32[8,128]{1,0:T(8,128)S(1)}, f32[8,128]{1,0:T(8,128)S(1)}, u32[]{:S(2)}, u32[]{:S(2)}) %collective-permute-start.6) | collective-permute-done | bytes 4128 | tf_op jit(solution)/shard_map/ppermute | solution.py:198
  37.4 0.1 maximum_maximum_fusion.4
  37.5 3.0 %collective-permute-start.7 = (f32[8,128]{1,0:T(8,128)S(1)}, f32[8,128]{1,0:T(8,128)S(1)}, u32[]{:S(2)}, u32[]{:S(2)}) collective-permute-start(f32[8,128]{1,0:T(8,128)S(1)} %maximum_maximum_fusion.4), channel_id=1, source_target_pairs={{0,32},{8,40},{16,48},{24,56},{32,0},{40,8},{48,16},{56,24},{64,96... | collective-permute-start | bytes 12296 | tf_op jit(solution)/shard_map/ppermute | solution.py:198
  40.5 1.1 %collective-permute-done.7 = f32[8,128]{1,0:T(8,128)S(1)} collective-permute-done((f32[8,128]{1,0:T(8,128)S(1)}, f32[8,128]{1,0:T(8,128)S(1)}, u32[]{:S(2)}, u32[]{:S(2)}) %collective-permute-start.7) | collective-permute-done | bytes 4128 | tf_op jit(solution)/shard_map/ppermute | solution.py:198
  41.7 0.1 maximum_maximum_fusion.5
  41.8 5.2 %collective-permute-start.8 = (f32[8,128]{1,0:T(8,128)S(1)}, f32[8,128]{1,0:T(8,128)S(1)}, u32[]{:S(2)}, u32[]{:S(2)}) collective-permute-start(f32[8,128]{1,0:T(8,128)S(1)} %maximum_maximum_fusion.5), channel_id=1, source_target_pairs={{0,64},{8,72},{16,80},{24,88},{32,96},{40,104},{48,112},{56,120},{... | collective-permute-start | bytes 12296 | tf_op jit(solution)/shard_map/ppermute | solution.py:198
  47.0 0.0 copy-done
  47.0 1.4 %scatter_fusion = s32[1024]{0:T(1024)S(1)} fusion(s32[1024]{0:T(1024)S(1)} %copy-done, s32[256]{0:T(256)S(1)} %compare_select_fusion.1, s32[256]{0:T(256)S(1)} %iota_add_fusion), kind=kCustom, calls=%fused_computation.1 | custom fusion | bytes 4096 | tf_op jit(solution)/shard_map/scatter | solution.py:220
  48.4 0.7 %scatter_fusion.1 = s32[1024]{0:T(1024)S(1)} fusion(s32[1024]{0:T(1024)S(1)} %scatter_fusion, s32[32]{0:T(128)S(1)} %compare_select_fusion.2, s32[32]{0:T(128)S(1)} %iota_add_fusion.1), kind=kCustom, calls=%fused_computation.2 | custom fusion | bytes 512 | tf_op jit(solution)/shard_map/scatter | solution.py:222
  49.1 0.0 collective-permute-done.8
  49.2 0.1 maximum_maximum_fusion.6
  49.2 2.7 %collective-permute-start.9 = (f32[8,128]{1,0:T(8,128)S(1)}, f32[8,128]{1,0:T(8,128)S(1)}, u32[]{:S(2)}, u32[]{:S(2)}) collective-permute-start(f32[8,128]{1,0:T(8,128)S(1)} %maximum_maximum_fusion.6), channel_id=1, source_target_pairs={{0,128},{8,136},{16,144},{24,152},{32,160},{40,168},{48,176},{56,1... | collective-permute-start | bytes 12296 | tf_op jit(solution)/shard_map/ppermute | solution.py:198
  51.9 1.3 %collective-permute-done.9 = f32[8,128]{1,0:T(8,128)S(1)} collective-permute-done((f32[8,128]{1,0:T(8,128)S(1)}, f32[8,128]{1,0:T(8,128)S(1)}, u32[]{:S(2)}, u32[]{:S(2)}) %collective-permute-start.9) | collective-permute-done | bytes 4128 | tf_op jit(solution)/shard_map/ppermute | solution.py:198
  53.3 0.0 collective-permute-done.1
  53.3 0.0 collective-permute-done
  53.3 0.7 %log_bitcast_fusion.2 = (f32[128]{0:T(128)S(1)}, f32[128]{0:T(128)S(1)}, f32[128]{0:T(128)S(1)}, f32[128]{0:T(128)S(1)}) fusion(f32[1,128]{1,0:T(1,128)S(1)} %get-tuple-element.12, f32[33,512]{1,0:T(8,128)S(1)} %collective-permute-done.1, f32[5,128]{1,0:T(8,128)S(1)} %multiply_add_fusion, f32[257,512]{1,0:T(8,128)S(1)} %collective-permute-done, ...), kind=kLoop, calls=%fused_computation.37 | loop fusion | flops 1920 | bytes 6144 | tf_op jit(solution)/shard_map/jit(_where)/broadcast_in_dim | solution.py:227
  54.0 0.6 divide_bitcast_fusion
  54.6 1.9 %pad_maximum_fusion = f32[1312,512]{1,0:T(8,128)S(1)} fusion(f32[32,512]{1,0:T(8,128)S(1)} %slice.133, f32[256,512]{1,0:T(8,128)S(1)} %slice.132, f32[1024,512]{1,0:T(8,128)} %get-tuple-element.7), kind=kLoop, calls=%fused_computation.3 | loop fusion | flops 1343488 | bytes 5373952 | tf_op jit(solution)/shard_map/concatenate | solution.py:224
  56.5 4.9 %gather_fusion = f32[1024,512]{1,0:T(8,128)} fusion(f32[1312,512]{1,0:T(8,128)S(1)} %pad_maximum_fusion, s32[1024]{0:T(1024)S(1)} %fusion), kind=kCustom, calls=%fused_computation | custom fusion | bytes 4198400 | tf_op jit(solution)/shard_map/gather | solution.py:225
  61.4 0.6 fusion.1
  (30 shorter events, 0.2 us)
Async XLA Ops:
  3.6 29.4 %copy-start.1 = (s32[256]{0:T(256)S(1)}, s32[256]{0:T(256)}, u32[]{:S(2)}) copy-start(s32[256]{0:T(256)} %cycle_pick_ref.1) | copy-start | bytes 3076
  3.6 30.4 %copy-start.2 = (s32[32]{0:T(128)S(1)}, s32[32]{0:T(128)}, u32[]{:S(2)}) copy-start(s32[32]{0:T(128)} %pair_pick_ref.1) | copy-start | bytes 388
  3.6 43.4 %copy-start = (s32[1024]{0:T(1024)S(1)}, s32[1024]{0:T(1024)}, u32[]{:S(2)}) copy-start(s32[1024]{0:T(1024)} %copy.19.ancestors_ref) | copy-start | bytes 12292
  15.5 3.3 %collective-permute-start.2 = (f32[8,128]{1,0:T(8,128)}, f32[8,128]{1,0:T(8,128)S(1)}, u32[]{:S(2)}, u32[]{:S(2)}) collective-permute-start(f32[8,128]{1,0:T(8,128)} %get-tuple-element.10), channel_id=1, source_target_pairs={{0,1},{1,0},{2,3},{3,2},{4,5},{5,4},{6,7},{7,6},{8,9},{9,8},{10,11... | collective-permute-start | bytes 12296 | tf_op jit(solution)/shard_map/ppermute | solution.py:198
  20.3 4.0 %collective-permute-start.3 = (f32[8,128]{1,0:T(8,128)S(1)}, f32[8,128]{1,0:T(8,128)S(1)}, u32[]{:S(2)}, u32[]{:S(2)}) collective-permute-start(f32[8,128]{1,0:T(8,128)S(1)} %maximum_maximum_fusion), channel_id=1, source_target_pairs={{0,2},{1,3},{2,0},{3,1},{4,6},{5,7},{6,4},{7,5},{8,10},{9,11},{10,... | collective-permute-start | bytes 12296 | tf_op jit(solution)/shard_map/ppermute | solution.py:198
  24.4 6.5 %collective-permute-start.4 = (f32[8,128]{1,0:T(8,128)S(1)}, f32[8,128]{1,0:T(8,128)S(1)}, u32[]{:S(2)}, u32[]{:S(2)}) collective-permute-start(f32[8,128]{1,0:T(8,128)S(1)} %maximum_maximum_fusion.1), channel_id=1, source_target_pairs={{0,4},{1,5},{2,6},{3,7},{4,0},{5,1},{6,2},{7,3},{8,12},{9,13},{10,... | collective-permute-start | bytes 12296 | tf_op jit(solution)/shard_map/ppermute | solution.py:198
  25.9 27.4 %collective-permute-start = (f32[257,512]{1,0:T(8,128)}, f32[257,512]{1,0:T(8,128)S(1)}, u32[]{:S(2)}, u32[]{:S(2)}) collective-permute-start(f32[257,512]{1,0:T(8,128)} %get-tuple-element.8), channel_id=1, source_target_pairs={{248,0},{0,8},{8,16},{16,24},{24,32},{32,40},{40,48},{48,56},{56,6... | collective-permute-start | bytes 1579016 | tf_op jit(solution)/shard_map/ppermute | solution.py:19
  30.7 22.5 %collective-permute-start.1 = (f32[33,512]{1,0:T(8,128)}, f32[33,512]{1,0:T(8,128)S(1)}, u32[]{:S(2)}, u32[]{:S(2)}) collective-permute-start(f32[33,512]{1,0:T(8,128)} %get-tuple-element.9), channel_id=1, source_target_pairs={{4,0},{5,1},{6,2},{7,3},{0,4},{1,5},{2,6},{3,7},{12,8},{13,9},{14,... | collective-permute-start | bytes 202760 | tf_op jit(solution)/shard_map/ppermute | solution.py:19
  31.0 2.9 %collective-permute-start.5 = (f32[8,128]{1,0:T(8,128)S(1)}, f32[8,128]{1,0:T(8,128)S(1)}, u32[]{:S(2)}, u32[]{:S(2)}) collective-permute-start(f32[8,128]{1,0:T(8,128)S(1)} %maximum_maximum_fusion.2), channel_id=1, source_target_pairs={{0,8},{8,0},{16,24},{24,16},{32,40},{40,32},{48,56},{56,48},{64,72... | collective-permute-start | bytes 12296 | tf_op jit(solution)/shard_map/ppermute | solution.py:198
  34.0 3.4 %collective-permute-start.6 = (f32[8,128]{1,0:T(8,128)S(1)}, f32[8,128]{1,0:T(8,128)S(1)}, u32[]{:S(2)}, u32[]{:S(2)}) collective-permute-start(f32[8,128]{1,0:T(8,128)S(1)} %maximum_maximum_fusion.3), channel_id=1, source_target_pairs={{0,16},{8,24},{16,0},{24,8},{32,48},{40,56},{48,32},{56,40},{64,80... | collective-permute-start | bytes 12296 | tf_op jit(solution)/shard_map/ppermute | solution.py:198
  37.5 4.2 %collective-permute-start.7 = (f32[8,128]{1,0:T(8,128)S(1)}, f32[8,128]{1,0:T(8,128)S(1)}, u32[]{:S(2)}, u32[]{:S(2)}) collective-permute-start(f32[8,128]{1,0:T(8,128)S(1)} %maximum_maximum_fusion.4), channel_id=1, source_target_pairs={{0,32},{8,40},{16,48},{24,56},{32,0},{40,8},{48,16},{56,24},{64,96... | collective-permute-start | bytes 12296 | tf_op jit(solution)/shard_map/ppermute | solution.py:198
  41.8 7.3 %collective-permute-start.8 = (f32[8,128]{1,0:T(8,128)S(1)}, f32[8,128]{1,0:T(8,128)S(1)}, u32[]{:S(2)}, u32[]{:S(2)}) collective-permute-start(f32[8,128]{1,0:T(8,128)S(1)} %maximum_maximum_fusion.5), channel_id=1, source_target_pairs={{0,64},{8,72},{16,80},{24,88},{32,96},{40,104},{48,112},{56,120},{... | collective-permute-start | bytes 12296 | tf_op jit(solution)/shard_map/ppermute | solution.py:198
  49.2 4.0 %collective-permute-start.9 = (f32[8,128]{1,0:T(8,128)S(1)}, f32[8,128]{1,0:T(8,128)S(1)}, u32[]{:S(2)}, u32[]{:S(2)}) collective-permute-start(f32[8,128]{1,0:T(8,128)S(1)} %maximum_maximum_fusion.6), channel_id=1, source_target_pairs={{0,128},{8,136},{16,144},{24,152},{32,160},{40,168},{48,176},{56,1... | collective-permute-start | bytes 12296 | tf_op jit(solution)/shard_map/ppermute | solution.py:198

commit v9 on v6

--- a/solution.py
+++ b/solution.py
@@ -149,8 +149,6 @@
     n_pairs = pair_pick.shape[0]
     lanes = message.shape[1]
     k = width // lanes
-    local_sum = message[k, 0]
-    local_peak = message[k + 1, 0]
     stamp = message[k : 2 * k].reshape(1, width)
 
     cycle_out = jnp.concatenate([state[ancestors[cycle_pick]], stamp])
@@ -159,26 +157,47 @@
     pair_in = shifted(pair_out, PAIR, n_pair // 2)
 
     pad = message.shape[0] - (k + 2)
-    for axis, size in ((PAIR, n_pair), (BLK, n_blk)):
-        bit = 1
-        while bit < size:
-            other = lax.ppermute(message, axis, [(i, i ^ bit) for i in range(size)])
-            peak_row = jnp.maximum(message[k + 1], other[k + 1])
-            mine_scale = jnp.exp(message[k + 1] - peak_row)
-            other_scale = jnp.exp(other[k + 1] - peak_row)
-            body = message[: k + 1] * mine_scale + other[: k + 1] * other_scale
-            message = jnp.concatenate([body, peak_row[None], jnp.zeros((pad, lanes), jnp.float32)])
-            bit *= 2
-    total = message[k, 0]
-    peak = message[k + 1, 0]
-    mean_state = message[:k].reshape(width) / total
-
-    def group_weight(device_peak, device_sum):
+
+    def combine(mine, other):
+        peak_row = jnp.maximum(mine[k + 1], other[k + 1])
+        mine_scale = jnp.exp(mine[k + 1] - peak_row)
+        other_scale = jnp.exp(other[k + 1] - peak_row)
+        body = mine[: k + 1] * mine_scale + other[: k + 1] * other_scale
+        return jnp.concatenate([body, peak_row[None], jnp.zeros((pad, lanes), jnp.float32)])
+
+    def ring_of_four(message, axis):
+        got = [lax.ppermute(message, axis, [(i, (i + s) % 4) for i in range(4)]) for s in (1, 2, 3)]
+        even = lax.axis_index(axis) % 2 == 0
+        own_pair = combine(message, jnp.where(even, got[2], got[0]))
+        other_pair = combine(got[1], jnp.where(even, got[0], got[2]))
+        return combine(own_pair, other_pair)
+
+    def swap(message, axis, bit):
+        size = lax.axis_size(axis)
+        return combine(message, lax.ppermute(message, axis, [(i, i ^ bit) for i in range(size)]))
+
+    stages = [
+        lambda m: ring_of_four(m, "pair_1"),
+        lambda m: ring_of_four(m, ("blk_0", "pair_0")),
+        lambda m: swap(m, "blk_2", 1),
+        lambda m: swap(m, "blk_1", 1),
+        lambda m: swap(m, "blk_1", 2),
+        lambda m: swap(m, "blk_1", 4),
+    ]
+    for stage in stages:
+        message = stage(message)
+    total = message[k : k + 1]
+    peak = message[k + 1 : k + 2]
+    mean_state = (message[:k] / total).reshape(width)
+
+    def group_weight(row):
+        device_sum = row[:, :lanes]
+        device_peak = row[:, lanes : 2 * lanes]
         return jnp.log(jnp.maximum(groups * (device_sum * jnp.exp(device_peak - peak)) / total, 0.1))
 
-    own_w = group_weight(local_peak, local_sum)
-    cycle_w = group_weight(cycle_in[n_cycle, lanes], cycle_in[n_cycle, 0])
-    pair_w = group_weight(pair_in[n_pairs, lanes], pair_in[n_pairs, 0])
+    own_w = group_weight(stamp)
+    cycle_w = group_weight(cycle_in[n_cycle : n_cycle + 1])
+    pair_w = group_weight(pair_in[n_pairs : n_pairs + 1])
 
     source = (
         ancestors.at[cycle_pick]
@@ -188,11 +207,12 @@
     )
     table = jnp.concatenate([state, cycle_in[:n_cycle], pair_in[:n_pairs]], axis=0)
     migrated = table[source]
+    tiles = source.reshape(rows_here // lanes, lanes)
     group_logw = jnp.where(
-        source >= rows_here + n_cycle,
+        tiles >= rows_here + n_cycle,
         pair_w,
-        jnp.where(source >= rows_here, cycle_w, own_w),
-    )
+        jnp.where(tiles >= rows_here, cycle_w, own_w),
+    ).reshape(rows_here)
     return (migrated, group_logw, mean_state)
 
 

time: 72.8 us -> 63.5 us (0.87)
  the two profiles are of different devices: /device:TPU:1 before, /device:TPU:2 now
where the time goes in v9:
time: 63.5 us; the launch traced here: 63.2 us
  starting transfers between devices  17.8 us (28%)
  local copies, waits for them, and re-layouts  17.3 us (27%)
  waiting for transfers between devices  14.6 us (23%)
  Pallas kernels  8.78 us (14%)
  other arithmetic  3.73 us (6%)
  between operations  0.96 us (2%)
    ppermute x4, waiting for transfers between devices, swap(): lax.ppermute(message, axis, [(i, i ^ bit) for i in range(size)])  11.3 us
    ppermute x6, starting transfers between devices, ring_of_four(): lax.ppermute(message, axis, [(i, (i + s) % 4) for i in range(4)])  10.7 us
    pallas_call x1, Pallas kernels, run_steps(): pl.pallas_call(steps_kernel, grid=(rows // block,), in_specs=[pl.BlockSpe...  8.78 us
    ppermute x4, starting transfers between devices, swap(): lax.ppermute(message, axis, [(i, i ^ bit) for i in range(size)])  6.99 us
    gather x1, local copies, waits for them, and re-layouts, window(): migrated = table[source]  4.87 us
    gather x2, local copies, waits for them, and re-layouts, window(): cycle_out = jnp.concatenate([state[ancestors[cycle_pick]], stamp])  4.17 us
    ppermute x6, waiting for transfers between devices, ring_of_four(): lax.ppermute(message, axis, [(i, (i + s) % 4) for i in range(4)])  3.28 us
    gather x2, local copies, waits for them, and re-layouts, window(): pair_out = jnp.concatenate([state[ancestors[pair_pick]], stamp])  2.89 us
  transfers between devices with their start and end apart: 12, of which 5 were waited for; matrix products, arithmetic and copies ran while one was open for 17% of the time, Pallas kernels for 0%

profile of v9, /device:TPU:2, one launch (start us, length us, event | category | flops | bytes accessed | tf_op | source)
XLA Modules:
  0.0 63.2 jit_solution(10230093843819704350)
XLA Ops:
  0.6 0.7 %copy.19 = s32[1024]{0:T(1024)S(1)} copy(s32[1024]{0:T(1024)} %param.21) | data formatting | bytes 8192
  1.3 1.7 %copy.15.prior_ref = f32[1024,1]{1,0:T(8,128)} copy(f32[1024,1]{0,1:T(1,128)} %bitcast.72) | data formatting | bytes 8192 | tf_op jit(solution)/shard_map/reshape | solution.py:117
  3.0 0.0 copy-start.1
  3.0 8.8 %shard_map.139 = (f32[1024,512]{1,0:T(8,128)}, f32[8,128]{1,0:T(8,128)}) custom-call(f32[4]{0:T(128)} %current_ref.1, f32[1024,512]{1,0:T(8,128)} %state_ref.1, f32[1024,1]{1,0:T(8,128)} %copy.15.prior_ref, bf16[512,512]{1,0:T(8,128)(2,1)} %transition_ref.1, f32[1,512]{1,0:T(1,128)} %bitcast.75, f32[1,512]{1,0:T(1,128)} %bitcast.76, ...), custom_call_target="tpu_custom_call" | custom-call | flops 2684354560 | bytes 4718592 | tf_op jit(solution)/shard_map/pallas_call | solution.py:81
  11.8 2.3 %collective-permute-start.2 = (f32[8,128]{1,0:T(8,128)}, f32[8,128]{1,0:T(8,128)S(1)}, u32[]{:S(2)}, u32[]{:S(2)}) collective-permute-start(f32[8,128]{1,0:T(8,128)} %get-tuple-element.6), channel_id=1, source_target_pairs={{0,3},{1,0},{2,1},{3,2},{4,7},{5,4},{6,5},{7,6},{8,11},{9,8},{10,9... | collective-permute-start | bytes 12296 | tf_op jit(solution)/shard_map/ppermute | solution.py:169
  14.1 0.0 collective-permute-start.3
  14.1 3.1 %collective-permute-start.4 = (f32[8,128]{1,0:T(8,128)}, f32[8,128]{1,0:T(8,128)S(1)}, u32[]{:S(2)}, u32[]{:S(2)}) collective-permute-start(f32[8,128]{1,0:T(8,128)} %get-tuple-element.6), channel_id=1, source_target_pairs={{0,2},{1,3},{2,0},{3,1},{4,6},{5,7},{6,4},{7,5},{8,10},{9,11},{10,... | collective-permute-start | bytes 12296 | tf_op jit(solution)/shard_map/ppermute | solution.py:169
  17.2 0.7 %slice.116 = f32[4,128]{1,0:T(4,128)S(1)} slice(f32[8,128]{1,0:T(8,128)} %get-tuple-element.6), slice={[4:8], [0:128]} | slice | bytes 4096 | tf_op jit(solution)/shard_map/slice | solution.py:152
  18.0 0.0 copy-done.1
  18.0 1.4 %gather_fusion = s32[256]{0:T(256)S(1)} fusion(s32[1024]{0:T(1024)S(1)} %copy.19, s32[1024]{0:T(1024)S(1)} %pad_clamp_fusion.3), kind=kCustom, calls=%fused_computation | custom fusion | bytes 3072 | tf_op jit(solution)/shard_map/gather | solution.py:154
  19.4 0.0 copy-start.2
  19.4 0.0 copy-start
  19.4 2.8 %gather_fusion.1 = f32[256,512]{1,0:T(8,128)S(1)} fusion(f32[1024,512]{1,0:T(8,128)} %get-tuple-element.5, s32[1024]{0:T(1024)S(1)} %pad_clamp_fusion.2), kind=kCustom, calls=%fused_computation.1 | custom fusion | bytes 1049600 | tf_op jit(solution)/shard_map/gather | solution.py:154
  22.3 0.1 collective-permute-start
  22.4 0.0 copy-done.2
  22.4 0.7 %gather_fusion.2 = s32[32]{0:T(128)S(1)} fusion(s32[1024]{0:T(1024)S(1)} %copy.19, s32[1024]{0:T(1024)S(1)} %pad_clamp_fusion.1), kind=kCustom, calls=%fused_computation.2 | custom fusion | bytes 384 | tf_op jit(solution)/shard_map/gather | solution.py:155
  23.1 0.1 pad.14.clone
  23.2 0.0 collective-permute-done.2
  23.2 0.0 collective-permute-done.3
  23.2 0.0 copy-done
  23.2 0.0 collective-permute-done.4
  23.3 0.1 maximum_maximum_fusion
  23.3 3.0 %collective-permute-start.5 = (f32[8,128]{1,0:T(8,128)S(1)}, f32[8,128]{1,0:T(8,128)S(1)}, u32[]{:S(2)}, u32[]{:S(2)}) collective-permute-start(f32[8,128]{1,0:T(8,128)S(1)} %maximum_maximum_fusion), channel_id=1, source_target_pairs={{0,132},{4,0},{128,4},{132,128},{1,133},{5,1},{129,5},{133,129},{2... | collective-permute-start | bytes 12296 | tf_op jit(solution)/shard_map/ppermute | solution.py:169
  26.4 0.0 collective-permute-start.6
  26.4 2.2 %collective-permute-start.7 = (f32[8,128]{1,0:T(8,128)S(1)}, f32[8,128]{1,0:T(8,128)S(1)}, u32[]{:S(2)}, u32[]{:S(2)}) collective-permute-start(f32[8,128]{1,0:T(8,128)S(1)} %maximum_maximum_fusion), channel_id=1, source_target_pairs={{0,128},{4,132},{128,0},{132,4},{1,129},{5,133},{129,1},{133,5},{2... | collective-permute-start | bytes 12296 | tf_op jit(solution)/shard_map/ppermute | solution.py:169
  28.6 0.0 collective-permute-done.5
  28.6 3.0 %collective-permute-done.6 = f32[8,128]{1,0:T(8,128)S(1)} collective-permute-done((f32[8,128]{1,0:T(8,128)S(1)}, f32[8,128]{1,0:T(8,128)S(1)}, u32[]{:S(2)}, u32[]{:S(2)}) %collective-permute-start.6) | collective-permute-done | bytes 4128 | tf_op jit(solution)/shard_map/ppermute | solution.py:169
  31.6 0.3 collective-permute-done.7
  31.9 0.1 maximum_maximum_fusion.1
  32.0 4.8 %collective-permute-start.8 = (f32[8,128]{1,0:T(8,128)S(1)}, f32[8,128]{1,0:T(8,128)S(1)}, u32[]{:S(2)}, u32[]{:S(2)}) collective-permute-start(f32[8,128]{1,0:T(8,128)S(1)} %maximum_maximum_fusion.1), channel_id=1, source_target_pairs={{0,8},{8,0},{1,9},{9,1},{2,10},{10,2},{3,11},{11,3},{4,12},{12,4},... | collective-permute-start | bytes 12296 | tf_op jit(solution)/shard_map/ppermute | solution.py:177
  36.8 2.2 %gather_fusion.3 = f32[32,512]{1,0:T(8,128)S(1)} fusion(f32[1024,512]{1,0:T(8,128)} %get-tuple-element.5, s32[1024]{0:T(1024)S(1)} %pad_clamp_fusion), kind=kCustom, calls=%fused_computation.3 | custom fusion | bytes 131200 | tf_op jit(solution)/shard_map/gather | solution.py:155
  39.0 0.0 collective-permute-done.8
  39.1 0.1 maximum_maximum_fusion.2
  39.2 0.0 collective-permute-start.9
  39.2 0.1 collective-permute-start.1
  39.3 3.5 %collective-permute-done.9 = f32[8,128]{1,0:T(8,128)S(1)} collective-permute-done((f32[8,128]{1,0:T(8,128)S(1)}, f32[8,128]{1,0:T(8,128)S(1)}, u32[]{:S(2)}, u32[]{:S(2)}) %collective-permute-start.9) | collective-permute-done | bytes 4128 | tf_op jit(solution)/shard_map/ppermute | solution.py:177
  42.8 0.1 maximum_maximum_fusion.3
  42.9 0.0 collective-permute-start.10
  42.9 1.4 %scatter_fusion = s32[1024]{0:T(1024)S(1)} fusion(s32[1024]{0:T(1024)S(1)} %copy.19, s32[256]{0:T(256)S(1)} %get-tuple-element.43, s32[256]{0:T(256)S(1)} %get-tuple-element.44), kind=kCustom, calls=%fused_computation.5 | custom fusion | bytes 4096 | tf_op jit(solution)/shard_map/scatter | solution.py:204
  44.4 0.7 %scatter_fusion.1 = s32[1024]{0:T(1024)S(1)} fusion(s32[1024]{0:T(1024)S(1)} %scatter_fusion, s32[32]{0:T(128)S(1)} %compare_select_fusion.4, s32[32]{0:T(128)S(1)} %iota_add_fusion.1), kind=kCustom, calls=%fused_computation.6 | custom fusion | bytes 512 | tf_op jit(solution)/shard_map/scatter | solution.py:206
  45.1 2.4 %collective-permute-done.10 = f32[8,128]{1,0:T(8,128)S(1)} collective-permute-done((f32[8,128]{1,0:T(8,128)S(1)}, f32[8,128]{1,0:T(8,128)S(1)}, u32[]{:S(2)}, u32[]{:S(2)}) %collective-permute-start.10) | collective-permute-done | bytes 4128 | tf_op jit(solution)/shard_map/ppermute | solution.py:177
  47.5 0.1 maximum_maximum_fusion.4
  47.5 2.1 %collective-permute-start.11 = (f32[8,128]{1,0:T(8,128)S(1)}, f32[8,128]{1,0:T(8,128)S(1)}, u32[]{:S(2)}, u32[]{:S(2)}) collective-permute-start(f32[8,128]{1,0:T(8,128)S(1)} %maximum_maximum_fusion.4), channel_id=1, source_target_pairs={{0,64},{16,80},{32,96},{48,112},{64,0},{80,16},{96,32},{112,48},{1... | collective-permute-start | bytes 12296 | tf_op jit(solution)/shard_map/ppermute | solution.py:177
  49.6 5.4 %collective-permute-done.11 = f32[8,128]{1,0:T(8,128)S(1)} collective-permute-done((f32[8,128]{1,0:T(8,128)S(1)}, f32[8,128]{1,0:T(8,128)S(1)}, u32[]{:S(2)}, u32[]{:S(2)}) %collective-permute-start.11) | collective-permute-done | bytes 4128 | tf_op jit(solution)/shard_map/ppermute | solution.py:177
  55.1 0.0 collective-permute-done.1
  55.1 0.0 collective-permute-done
  55.2 0.6 divide_bitcast_fusion
  55.8 1.9 %pad_maximum_fusion = f32[1312,512]{1,0:T(8,128)S(1)} fusion(f32[32,512]{1,0:T(8,128)S(1)} %slice.160, f32[256,512]{1,0:T(8,128)S(1)} %slice.159, f32[1024,512]{1,0:T(8,128)} %get-tuple-element.5), kind=kLoop, calls=%fused_computation.7 | loop fusion | flops 1343488 | bytes 5373952 | tf_op jit(solution)/shard_map/concatenate | solution.py:208
  57.7 4.9 %gather_fusion.4 = f32[1024,512]{1,0:T(8,128)} fusion(f32[1312,512]{1,0:T(8,128)S(1)} %pad_maximum_fusion, s32[1024]{0:T(1024)S(1)} %fusion), kind=kCustom, calls=%fused_computation.4 | custom fusion | bytes 4198400 | tf_op jit(solution)/shard_map/gather | solution.py:209
  62.6 0.6 fusion.1
  (37 shorter events, 0.3 us)
Async XLA Ops:
  3.0 14.9 %copy-start.1 = (s32[256]{0:T(256)S(1)}, s32[256]{0:T(256)}, u32[]{:S(2)}) copy-start(s32[256]{0:T(256)} %param.22) | copy-start | bytes 3076
  11.8 11.3 %collective-permute-start.2 = (f32[8,128]{1,0:T(8,128)}, f32[8,128]{1,0:T(8,128)S(1)}, u32[]{:S(2)}, u32[]{:S(2)}) collective-permute-start(f32[8,128]{1,0:T(8,128)} %get-tuple-element.6), channel_id=1, source_target_pairs={{0,3},{1,0},{2,1},{3,2},{4,7},{5,4},{6,5},{7,6},{8,11},{9,8},{10,9... | collective-permute-start | bytes 12296 | tf_op jit(solution)/shard_map/ppermute | solution.py:169
  14.1 9.0 %collective-permute-start.3 = (f32[8,128]{1,0:T(8,128)}, f32[8,128]{1,0:T(8,128)S(1)}, u32[]{:S(2)}, u32[]{:S(2)}) collective-permute-start(f32[8,128]{1,0:T(8,128)} %get-tuple-element.6), channel_id=1, source_target_pairs={{0,1},{1,2},{2,3},{3,0},{4,5},{5,6},{6,7},{7,4},{8,9},{9,10},{10,1... | collective-permute-start | bytes 12296 | tf_op jit(solution)/shard_map/ppermute | solution.py:169
  14.1 9.1 %collective-permute-start.4 = (f32[8,128]{1,0:T(8,128)}, f32[8,128]{1,0:T(8,128)S(1)}, u32[]{:S(2)}, u32[]{:S(2)}) collective-permute-start(f32[8,128]{1,0:T(8,128)} %get-tuple-element.6), channel_id=1, source_target_pairs={{0,2},{1,3},{2,0},{3,1},{4,6},{5,7},{6,4},{7,5},{8,10},{9,11},{10,... | collective-permute-start | bytes 12296 | tf_op jit(solution)/shard_map/ppermute | solution.py:169
  19.4 3.0 %copy-start.2 = (s32[32]{0:T(128)S(1)}, s32[32]{0:T(128)}, u32[]{:S(2)}) copy-start(s32[32]{0:T(128)} %param.23) | copy-start | bytes 388
  19.4 3.8 %copy-start = (f32[8,128]{1,0:T(8,128)S(1)}, f32[8,128]{1,0:T(8,128)}, u32[]{:S(2)}) copy-start(f32[8,128]{1,0:T(8,128)} %get-tuple-element.6) | copy-start | bytes 12292
  22.3 32.9 %collective-permute-start = (f32[257,512]{1,0:T(8,128)S(1)}, f32[257,512]{1,0:T(8,128)S(1)}, u32[]{:S(2)}, u32[]{:S(2)}) collective-permute-start(f32[257,512]{1,0:T(8,128)S(1)} %pad_maximum_fusion.1), channel_id=1, source_target_pairs={{248,0},{0,8},{8,16},{16,24},{24,32},{32,40},{40,48},{48,56},{56,6... | collective-permute-start | bytes 1579016 | tf_op jit(solution)/shard_map/ppermute | solution.py:19
  23.3 5.3 %collective-permute-start.5 = (f32[8,128]{1,0:T(8,128)S(1)}, f32[8,128]{1,0:T(8,128)S(1)}, u32[]{:S(2)}, u32[]{:S(2)}) collective-permute-start(f32[8,128]{1,0:T(8,128)S(1)} %maximum_maximum_fusion), channel_id=1, source_target_pairs={{0,132},{4,0},{128,4},{132,128},{1,133},{5,1},{129,5},{133,129},{2... | collective-permute-start | bytes 12296 | tf_op jit(solution)/shard_map/ppermute | solution.py:169
  26.4 5.2 %collective-permute-start.6 = (f32[8,128]{1,0:T(8,128)S(1)}, f32[8,128]{1,0:T(8,128)S(1)}, u32[]{:S(2)}, u32[]{:S(2)}) collective-permute-start(f32[8,128]{1,0:T(8,128)S(1)} %maximum_maximum_fusion), channel_id=1, source_target_pairs={{0,4},{4,128},{128,132},{132,0},{1,5},{5,129},{129,133},{133,1},{2... | collective-permute-start | bytes 12296 | tf_op jit(solution)/shard_map/ppermute | solution.py:169
  26.4 5.5 %collective-permute-start.7 = (f32[8,128]{1,0:T(8,128)S(1)}, f32[8,128]{1,0:T(8,128)S(1)}, u32[]{:S(2)}, u32[]{:S(2)}) collective-permute-start(f32[8,128]{1,0:T(8,128)S(1)} %maximum_maximum_fusion), channel_id=1, source_target_pairs={{0,128},{4,132},{128,0},{132,4},{1,129},{5,133},{129,1},{133,5},{2... | collective-permute-start | bytes 12296 | tf_op jit(solution)/shard_map/ppermute | solution.py:169
  32.0 7.0 %collective-permute-start.8 = (f32[8,128]{1,0:T(8,128)S(1)}, f32[8,128]{1,0:T(8,128)S(1)}, u32[]{:S(2)}, u32[]{:S(2)}) collective-permute-start(f32[8,128]{1,0:T(8,128)S(1)} %maximum_maximum_fusion.1), channel_id=1, source_target_pairs={{0,8},{8,0},{1,9},{9,1},{2,10},{10,2},{3,11},{11,3},{4,12},{12,4},... | collective-permute-start | bytes 12296 | tf_op jit(solution)/shard_map/ppermute | solution.py:177
  39.2 3.6 %collective-permute-start.9 = (f32[8,128]{1,0:T(8,128)S(1)}, f32[8,128]{1,0:T(8,128)S(1)}, u32[]{:S(2)}, u32[]{:S(2)}) collective-permute-start(f32[8,128]{1,0:T(8,128)S(1)} %maximum_maximum_fusion.2), channel_id=1, source_target_pairs={{0,16},{16,0},{32,48},{48,32},{64,80},{80,64},{96,112},{112,96},{1... | collective-permute-start | bytes 12296 | tf_op jit(solution)/shard_map/ppermute | solution.py:177
  39.2 15.9 %collective-permute-start.1 = (f32[33,512]{1,0:T(8,128)S(1)}, f32[33,512]{1,0:T(8,128)S(1)}, u32[]{:S(2)}, u32[]{:S(2)}) collective-permute-start(f32[33,512]{1,0:T(8,128)S(1)} %pad_maximum_fusion.2), channel_id=1, source_target_pairs={{4,0},{5,1},{6,2},{7,3},{0,4},{1,5},{2,6},{3,7},{12,8},{13,9},{14,... | collective-permute-start | bytes 202760 | tf_op jit(solution)/shard_map/ppermute | solution.py:19
  42.9 4.5 %collective-permute-start.10 = (f32[8,128]{1,0:T(8,128)S(1)}, f32[8,128]{1,0:T(8,128)S(1)}, u32[]{:S(2)}, u32[]{:S(2)}) collective-permute-start(f32[8,128]{1,0:T(8,128)S(1)} %maximum_maximum_fusion.3), channel_id=1, source_target_pairs={{0,32},{16,48},{32,0},{48,16},{64,96},{80,112},{96,64},{112,80},{1... | collective-permute-start | bytes 12296 | tf_op jit(solution)/shard_map/ppermute | solution.py:177
  47.5 7.5 %collective-permute-start.11 = (f32[8,128]{1,0:T(8,128)S(1)}, f32[8,128]{1,0:T(8,128)S(1)}, u32[]{:S(2)}, u32[]{:S(2)}) collective-permute-start(f32[8,128]{1,0:T(8,128)S(1)} %maximum_maximum_fusion.4), channel_id=1, source_target_pairs={{0,64},{16,80},{32,96},{48,112},{64,0},{80,16},{96,32},{112,48},{1... | collective-permute-start | bytes 12296 | tf_op jit(solution)/shard_map/ppermute | solution.py:177

commit v10 on v6

--- a/solution.py
+++ b/solution.py
@@ -73,7 +73,7 @@
 def run_steps(particles, log_prior, transition, drive_vector, current, decay_rate, obs_matrix, obs_weight, observed):
     rows, width = particles.shape
     n_obs = obs_matrix.shape[1]
-    block = 256
+    block = 1024
     lanes = 128
     k = width // lanes
     message_rows = max(-(-(k + 2) // 8) * 8, 2 * k)
@@ -149,8 +149,6 @@
     n_pairs = pair_pick.shape[0]
     lanes = message.shape[1]
     k = width // lanes
-    local_sum = message[k, 0]
-    local_peak = message[k + 1, 0]
     stamp = message[k : 2 * k].reshape(1, width)
 
     cycle_out = jnp.concatenate([state[ancestors[cycle_pick]], stamp])
@@ -169,16 +167,18 @@
             body = message[: k + 1] * mine_scale + other[: k + 1] * other_scale
             message = jnp.concatenate([body, peak_row[None], jnp.zeros((pad, lanes), jnp.float32)])
             bit *= 2
-    total = message[k, 0]
-    peak = message[k + 1, 0]
-    mean_state = message[:k].reshape(width) / total
-
-    def group_weight(device_peak, device_sum):
+    total = message[k : k + 1]
+    peak = message[k + 1 : k + 2]
+    mean_state = (message[:k] / total).reshape(width)
+
+    def group_weight(row):
+        device_sum = row[:, :lanes]
+        device_peak = row[:, lanes : 2 * lanes]
         return jnp.log(jnp.maximum(groups * (device_sum * jnp.exp(device_peak - peak)) / total, 0.1))
 
-    own_w = group_weight(local_peak, local_sum)
-    cycle_w = group_weight(cycle_in[n_cycle, lanes], cycle_in[n_cycle, 0])
-    pair_w = group_weight(pair_in[n_pairs, lanes], pair_in[n_pairs, 0])
+    own_w = group_weight(stamp)
+    cycle_w = group_weight(cycle_in[n_cycle : n_cycle + 1])
+    pair_w = group_weight(pair_in[n_pairs : n_pairs + 1])
 
     source = (
         ancestors.at[cycle_pick]
@@ -188,11 +188,12 @@
     )
     table = jnp.concatenate([state, cycle_in[:n_cycle], pair_in[:n_pairs]], axis=0)
     migrated = table[source]
+    tiles = source.reshape(rows_here // lanes, lanes)
     group_logw = jnp.where(
-        source >= rows_here + n_cycle,
+        tiles >= rows_here + n_cycle,
         pair_w,
-        jnp.where(source >= rows_here, cycle_w, own_w),
-    )
+        jnp.where(tiles >= rows_here, cycle_w, own_w),
+    ).reshape(rows_here)
     return (migrated, group_logw, mean_state)
 
 

time: 72.8 us -> 58.2 us (0.80)
  the two profiles are of different devices: /device:TPU:1 before, /device:TPU:16 now
where the time goes in v10:
time: 58.2 us; the launch traced here: 57.9 us
  starting transfers between devices  18.1 us (31%)
  local copies, waits for them, and re-layouts  17.3 us (30%)
  waiting for transfers between devices  11.1 us (19%)
  Pallas kernels  6.7 us (12%)
  other arithmetic  3.87 us (7%)
  between operations  0.88 us (2%)
    ppermute x8, starting transfers between devices, window(): other = lax.ppermute(message, axis, [(i, i ^ bit) for i in range(size)])  16.6 us
    ppermute x8, waiting for transfers between devices, window(): other = lax.ppermute(message, axis, [(i, i ^ bit) for i in range(size)])  11.1 us
    pallas_call x1, Pallas kernels, run_steps(): pl.pallas_call(steps_kernel, grid=(rows // block,), in_specs=[pl.BlockSpe...  6.7 us
    gather x1, local copies, waits for them, and re-layouts, window(): migrated = table[source]  4.87 us
    gather x2, local copies, waits for them, and re-layouts, window(): cycle_out = jnp.concatenate([state[ancestors[cycle_pick]], stamp])  4.17 us
    gather x2, local copies, waits for them, and re-layouts, window(): pair_out = jnp.concatenate([state[ancestors[pair_pick]], stamp])  2.89 us
    scatter x2, local copies, waits for them, and re-layouts, window(): source = ancestors.at[cycle_pick].set(rows_here + jnp.arange(n_cycle, dty...  2.09 us
    concatenate x1, other arithmetic, window(): jnp.concatenate([state, cycle_in[:n_cycle], pair_in[:n_pairs]], axis=0)  1.9 us
  transfers between devices with their start and end apart: 10, of which 6 were waited for; matrix products, arithmetic and copies ran while one was open for 19% of the time, Pallas kernels for 0%

profile of v10, /device:TPU:16, one launch (start us, length us, event | category | flops | bytes accessed | tf_op | source)
XLA Modules:
  0.0 57.9 jit_solution(279624225869709863)
XLA Ops:
  0.6 0.7 %copy.19 = s32[1024]{0:T(1024)S(1)} copy(s32[1024]{0:T(1024)} %param.21) | data formatting | bytes 8192
  1.3 1.7 %copy.15.prior_ref = f32[1024,1]{1,0:T(8,128)} copy(f32[1024,1]{0,1:T(1,128)} %bitcast.64) | data formatting | bytes 8192 | tf_op jit(solution)/shard_map/reshape | solution.py:117
  3.0 0.0 copy-start.1
  3.0 6.7 %shard_map.139 = (f32[1024,512]{1,0:T(8,128)}, f32[8,128]{1,0:T(8,128)}) custom-call(f32[4]{0:T(128)} %current_ref.1, f32[1024,512]{1,0:T(8,128)} %state_ref.1, f32[1024,1]{1,0:T(8,128)} %copy.15.prior_ref, bf16[512,512]{1,0:T(8,128)(2,1)} %transition_ref.1, f32[1,512]{1,0:T(1,128)} %bitcast.67, f32[1,512]{1,0:T(1,128)} %bitcast.68, ...), custom_call_target="tpu_custom_call" | custom-call | flops 2684354560 | bytes 4718592 | tf_op jit(solution)/shard_map/pallas_call | solution.py:81
  9.7 1.5 %collective-permute-start.2 = (f32[8,128]{1,0:T(8,128)}, f32[8,128]{1,0:T(8,128)S(1)}, u32[]{:S(2)}, u32[]{:S(2)}) collective-permute-start(f32[8,128]{1,0:T(8,128)} %get-tuple-element.6), channel_id=1, source_target_pairs={{0,1},{1,0},{2,3},{3,2},{4,5},{5,4},{6,7},{7,6},{8,9},{9,8},{10,11... | collective-permute-start | bytes 12296 | tf_op jit(solution)/shard_map/ppermute | solution.py:163
  11.2 0.7 %slice.102 = f32[4,128]{1,0:T(4,128)S(1)} slice(f32[8,128]{1,0:T(8,128)} %get-tuple-element.6), slice={[4:8], [0:128]} | slice | bytes 4096 | tf_op jit(solution)/shard_map/slice | solution.py:152
  11.9 0.0 copy-done.1
  12.0 1.4 %gather_fusion = s32[256]{0:T(256)S(1)} fusion(s32[1024]{0:T(1024)S(1)} %copy.19, s32[1024]{0:T(1024)S(1)} %pad_clamp_fusion.3), kind=kCustom, calls=%fused_computation | custom fusion | bytes 3072 | tf_op jit(solution)/shard_map/gather | solution.py:154
  13.4 0.0 copy-start
  13.4 0.0 copy-start.2
  13.4 2.8 %gather_fusion.1 = f32[256,512]{1,0:T(8,128)S(1)} fusion(f32[1024,512]{1,0:T(8,128)} %get-tuple-element.5, s32[1024]{0:T(1024)S(1)} %pad_clamp_fusion.2), kind=kCustom, calls=%fused_computation.1 | custom fusion | bytes 1049600 | tf_op jit(solution)/shard_map/gather | solution.py:154
  16.2 0.1 collective-permute-start
  16.3 0.1 pad.20.clone
  16.4 0.0 collective-permute-done.2
  16.4 0.0 copy-done
  16.5 0.1 maximum_maximum_fusion
  16.5 2.8 %collective-permute-start.3 = (f32[8,128]{1,0:T(8,128)S(1)}, f32[8,128]{1,0:T(8,128)S(1)}, u32[]{:S(2)}, u32[]{:S(2)}) collective-permute-start(f32[8,128]{1,0:T(8,128)S(1)} %maximum_maximum_fusion), channel_id=1, source_target_pairs={{0,2},{1,3},{2,0},{3,1},{4,6},{5,7},{6,4},{7,5},{8,10},{9,11},{10,... | collective-permute-start | bytes 12296 | tf_op jit(solution)/shard_map/ppermute | solution.py:163
  19.3 0.0 copy-done.2
  19.3 2.4 %collective-permute-done.3 = f32[8,128]{1,0:T(8,128)S(1)} collective-permute-done((f32[8,128]{1,0:T(8,128)S(1)}, f32[8,128]{1,0:T(8,128)S(1)}, u32[]{:S(2)}, u32[]{:S(2)}) %collective-permute-start.3) | collective-permute-done | bytes 4128 | tf_op jit(solution)/shard_map/ppermute | solution.py:163
  21.7 0.1 maximum_maximum_fusion.1
  21.8 1.3 %collective-permute-start.4 = (f32[8,128]{1,0:T(8,128)S(1)}, f32[8,128]{1,0:T(8,128)S(1)}, u32[]{:S(2)}, u32[]{:S(2)}) collective-permute-start(f32[8,128]{1,0:T(8,128)S(1)} %maximum_maximum_fusion.1), channel_id=1, source_target_pairs={{0,4},{1,5},{2,6},{3,7},{4,0},{5,1},{6,2},{7,3},{8,12},{9,13},{10,... | collective-permute-start | bytes 12296 | tf_op jit(solution)/shard_map/ppermute | solution.py:163
  23.1 0.7 %gather_fusion.2 = s32[32]{0:T(128)S(1)} fusion(s32[1024]{0:T(1024)S(1)} %copy.19, s32[1024]{0:T(1024)S(1)} %pad_clamp_fusion.1), kind=kCustom, calls=%fused_computation.2 | custom fusion | bytes 384 | tf_op jit(solution)/shard_map/gather | solution.py:155
  23.8 2.4 %collective-permute-done.4 = f32[8,128]{1,0:T(8,128)S(1)} collective-permute-done((f32[8,128]{1,0:T(8,128)S(1)}, f32[8,128]{1,0:T(8,128)S(1)}, u32[]{:S(2)}, u32[]{:S(2)}) %collective-permute-start.4) | collective-permute-done | bytes 4128 | tf_op jit(solution)/shard_map/ppermute | solution.py:163
  26.2 0.1 maximum_maximum_fusion.2
  26.2 0.0 collective-permute-start.5
  26.3 1.1 %collective-permute-done.5 = f32[8,128]{1,0:T(8,128)S(1)} collective-permute-done((f32[8,128]{1,0:T(8,128)S(1)}, f32[8,128]{1,0:T(8,128)S(1)}, u32[]{:S(2)}, u32[]{:S(2)}) %collective-permute-start.5) | collective-permute-done | bytes 4128 | tf_op jit(solution)/shard_map/ppermute | solution.py:163
  27.5 0.1 maximum_maximum_fusion.3
  27.5 1.2 %collective-permute-start.6 = (f32[8,128]{1,0:T(8,128)S(1)}, f32[8,128]{1,0:T(8,128)S(1)}, u32[]{:S(2)}, u32[]{:S(2)}) collective-permute-start(f32[8,128]{1,0:T(8,128)S(1)} %maximum_maximum_fusion.3), channel_id=1, source_target_pairs={{0,16},{8,24},{16,0},{24,8},{32,48},{40,56},{48,32},{56,40},{64,80... | collective-permute-start | bytes 12296 | tf_op jit(solution)/shard_map/ppermute | solution.py:163
  28.8 2.2 %gather_fusion.3 = f32[32,512]{1,0:T(8,128)S(1)} fusion(f32[1024,512]{1,0:T(8,128)} %get-tuple-element.5, s32[1024]{0:T(1024)S(1)} %pad_clamp_fusion), kind=kCustom, calls=%fused_computation.3 | custom fusion | bytes 131200 | tf_op jit(solution)/shard_map/gather | solution.py:155
  31.0 0.2 collective-permute-done.6
  31.2 0.1 maximum_maximum_fusion.4
  31.3 3.7 %collective-permute-start.7 = (f32[8,128]{1,0:T(8,128)S(1)}, f32[8,128]{1,0:T(8,128)S(1)}, u32[]{:S(2)}, u32[]{:S(2)}) collective-permute-start(f32[8,128]{1,0:T(8,128)S(1)} %maximum_maximum_fusion.4), channel_id=1, source_target_pairs={{0,32},{8,40},{16,48},{24,56},{32,0},{40,8},{48,16},{56,24},{64,96... | collective-permute-start | bytes 12296 | tf_op jit(solution)/shard_map/ppermute | solution.py:163
  35.0 1.4 %collective-permute-start.1 = (f32[33,512]{1,0:T(8,128)S(1)}, f32[33,512]{1,0:T(8,128)S(1)}, u32[]{:S(2)}, u32[]{:S(2)}) collective-permute-start(f32[33,512]{1,0:T(8,128)S(1)} %pad_maximum_fusion.2), channel_id=1, source_target_pairs={{4,0},{5,1},{6,2},{7,3},{0,4},{1,5},{2,6},{3,7},{12,8},{13,9},{14,... | collective-permute-start | bytes 202760 | tf_op jit(solution)/shard_map/ppermute | solution.py:19
  36.4 0.2 collective-permute-done.7
  36.6 0.1 maximum_maximum_fusion.5
  36.7 5.7 %collective-permute-start.8 = (f32[8,128]{1,0:T(8,128)S(1)}, f32[8,128]{1,0:T(8,128)S(1)}, u32[]{:S(2)}, u32[]{:S(2)}) collective-permute-start(f32[8,128]{1,0:T(8,128)S(1)} %maximum_maximum_fusion.5), channel_id=1, source_target_pairs={{0,64},{8,72},{16,80},{24,88},{32,96},{40,104},{48,112},{56,120},{... | collective-permute-start | bytes 12296 | tf_op jit(solution)/shard_map/ppermute | solution.py:163
  42.4 1.4 %scatter_fusion = s32[1024]{0:T(1024)S(1)} fusion(s32[1024]{0:T(1024)S(1)} %copy.19, s32[256]{0:T(256)S(1)} %get-tuple-element.27, s32[256]{0:T(256)S(1)} %get-tuple-element.28), kind=kCustom, calls=%fused_computation.5 | custom fusion | bytes 4096 | tf_op jit(solution)/shard_map/scatter | solution.py:185
  43.8 0.7 %scatter_fusion.1 = s32[1024]{0:T(1024)S(1)} fusion(s32[1024]{0:T(1024)S(1)} %scatter_fusion, s32[32]{0:T(128)S(1)} %compare_select_fusion.4, s32[32]{0:T(128)S(1)} %iota_add_fusion.1), kind=kCustom, calls=%fused_computation.6 | custom fusion | bytes 512 | tf_op jit(solution)/shard_map/scatter | solution.py:187
  44.5 0.0 collective-permute-done.8
  44.6 0.1 maximum_maximum_fusion.6
  44.7 0.4 collective-permute-start.9
  45.0 4.8 %collective-permute-done.9 = f32[8,128]{1,0:T(8,128)S(1)} collective-permute-done((f32[8,128]{1,0:T(8,128)S(1)}, f32[8,128]{1,0:T(8,128)S(1)}, u32[]{:S(2)}, u32[]{:S(2)}) %collective-permute-start.9) | collective-permute-done | bytes 4128 | tf_op jit(solution)/shard_map/ppermute | solution.py:163
  49.8 0.0 collective-permute-done.1
  49.8 0.0 collective-permute-done
  49.9 0.6 %divide_bitcast_fusion = f32[512]{0:T(512)} fusion(f32[5,128]{1,0:T(8,128)S(1)} %multiply_add_fusion, f32[128]{0:T(128)S(1)} %get-tuple-element.26), kind=kLoop, calls=%fused_computation.37 | loop fusion | flops 512 | bytes 4608 | tf_op jit(solution)/shard_map/reshape | solution.py:172
  50.5 1.9 %pad_maximum_fusion = f32[1312,512]{1,0:T(8,128)S(1)} fusion(f32[32,512]{1,0:T(8,128)S(1)} %slice.142, f32[256,512]{1,0:T(8,128)S(1)} %slice.141, f32[1024,512]{1,0:T(8,128)} %get-tuple-element.5), kind=kLoop, calls=%fused_computation.7 | loop fusion | flops 1343488 | bytes 5373952 | tf_op jit(solution)/shard_map/concatenate | solution.py:189
  52.4 4.9 %gather_fusion.4 = f32[1024,512]{1,0:T(8,128)} fusion(f32[1312,512]{1,0:T(8,128)S(1)} %pad_maximum_fusion, s32[1024]{0:T(1024)S(1)} %fusion), kind=kCustom, calls=%fused_computation.4 | custom fusion | bytes 4198400 | tf_op jit(solution)/shard_map/gather | solution.py:190
  57.3 0.6 %fusion.1 = f32[1024]{0:T(1024)} fusion(s32[1024]{0:T(1024)S(1)} %scatter_fusion.1, f32[128]{0:T(128)S(1)} %get-tuple-element.25, f32[128]{0:T(128)S(1)} %get-tuple-element.24, f32[128]{0:T(128)S(1)} %get-tuple-element.23), kind=kLoop, calls=%fused_computation.25 | loop fusion | flops 4096 | bytes 9728 | tf_op jit(solution)/shard_map/jit(_where)/select_n | solution.py:192
  (40 shorter events, 0.3 us)
Async XLA Ops:
  3.0 8.9 %copy-start.1 = (s32[256]{0:T(256)S(1)}, s32[256]{0:T(256)}, u32[]{:S(2)}) copy-start(s32[256]{0:T(256)} %param.22) | copy-start | bytes 3076
  9.7 6.7 %collective-permute-start.2 = (f32[8,128]{1,0:T(8,128)}, f32[8,128]{1,0:T(8,128)S(1)}, u32[]{:S(2)}, u32[]{:S(2)}) collective-permute-start(f32[8,128]{1,0:T(8,128)} %get-tuple-element.6), channel_id=1, source_target_pairs={{0,1},{1,0},{2,3},{3,2},{4,5},{5,4},{6,7},{7,6},{8,9},{9,8},{10,11... | collective-permute-start | bytes 12296 | tf_op jit(solution)/shard_map/ppermute | solution.py:163
  13.4 3.1 %copy-start = (f32[8,128]{1,0:T(8,128)S(1)}, f32[8,128]{1,0:T(8,128)}, u32[]{:S(2)}) copy-start(f32[8,128]{1,0:T(8,128)} %get-tuple-element.6) | copy-start | bytes 12292
  13.4 5.9 %copy-start.2 = (s32[32]{0:T(128)S(1)}, s32[32]{0:T(128)}, u32[]{:S(2)}) copy-start(s32[32]{0:T(128)} %param.23) | copy-start | bytes 388
  16.2 33.6 %collective-permute-start = (f32[257,512]{1,0:T(8,128)S(1)}, f32[257,512]{1,0:T(8,128)S(1)}, u32[]{:S(2)}, u32[]{:S(2)}) collective-permute-start(f32[257,512]{1,0:T(8,128)S(1)} %pad_maximum_fusion.1), channel_id=1, source_target_pairs={{248,0},{0,8},{8,16},{16,24},{24,32},{32,40},{40,48},{48,56},{56,6... | collective-permute-start | bytes 1579016 | tf_op jit(solution)/shard_map/ppermute | solution.py:19
  16.5 5.1 %collective-permute-start.3 = (f32[8,128]{1,0:T(8,128)S(1)}, f32[8,128]{1,0:T(8,128)S(1)}, u32[]{:S(2)}, u32[]{:S(2)}) collective-permute-start(f32[8,128]{1,0:T(8,128)S(1)} %maximum_maximum_fusion), channel_id=1, source_target_pairs={{0,2},{1,3},{2,0},{3,1},{4,6},{5,7},{6,4},{7,5},{8,10},{9,11},{10,... | collective-permute-start | bytes 12296 | tf_op jit(solution)/shard_map/ppermute | solution.py:163
  21.8 4.4 %collective-permute-start.4 = (f32[8,128]{1,0:T(8,128)S(1)}, f32[8,128]{1,0:T(8,128)S(1)}, u32[]{:S(2)}, u32[]{:S(2)}) collective-permute-start(f32[8,128]{1,0:T(8,128)S(1)} %maximum_maximum_fusion.1), channel_id=1, source_target_pairs={{0,4},{1,5},{2,6},{3,7},{4,0},{5,1},{6,2},{7,3},{8,12},{9,13},{10,... | collective-permute-start | bytes 12296 | tf_op jit(solution)/shard_map/ppermute | solution.py:163
  26.2 1.2 %collective-permute-start.5 = (f32[8,128]{1,0:T(8,128)S(1)}, f32[8,128]{1,0:T(8,128)S(1)}, u32[]{:S(2)}, u32[]{:S(2)}) collective-permute-start(f32[8,128]{1,0:T(8,128)S(1)} %maximum_maximum_fusion.2), channel_id=1, source_target_pairs={{0,8},{8,0},{16,24},{24,16},{32,40},{40,32},{48,56},{56,48},{64,72... | collective-permute-start | bytes 12296 | tf_op jit(solution)/shard_map/ppermute | solution.py:163
  27.5 3.6 %collective-permute-start.6 = (f32[8,128]{1,0:T(8,128)S(1)}, f32[8,128]{1,0:T(8,128)S(1)}, u32[]{:S(2)}, u32[]{:S(2)}) collective-permute-start(f32[8,128]{1,0:T(8,128)S(1)} %maximum_maximum_fusion.3), channel_id=1, source_target_pairs={{0,16},{8,24},{16,0},{24,8},{32,48},{40,56},{48,32},{56,40},{64,80... | collective-permute-start | bytes 12296 | tf_op jit(solution)/shard_map/ppermute | solution.py:163
  31.3 5.3 %collective-permute-start.7 = (f32[8,128]{1,0:T(8,128)S(1)}, f32[8,128]{1,0:T(8,128)S(1)}, u32[]{:S(2)}, u32[]{:S(2)}) collective-permute-start(f32[8,128]{1,0:T(8,128)S(1)} %maximum_maximum_fusion.4), channel_id=1, source_target_pairs={{0,32},{8,40},{16,48},{24,56},{32,0},{40,8},{48,16},{56,24},{64,96... | collective-permute-start | bytes 12296 | tf_op jit(solution)/shard_map/ppermute | solution.py:163
  35.0 14.8 %collective-permute-start.1 = (f32[33,512]{1,0:T(8,128)S(1)}, f32[33,512]{1,0:T(8,128)S(1)}, u32[]{:S(2)}, u32[]{:S(2)}) collective-permute-start(f32[33,512]{1,0:T(8,128)S(1)} %pad_maximum_fusion.2), channel_id=1, source_target_pairs={{4,0},{5,1},{6,2},{7,3},{0,4},{1,5},{2,6},{3,7},{12,8},{13,9},{14,... | collective-permute-start | bytes 202760 | tf_op jit(solution)/shard_map/ppermute | solution.py:19
  36.7 7.8 %collective-permute-start.8 = (f32[8,128]{1,0:T(8,128)S(1)}, f32[8,128]{1,0:T(8,128)S(1)}, u32[]{:S(2)}, u32[]{:S(2)}) collective-permute-start(f32[8,128]{1,0:T(8,128)S(1)} %maximum_maximum_fusion.5), channel_id=1, source_target_pairs={{0,64},{8,72},{16,80},{24,88},{32,96},{40,104},{48,112},{56,120},{... | collective-permute-start | bytes 12296 | tf_op jit(solution)/shard_map/ppermute | solution.py:163
  44.7 5.1 %collective-permute-start.9 = (f32[8,128]{1,0:T(8,128)S(1)}, f32[8,128]{1,0:T(8,128)S(1)}, u32[]{:S(2)}, u32[]{:S(2)}) collective-permute-start(f32[8,128]{1,0:T(8,128)S(1)} %maximum_maximum_fusion.6), channel_id=1, source_target_pairs={{0,128},{8,136},{16,144},{24,152},{32,160},{40,168},{48,176},{56,1... | collective-permute-start | bytes 12296 | tf_op jit(solution)/shard_map/ppermute | solution.py:163
